TPU v7x, 128 devices: a whole 4x4x4 slice. The times are simulated.
128 devices in a mesh: dp: 16 (over z, y_lo, core), tensor: 8 (over x, y_hi).
Axes of the slice: x: 4, y: 4 (y_hi: 2, y_lo: 2; y = y_hi * 2 + y_lo), z: 4, core: 2. Of those that a mesh axis runs over, the one named last changes fastest.
Arguments:
- token_ids: int32 [512], P('dp'), may hold values from 0 to 128255, as said below
- hidden_in: bfloat16 [512, 8192], P('dp'), may hold values from -6 to 6
- cotangent: bfloat16 [512, 8192], P('dp'), may hold values from -6 to 6
- gate_weight: bfloat16 [8192, 28672], P(None, ('dp', 'tensor')), may hold values from -0.0625 to 0.0625
- up_weight: bfloat16 [8192, 28672], P(None, ('dp', 'tensor')), may hold values from -0.0625 to 0.0625
- down_weight: bfloat16 [28672, 8192], P(('dp', 'tensor')), may hold values from -0.03125 to 0.03125
- gate_in_proj: bfloat16 [8192, 64], replicated, may hold values from -0.0625 to 0.0625
- up_in_proj: bfloat16 [8192, 64], replicated, may hold values from -0.0625 to 0.0625
- down_out_proj: bfloat16 [8192, 64], replicated, may hold values from -0.0625 to 0.0625
- gate_out_proj: bfloat16 [28672, 64], P(('dp', 'tensor')), may hold values from -0.03125 to 0.03125
- up_out_proj: bfloat16 [28672, 64], P(('dp', 'tensor')), may hold values from -0.03125 to 0.03125
- down_in_proj: bfloat16 [28672, 64], P(('dp', 'tensor')), may hold values from -0.03125 to 0.03125
- stored_grads: bfloat16 [4096, 12288], P(('dp', 'tensor')), may hold values from -0.0546875 to 0.0546875
- example_ids: int32 [4096], P(('dp', 'tensor')), may hold values from 0 to 1023
Outputs:
- doc_grads: bfloat16 [16, 12288], P('dp')
- example_scores: float32 [16, 1024], P(None, ('dp', 'tensor'))
Inputs may be any that keep to these rules, and one draw needn't show every extreme that they name: `token_ids`: 0 marks padding, which only fills the end of a document of 32 tokens; each document has 16 or more tokens other than 0.
All inputs are finite; a program needn't handle non-finite values.
Results may differ from a plain program's by a relative error of at most 0.0051.
Values may be sent and summed in bfloat16 or wider, within the bound.
No kernel may reach another device: no remote copies, remote signals or barrier semaphores. Data moves between devices by JAX's collectives and lax.ppermute only.
A program may use at most 128 MiB of HBM per device.

v0:
```python
import jax
import jax.numpy as jnp
from jax import lax
from jax.sharding import PartitionSpec as P

LEN = 32
EX_DEV = 8


def through_layer(act_rows, cot_rows, gate_part, up_part, down_part):
    gate_pre = jnp.dot(act_rows, gate_part, preferred_element_type=jnp.float32)
    up_pre = jnp.dot(act_rows, up_part, preferred_element_type=jnp.float32)
    back_pre = lax.dot_general(
        cot_rows, down_part, (((1,), (1,)), ((), ())), preferred_element_type=jnp.float32
    )
    return (gate_pre, up_pre, back_pre)


def project_rows(gate_pre, up_pre, back_pre, gate_out_proj, up_out_proj, down_in_proj):
    squash = jax.nn.sigmoid(gate_pre)
    hidden = (gate_pre * squash * up_pre).astype(jnp.bfloat16)
    grad_up = (back_pre * gate_pre * squash).astype(jnp.bfloat16)
    grad_gate = (back_pre * up_pre * squash * (1.0 + gate_pre * (1.0 - squash))).astype(
        jnp.bfloat16
    )
    side_gate = jnp.dot(grad_gate, gate_out_proj, preferred_element_type=jnp.float32)
    side_up = jnp.dot(grad_up, up_out_proj, preferred_element_type=jnp.float32)
    side_down = jnp.dot(hidden, down_in_proj, preferred_element_type=jnp.float32)
    return jnp.concatenate([side_gate, side_up, side_down], axis=1)


def body(
    token_ids,
    hidden_in,
    cotangent,
    gate_weight,
    up_weight,
    down_weight,
    gate_in_proj,
    up_in_proj,
    down_out_proj,
    gate_out_proj,
    up_out_proj,
    down_in_proj,
    stored_grads,
    example_ids,
):
    tok_rows = hidden_in.shape[0]
    proj_rank = gate_in_proj.shape[1]
    pad_mask = (token_ids != 0).astype(jnp.bfloat16)[:, None]
    masked = cotangent * pad_mask
    act_rows = lax.all_gather(hidden_in, "dp", axis=0, tiled=True)
    cot_rows = lax.all_gather(masked, "dp", axis=0, tiled=True)
    gate_pre, up_pre, back_pre = through_layer(
        act_rows, cot_rows, gate_weight, up_weight, down_weight
    )
    block = project_rows(gate_pre, up_pre, back_pre, gate_out_proj, up_out_proj, down_in_proj)
    summed = lax.psum(block, ("dp", "tensor"))
    home_rows = lax.dynamic_slice_in_dim(summed, lax.axis_index("dp") * tok_rows, tok_rows, 0)
    in_gate = jnp.dot(hidden_in, gate_in_proj, preferred_element_type=jnp.float32)
    in_up = jnp.dot(hidden_in, up_in_proj, preferred_element_type=jnp.float32)
    out_down = jnp.dot(masked, down_out_proj, preferred_element_type=jnp.float32)
    docs_here = tok_rows // LEN

    def doc_outer(left, right):
        left_docs = left.reshape(docs_here, LEN, proj_rank)
        right_docs = right.reshape(docs_here, LEN, proj_rank)
        return jnp.einsum("dlr,dls->drs", left_docs, right_docs, precision=lax.Precision.HIGHEST)

    side_gate = home_rows[:, :proj_rank]
    side_up = home_rows[:, proj_rank : 2 * proj_rank]
    side_down = home_rows[:, 2 * proj_rank :]
    blocks = jnp.stack(
        [doc_outer(in_gate, side_gate), doc_outer(in_up, side_up), doc_outer(side_down, out_down)],
        axis=1,
    )
    doc_grads = blocks.reshape(docs_here, 3 * proj_rank * proj_rank).astype(jnp.bfloat16)
    examples_all = EX_DEV * lax.axis_size("dp") * lax.axis_size("tensor")
    onehot = (example_ids[:, None] == jnp.arange(examples_all, dtype=jnp.int32)[None, :]).astype(
        jnp.float32
    )
    raw_scores = lax.dot_general(
        lax.all_gather(doc_grads, "dp", axis=0, tiled=True),
        stored_grads,
        (((1,), (1,)), ((), ())),
        preferred_element_type=jnp.float32,
    )
    partial_scores = jnp.dot(raw_scores, onehot, precision=lax.Precision.HIGHEST)
    totals = lax.psum_scatter(partial_scores, ("dp", "tensor"), scatter_dimension=1, tiled=True)
    return (doc_grads, totals)


def solution(mesh):
    return jax.shard_map(
        body,
        mesh=mesh,
        in_specs=(
            P("dp"),
            P("dp", None),
            P("dp", None),
            P(None, ("dp", "tensor")),
            P(None, ("dp", "tensor")),
            P(("dp", "tensor"), None),
            P(),
            P(),
            P(),
            P(("dp", "tensor"), None),
            P(("dp", "tensor"), None),
            P(("dp", "tensor"), None),
            P(("dp", "tensor"), None),
            P(("dp", "tensor")),
        ),
        out_specs=(P("dp", None), P(None, ("dp", "tensor"))),
        check_vma=False,
    )
```

profile of v0, /device:TPU:1, one launch (start us, length us, event | category | flops | bytes accessed | tf_op | source)
XLA Modules:
  0.0 456.6 jit_solution(712258899726448232)
XLA Ops:
  7.2 0.7 all-gather.6.cloned.1.call-update
  8.0 0.7 compare_convert_fusion
  8.6 1.9 broadcast_multiply_fusion
  10.7 2.1 fusion.23
  12.7 0.4 fusion.22
  13.1 52.3 %all-gather.6.cloned.1.call-done = bf16[512,8192]{1,0:T(8,128)(2,1)} async-done(((bf16[32,8192]{1,0:T(8,128)(2,1)}), bf16[512,8192]{1,0:T(8,128)(2,1)}) %all-gather.6.cloned.1.call-update) | async-done | bytes 8388624 | tf_op jit(solution)/shard_map/all_gather | solution.py:52
  65.4 7.3 %fusion.20 = f32[512,224]{0,1:T(8,128)S(1)} fusion(bf16[512,8192]{1,0:T(8,128)(2,1)} %all-gather.6.cloned.1.call-done, bf16[8192,224]{0,1:T(8,128)(2,1)} %param.18), kind=kOutput, calls=%fused_computation.33 | convolution fusion | flops 1879048192 | bytes 12517376 | tf_op jit(solution)/shard_map/dot_general | solution.py:12
  72.7 0.6 copy-done.6
  73.3 2.7 fusion.21
  76.3 44.0 %all-gather.4.cloned.1.call-done = bf16[512,8192]{1,0:T(8,128)(2,1)} async-done(((bf16[32,8192]{1,0:T(8,128)(2,1)}), bf16[512,8192]{1,0:T(8,128)(2,1)}) %all-gather.4.cloned.1.call-update) | async-done | bytes 8388624 | tf_op jit(solution)/shard_map/all_gather | solution.py:53
  120.3 7.2 %fusion.19 = f32[512,224]{0,1:T(8,128)S(1)} fusion(bf16[512,8192]{1,0:T(8,128)(2,1)} %all-gather.4.cloned.1.call-done, bf16[224,8192]{1,0:T(8,128)(2,1)} %param.19), kind=kOutput, calls=%fused_computation.32 | convolution fusion | flops 1879048192 | bytes 12517376 | tf_op jit(solution)/shard_map/dot_general | solution.py:13
  127.7 1.4 fusion.8
  129.1 0.8 pad_maximum_fusion
  130.0 0.4 fusion.18
  130.4 145.8 %all-reduce.4.cloned.1.call-done = f32[512,192]{0,1:T(8,128)} async-done(((f32[512,192]{0,1:T(8,128)}), f32[512,192]{0,1:T(8,128)}) %all-reduce.4.cloned.1.call-update) | async-done | bytes 393232 | tf_op jit(solution)/shard_map/psum | solution.py:58
  276.2 1.0 fusion
  277.3 1.0 fusion.2
  278.3 1.0 fusion.1
  279.4 23.4 %all-gather = bf16[16,1,12288]{2,1,0:T(2,128)(2,1)S(1)} all-gather(bf16[1,1,12288]{2,1,0:T(2,128)(2,1)S(1)} %reshape.44), channel_id=1, replica_groups=mesh['dp'=16,'tensor'=8] {'dp'}, dimensions={0}, use_global_device_ids=true | all-gather | bytes 417792 | tf_op jit(solution)/shard_map/all_gather | solution.py:83
  302.8 0.6 fusion.3
  303.4 2.1 fusion.9
  305.6 0.7 convert_element_type.29
  306.3 142.5 %all-reduce.6.cloned.1.call-done = f32[16,1024]{0,1:T(8,128)} async-done(((f32[16,1024]{0,1:T(8,128)}), f32[16,1024]{0,1:T(8,128)}) %all-reduce.6.cloned.1.call-update) | async-done | bytes 65552
  448.8 1.3 constant_dynamic-slice_fusion
  (36 shorter events, 0.9 us)
Async XLA Ops:
  7.2 3.5 copy-start
  7.2 5.6 %copy-start.1 = (bf16[32,8192]{1,0:T(8,128)(2,1)S(1)}, bf16[32,8192]{1,0:T(8,128)(2,1)}, u32[]{:S(2)}) copy-start(bf16[32,8192]{1,0:T(8,128)(2,1)} %param.15) | copy-start | bytes 1572868
  7.2 5.5 %copy-start.2 = (bf16[8192,64]{0,1:T(8,128)(2,1)S(1)}, bf16[8192,64]{0,1:T(8,128)(2,1)}, u32[]{:S(2)}) copy-start(bf16[8192,64]{0,1:T(8,128)(2,1)} %param.21) | copy-start | bytes 3145732
  7.2 58.2 %all-gather.6.cloned.1.call-start = ((), (), s32[]{:S(2)}) async-start(), calls=%async_computation.1 | async-start | bytes 8912896 | tf_op jit(solution)/shard_map/all_gather | solution.py:52
  7.9 112.3 %all-gather.4.cloned.1.call-start = ((), (), s32[]{:S(2)}) async-start(), calls=%async_computation | async-start | bytes 8912896 | tf_op jit(solution)/shard_map/all_gather | solution.py:53
  10.6 265.6 %all-reduce.4.cloned.1.call-start = ((), (), s32[]{:S(2)}) async-start(), calls=%async_computation.2 | async-start | bytes 786432 | tf_op jit(solution)/shard_map/psum | solution.py:58
  65.4 7.3 %copy-start.5 = (bf16[512,8192]{1,0:T(8,128)(2,1)S(1)}, bf16[512,8192]{1,0:T(8,128)(2,1)}, u32[]{:S(2)}) copy-start(bf16[512,8192]{1,0:T(8,128)(2,1)} %all-gather.6.cloned.1.call-done) | copy-start | bytes 25165828
  65.4 7.9 %copy-start.6 = (bf16[8192,224]{0,1:T(8,128)(2,1)S(1)}, bf16[8192,224]{0,1:T(8,128)(2,1)}, u32[]{:S(2)}) copy-start(bf16[8192,224]{0,1:T(8,128)(2,1)} %param.17) | copy-start | bytes 11010052
  73.3 2.7 copy-start.10
  73.3 2.7 copy-start.7
  76.0 51.4 %copy-start.12 = (f32[512,224]{0,1:T(8,128)}, f32[512,224]{0,1:T(8,128)S(1)}, u32[]{:S(2)}) copy-start(f32[512,224]{0,1:T(8,128)S(1)} %fusion.21) | copy-start | bytes 1376260
  76.3 51.1 %copy-start.8 = (bf16[224,64]{0,1:T(8,128)(2,1)S(1)}, bf16[224,64]{0,1:T(8,128)(2,1)}, u32[]{:S(2)}) copy-start(bf16[224,64]{0,1:T(8,128)(2,1)} %param.24) | copy-start | bytes 86020
  120.2 7.5 %copy-start.9 = (bf16[224,64]{0,1:T(8,128)(2,1)S(1)}, bf16[224,64]{0,1:T(8,128)(2,1)}, u32[]{:S(2)}) copy-start(bf16[224,64]{0,1:T(8,128)(2,1)} %param.23) | copy-start | bytes 86020
  120.2 7.5 %copy-start.11 = (f32[512,224]{0,1:T(8,128)S(1)}, f32[512,224]{0,1:T(8,128)}, u32[]{:S(2)}) copy-start(f32[512,224]{0,1:T(8,128)} %copy-done.10) | copy-start | bytes 1376260
  127.4 2.6 copy-start.3
  127.7 175.1 %copy-start.4 = (bf16[32,12288]{1,0:T(8,128)(2,1)S(1)}, bf16[32,12288]{1,0:T(8,128)(2,1)}, u32[]{:S(2)}) copy-start(bf16[32,12288]{1,0:T(8,128)(2,1)} %param.26) | copy-start | bytes 2359300
  129.9 318.9 %all-reduce.6.cloned.1.call-start = ((), (), s32[]{:S(2)}) async-start(), calls=%async_computation.3 | async-start | bytes 1048576
Sparse Core Ops, SparseCore 0:
  9.7 55.6 all-gather.5
  67.1 53.0 all-gather.3
  130.1 146.1 all-reduce.3
  305.7 143.0 all-reduce.5
where the time goes:
time: 457 us
  waiting for transfers between devices  385 us (84%)
  matrix products  27.6 us (6%)
  blocking collectives  23.4 us (5%)
  between operations  14 us (3%)
    psum x1, waiting for transfers between devices, body(): summed = lax.psum(block, ('dp', 'tensor'))  146 us
    unnamed x5, waiting for transfers between devices  143 us
    all_gather x1, waiting for transfers between devices, body(): act_rows = lax.all_gather(hidden_in, 'dp', axis=0, tiled=True)  52.3 us
    all_gather x1, waiting for transfers between devices, body(): cot_rows = lax.all_gather(masked, 'dp', axis=0, tiled=True)  44 us
    all_gather x1, blocking collectives, body(): lax.all_gather(doc_grads, 'dp', axis=0, tiled=True)  23.4 us
  transfers between devices with their start and end apart: 4, of which 4 were waited for; matrix products, arithmetic and copies ran while one was open for 4% of the time, Pallas kernels for 0%

commit v1 on v0

--- a/solution.py
+++ b/solution.py
@@ -5,6 +5,7 @@
 
 LEN = 32
 EX_DEV = 8
+ALL = ("dp", "tensor")
 
 
 def through_layer(act_rows, cot_rows, gate_part, up_part, down_part):
@@ -29,6 +30,17 @@
     return jnp.concatenate([side_gate, side_up, side_down], axis=1)
 
 
+def scatter_sum(x, n):
+    blocks = x.reshape((n, x.shape[0] // n) + x.shape[1:])
+    return jnp.sum(lax.all_to_all(blocks, ALL, 0, 0, tiled=False), axis=0)
+
+
+def gather_rows(x, n):
+    copies = jnp.broadcast_to(x[None], (n,) + x.shape)
+    got = lax.all_to_all(copies, ALL, 0, 0, tiled=False)
+    return got.reshape((n * x.shape[0],) + x.shape[1:])
+
+
 def body(
     token_ids,
     hidden_in,
@@ -45,7 +57,7 @@
     stored_grads,
     example_ids,
 ):
-    tok_rows = hidden_in.shape[0]
+    n_all = lax.axis_size("dp") * lax.axis_size("tensor")
     proj_rank = gate_in_proj.shape[1]
     pad_mask = (token_ids != 0).astype(jnp.bfloat16)[:, None]
     masked = cotangent * pad_mask
@@ -55,38 +67,39 @@
         act_rows, cot_rows, gate_weight, up_weight, down_weight
     )
     block = project_rows(gate_pre, up_pre, back_pre, gate_out_proj, up_out_proj, down_in_proj)
-    summed = lax.psum(block, ("dp", "tensor"))
-    home_rows = lax.dynamic_slice_in_dim(summed, lax.axis_index("dp") * tok_rows, tok_rows, 0)
-    in_gate = jnp.dot(hidden_in, gate_in_proj, preferred_element_type=jnp.float32)
-    in_up = jnp.dot(hidden_in, up_in_proj, preferred_element_type=jnp.float32)
-    out_down = jnp.dot(masked, down_out_proj, preferred_element_type=jnp.float32)
-    docs_here = tok_rows // LEN
+    summed = gather_rows(scatter_sum(block, n_all), n_all)
+    in_gate = jnp.dot(act_rows, gate_in_proj, preferred_element_type=jnp.float32)
+    in_up = jnp.dot(act_rows, up_in_proj, preferred_element_type=jnp.float32)
+    out_down = jnp.dot(cot_rows, down_out_proj, preferred_element_type=jnp.float32)
+    docs = act_rows.shape[0] // LEN
 
     def doc_outer(left, right):
-        left_docs = left.reshape(docs_here, LEN, proj_rank)
-        right_docs = right.reshape(docs_here, LEN, proj_rank)
+        left_docs = left.reshape(docs, LEN, proj_rank)
+        right_docs = right.reshape(docs, LEN, proj_rank)
         return jnp.einsum("dlr,dls->drs", left_docs, right_docs, precision=lax.Precision.HIGHEST)
 
-    side_gate = home_rows[:, :proj_rank]
-    side_up = home_rows[:, proj_rank : 2 * proj_rank]
-    side_down = home_rows[:, 2 * proj_rank :]
+    side_gate = summed[:, :proj_rank]
+    side_up = summed[:, proj_rank : 2 * proj_rank]
+    side_down = summed[:, 2 * proj_rank :]
     blocks = jnp.stack(
         [doc_outer(in_gate, side_gate), doc_outer(in_up, side_up), doc_outer(side_down, out_down)],
         axis=1,
     )
-    doc_grads = blocks.reshape(docs_here, 3 * proj_rank * proj_rank).astype(jnp.bfloat16)
-    examples_all = EX_DEV * lax.axis_size("dp") * lax.axis_size("tensor")
+    all_docs = blocks.reshape(docs, 3 * proj_rank * proj_rank).astype(jnp.bfloat16)
+    docs_here = hidden_in.shape[0] // LEN
+    doc_grads = lax.dynamic_slice_in_dim(all_docs, lax.axis_index("dp") * docs_here, docs_here, 0)
+    examples_all = EX_DEV * n_all
     onehot = (example_ids[:, None] == jnp.arange(examples_all, dtype=jnp.int32)[None, :]).astype(
         jnp.float32
     )
     raw_scores = lax.dot_general(
-        lax.all_gather(doc_grads, "dp", axis=0, tiled=True),
+        all_docs,
         stored_grads,
         (((1,), (1,)), ((), ())),
         preferred_element_type=jnp.float32,
     )
     partial_scores = jnp.dot(raw_scores, onehot, precision=lax.Precision.HIGHEST)
-    totals = lax.psum_scatter(partial_scores, ("dp", "tensor"), scatter_dimension=1, tiled=True)
+    totals = scatter_sum(partial_scores.T, n_all).T
     return (doc_grads, totals)
 
 

time: 457 us -> 205 us (0.45)
  waiting for transfers between devices: 385 us -> 119 us
  blocking collectives: 23.4 us -> 0 us
  starting transfers between devices: 0.16 us -> 19.9 us
  matrix products: 27.6 us -> 41 us
    psum x1 -> x0, waiting for transfers between devices: 146 us -> none  [body(): summed = lax.psum(block, ('dp', 'tensor'))]
    unnamed x5 -> x2, waiting for transfers between devices: 143 us -> 0.7 us
    all_gather x1 -> x0, blocking collectives: 23.4 us -> none  [body(): lax.all_gather(doc_grads, 'dp', axis=0, tiled=True)]
    all_to_all x0 -> x3, starting transfers between devices: none -> 19.8 us  [the longest x2 12.7 us: scatter_sum(): return jnp.sum(lax.all_to_all(blocks, ALL, 0, 0, tiled=False), axis=0)]
    all_to_all x0 -> x3, waiting for transfers between devices: none -> 19.2 us  [the longest x2 11.9 us: scatter_sum(): return jnp.sum(lax.all_to_all(blocks, ALL, 0, 0, tiled=False), axis=0)]
    dot_general x4, matrix products: 3.46 us -> 18.4 us  [the longest x1 6.71 us: body(): jnp.dot(cot_rows, down_out_proj, preferred_element_type=jnp.float32)]
    dot_general x1, matrix products: 7.26 us -> 2.68 us  [through_layer(): up_pre = jnp.dot(act_rows, up_part, preferred_element_type=jnp.float32)]
    dot_general x1, matrix products: 2.67 us -> 7.25 us  [through_layer(): gate_pre = jnp.dot(act_rows, gate_part, preferred_element_type=jnp.float32)]
  transfers between devices with their start and end apart: 4 -> 5, of which waited for: 4 -> 5; matrix products, arithmetic and copies ran while one was open for 4% -> 15% of each run, Pallas kernels for 0% -> 0%
where the time goes in v1:
time: 205 us; the launch traced here: 204 us
  waiting for transfers between devices  119 us (58%)
  matrix products  41 us (20%)
  starting transfers between devices  19.9 us (10%)
  between operations  14.3 us (7%)
  local copies, waits for them, and re-layouts  5.94 us (3%)
  other arithmetic  4.51 us (2%)
    all_gather x1, waiting for transfers between devices, body(): act_rows = lax.all_gather(hidden_in, 'dp', axis=0, tiled=True)  54.8 us
    all_gather x1, waiting for transfers between devices, body(): cot_rows = lax.all_gather(masked, 'dp', axis=0, tiled=True)  44 us
    all_to_all x2, starting transfers between devices, scatter_sum(): return jnp.sum(lax.all_to_all(blocks, ALL, 0, 0, tiled=False), axis=0)  12.7 us
    all_to_all x2, waiting for transfers between devices, scatter_sum(): return jnp.sum(lax.all_to_all(blocks, ALL, 0, 0, tiled=False), axis=0)  11.9 us
    all_to_all x1, waiting for transfers between devices, gather_rows(): got = lax.all_to_all(copies, ALL, 0, 0, tiled=False)  7.3 us
    dot_general x1, matrix products, through_layer(): gate_pre = jnp.dot(act_rows, gate_part, preferred_element_type=jnp.float32)  7.25 us
    all_to_all x1, starting transfers between devices, gather_rows(): got = lax.all_to_all(copies, ALL, 0, 0, tiled=False)  7.15 us
    dot_general x1, matrix products, through_layer(): lax.dot_general(cot_rows, down_part, (((1,), (1,)), ((), ())), preferred_...  7.11 us
  transfers between devices with their start and end apart: 5, of which 5 were waited for; matrix products, arithmetic and copies ran while one was open for 15% of the time, Pallas kernels for 0%

profile of v1, /device:TPU:1, one launch (start us, length us, event | category | flops | bytes accessed | tf_op | source)
XLA Modules:
  0.0 204.3 jit_solution(17651150017102191062)
XLA Ops:
  8.6 1.9 broadcast_multiply_fusion
  10.6 54.8 %all-gather.3.cloned.1.call-done = bf16[512,8192]{1,0:T(8,128)(2,1)} async-done(((bf16[32,8192]{1,0:T(8,128)(2,1)}), bf16[512,8192]{1,0:T(8,128)(2,1)}) %all-gather.3.cloned.1.call-update) | async-done | bytes 8388624 | tf_op jit(solution)/shard_map/all_gather | solution.py:64
  65.4 7.2 %fusion.16 = f32[512,224]{0,1:T(8,128)S(1)} fusion(bf16[512,8192]{1,0:T(8,128)(2,1)} %all-gather.3.cloned.1.call-done, bf16[8192,224]{0,1:T(8,128)(2,1)} %param.17), kind=kOutput, calls=%fused_computation.29 | convolution fusion | flops 1879048192 | bytes 12517376 | tf_op jit(solution)/shard_map/dot_general | solution.py:12
  73.3 2.7 %fusion.15 = f32[512,224]{0,1:T(8,128)S(1)} fusion(bf16[512,8192]{1,0:T(8,128)(2,1)S(1)} %copy-done.3, bf16[8192,224]{0,1:T(8,128)(2,1)S(1)} %copy-done.4), kind=kOutput, calls=%fused_computation.28 | convolution fusion | flops 1879048192 | bytes 12517376 | tf_op jit(solution)/shard_map/dot_general | solution.py:13
  76.3 44.0 %all-gather.5.cloned.1.call-done = bf16[512,8192]{1,0:T(8,128)(2,1)} async-done(((bf16[32,8192]{1,0:T(8,128)(2,1)}), bf16[512,8192]{1,0:T(8,128)(2,1)}) %all-gather.5.cloned.1.call-update) | async-done | bytes 8388624 | tf_op jit(solution)/shard_map/all_gather | solution.py:65
  120.3 7.1 %fusion.14 = f32[512,224]{0,1:T(8,128)S(1)} fusion(bf16[512,8192]{1,0:T(8,128)(2,1)} %all-gather.5.cloned.1.call-done, bf16[224,8192]{1,0:T(8,128)(2,1)} %param.19), kind=kOutput, calls=%fused_computation.27 | convolution fusion | flops 1879048192 | bytes 12517376 | tf_op jit(solution)/shard_map/dot_general | solution.py:14
  128.3 1.0 reshape.37
  129.2 8.8 %all-to-all-start = ((f32[128,4,192]{2,1,0:T(4,128)}), f32[128,4,192]{2,1,0:T(4,128)S(1)}, u32[]{:S(2)}, u32[]{:S(2)}) async-start(f32[128,4,192]{2,1,0:T(4,128)} %reshape.37), calls=%async_computation | async-start | bytes 1048576 | tf_op jit(solution)/shard_map/all_to_all | solution.py:35
  138.0 5.7 %fusion.17 = f32[512,64]{1,0:T(8,128)S(1)} fusion(bf16[512,8192]{1,0:T(8,128)(2,1)} %all-gather.3.cloned.1.call-done, bf16[8192,64]{0,1:T(8,128)(2,1)S(1)} %copy-done), kind=kOutput, calls=%fused_computation.30 | convolution fusion | flops 536870912 | bytes 9568256 | tf_op jit(solution)/shard_map/dot_general | solution.py:72
  143.7 5.7 %fusion.13 = f32[512,64]{1,0:T(8,128)S(1)} fusion(bf16[512,8192]{1,0:T(8,128)(2,1)} %all-gather.3.cloned.1.call-done, bf16[8192,64]{0,1:T(8,128)(2,1)S(1)} %copy-done.5), kind=kOutput, calls=%fused_computation.26 | convolution fusion | flops 536870912 | bytes 9568256 | tf_op jit(solution)/shard_map/dot_general | solution.py:71
  149.4 2.6 %all-to-all-done = f32[128,4,192]{2,1,0:T(4,128)S(1)} async-done(((f32[128,4,192]{2,1,0:T(4,128)}), f32[128,4,192]{2,1,0:T(4,128)S(1)}, u32[]{:S(2)}, u32[]{:S(2)}) %all-to-all-start) | async-done | bytes 393248 | tf_op jit(solution)/shard_map/all_to_all | solution.py:35
  152.2 0.9 broadcast_in_dim.2
  153.1 7.2 %all-to-all-start.1 = ((f32[128,4,192]{2,1,0:T(4,128)}), f32[128,4,192]{2,1,0:T(4,128)S(1)}, u32[]{:S(2)}, u32[]{:S(2)}) async-start(f32[128,4,192]{2,1,0:T(4,128)} %broadcast_in_dim.2), calls=%async_computation.1 | async-start | bytes 1048576 | tf_op jit(solution)/shard_map/all_to_all | solution.py:40
  160.3 6.7 %fusion.18 = f32[512,64]{1,0:T(8,128)} fusion(bf16[512,8192]{1,0:T(8,128)(2,1)} %all-gather.5.cloned.1.call-done, bf16[8192,64]{0,1:T(8,128)(2,1)} %param.22), kind=kOutput, calls=%fused_computation.31 | convolution fusion | flops 536870912 | bytes 9568256 | tf_op jit(solution)/shard_map/dot_general | solution.py:73
  167.0 7.3 %all-to-all-done.1 = f32[128,4,192]{2,1,0:T(4,128)S(1)} async-done(((f32[128,4,192]{2,1,0:T(4,128)}), f32[128,4,192]{2,1,0:T(4,128)S(1)}, u32[]{:S(2)}, u32[]{:S(2)}) %all-to-all-start.1) | async-done | bytes 393248 | tf_op jit(solution)/shard_map/all_to_all | solution.py:40
  174.6 1.1 fusion.1
  175.7 1.1 fusion
  176.8 2.0 fusion.2
  180.6 0.9 reshape.45
  181.4 3.9 %all-to-all-start.2 = ((f32[128,1,128]{2,1,0:T(1,128)}), f32[128,1,128]{2,1,0:T(1,128)S(1)}, u32[]{:S(2)}, u32[]{:S(2)}) async-start(f32[128,1,128]{2,1,0:T(1,128)} %reshape.45), calls=%async_computation.2 | async-start | bytes 131072 | tf_op jit(solution)/shard_map/all_to_all | solution.py:35
  185.3 0.7 constant_dynamic-slice_fusion
  186.0 9.2 %all-to-all-done.2 = f32[128,1,128]{2,1,0:T(1,128)S(1)} async-done(((f32[128,1,128]{2,1,0:T(1,128)}), f32[128,1,128]{2,1,0:T(1,128)S(1)}, u32[]{:S(2)}, u32[]{:S(2)}) %all-to-all-start.2) | async-done | bytes 65568 | tf_op jit(solution)/shard_map/all_to_all | solution.py:35
  195.8 0.8 reduce
  196.8 0.7 reduce_sum.19
  (38 shorter events, 6.0 us)
Async XLA Ops:
  7.2 130.9 %copy-start = (bf16[8192,64]{0,1:T(8,128)(2,1)S(1)}, bf16[8192,64]{0,1:T(8,128)(2,1)}, u32[]{:S(2)}) copy-start(bf16[8192,64]{0,1:T(8,128)(2,1)} %param.21) | copy-start | bytes 3145732
  7.2 58.2 %all-gather.3.cloned.1.call-start = ((), (), s32[]{:S(2)}) async-start(), calls=%async_computation.3 | async-start | bytes 8912896 | tf_op jit(solution)/shard_map/all_gather | solution.py:64
  7.9 112.4 %all-gather.5.cloned.1.call-start = ((), (), s32[]{:S(2)}) async-start(), calls=%async_computation.4 | async-start | bytes 8912896 | tf_op jit(solution)/shard_map/all_gather | solution.py:65
  65.4 7.3 %copy-start.3 = (bf16[512,8192]{1,0:T(8,128)(2,1)S(1)}, bf16[512,8192]{1,0:T(8,128)(2,1)}, u32[]{:S(2)}) copy-start(bf16[512,8192]{1,0:T(8,128)(2,1)} %all-gather.3.cloned.1.call-done) | copy-start | bytes 25165828
  65.4 7.9 %copy-start.4 = (bf16[8192,224]{0,1:T(8,128)(2,1)S(1)}, bf16[8192,224]{0,1:T(8,128)(2,1)}, u32[]{:S(2)}) copy-start(bf16[8192,224]{0,1:T(8,128)(2,1)} %param.18) | copy-start | bytes 11010052
  73.3 2.7 %copy-start.6 = (bf16[224,64]{0,1:T(8,128)(2,1)S(1)}, bf16[224,64]{0,1:T(8,128)(2,1)}, u32[]{:S(2)}) copy-start(bf16[224,64]{0,1:T(8,128)(2,1)} %param.25) | copy-start | bytes 86020
  76.0 51.4 %copy-start.7 = (bf16[224,64]{0,1:T(8,128)(2,1)S(1)}, bf16[224,64]{0,1:T(8,128)(2,1)}, u32[]{:S(2)}) copy-start(bf16[224,64]{0,1:T(8,128)(2,1)} %param.23) | copy-start | bytes 86020
  76.3 51.5 %copy-start.8 = (bf16[224,64]{0,1:T(8,128)(2,1)S(1)}, bf16[224,64]{0,1:T(8,128)(2,1)}, u32[]{:S(2)}) copy-start(bf16[224,64]{0,1:T(8,128)(2,1)} %param.24) | copy-start | bytes 86020
  127.8 16.0 %copy-start.5 = (bf16[8192,64]{0,1:T(8,128)(2,1)S(1)}, bf16[8192,64]{0,1:T(8,128)(2,1)}, u32[]{:S(2)}) copy-start(bf16[8192,64]{0,1:T(8,128)(2,1)} %param.20) | copy-start | bytes 3145732
  129.2 22.8 %all-to-all-start = ((f32[128,4,192]{2,1,0:T(4,128)}), f32[128,4,192]{2,1,0:T(4,128)S(1)}, u32[]{:S(2)}, u32[]{:S(2)}) async-start(f32[128,4,192]{2,1,0:T(4,128)} %reshape.37), calls=%async_computation | async-start | bytes 1048576 | tf_op jit(solution)/shard_map/all_to_all | solution.py:35
  153.1 21.2 %all-to-all-start.1 = ((f32[128,4,192]{2,1,0:T(4,128)}), f32[128,4,192]{2,1,0:T(4,128)S(1)}, u32[]{:S(2)}, u32[]{:S(2)}) async-start(f32[128,4,192]{2,1,0:T(4,128)} %broadcast_in_dim.2), calls=%async_computation.1 | async-start | bytes 1048576 | tf_op jit(solution)/shard_map/all_to_all | solution.py:40
  160.3 19.5 %copy-start.1 = (bf16[32,12288]{1,0:T(8,128)(2,1)S(1)}, bf16[32,12288]{1,0:T(8,128)(2,1)}, u32[]{:S(2)}) copy-start(bf16[32,12288]{1,0:T(8,128)(2,1)} %param.26) | copy-start | bytes 2359300
  160.3 19.8 %copy-start.2 = (s32[32]{0:T(128)S(1)}, s32[32]{0:T(128)}, u32[]{:S(2)}) copy-start(s32[32]{0:T(128)} %param.27) | copy-start | bytes 388
  181.4 13.8 %all-to-all-start.2 = ((f32[128,1,128]{2,1,0:T(1,128)}), f32[128,1,128]{2,1,0:T(1,128)S(1)}, u32[]{:S(2)}, u32[]{:S(2)}) async-start(f32[128,1,128]{2,1,0:T(1,128)} %reshape.45), calls=%async_computation.2 | async-start | bytes 131072 | tf_op jit(solution)/shard_map/all_to_all | solution.py:35
Sparse Core Ops, SparseCore 0:
  9.7 55.6 all-gather.2
  67.1 53.1 all-gather.4

commit v2 on v1

--- a/solution.py
+++ b/solution.py
@@ -61,8 +61,9 @@
     proj_rank = gate_in_proj.shape[1]
     pad_mask = (token_ids != 0).astype(jnp.bfloat16)[:, None]
     masked = cotangent * pad_mask
-    act_rows = lax.all_gather(hidden_in, "dp", axis=0, tiled=True)
-    cot_rows = lax.all_gather(masked, "dp", axis=0, tiled=True)
+    both = lax.all_gather(jnp.concatenate([hidden_in, masked], axis=1), "dp", axis=0, tiled=True)
+    act_rows = both[:, : hidden_in.shape[1]]
+    cot_rows = both[:, hidden_in.shape[1] :]
     gate_pre, up_pre, back_pre = through_layer(
         act_rows, cot_rows, gate_weight, up_weight, down_weight
     )

time: 205 us -> 201 us (0.980)
  waiting for transfers between devices: 119 us -> 115 us
  matrix products: 41 us -> 38.7 us
    all_gather x2 -> x1, waiting for transfers between devices: 98.9 us -> 95.4 us  [body(): lax.all_gather(jnp.concatenate([hidden_in, masked], axis=1), 'dp', axis=0...]
    dot_general x1, matrix products: 7.11 us -> 4.87 us  [through_layer(): lax.dot_general(cot_rows, down_part, (((1,), (1,)), ((), ())), preferred_...]
    concatenate x0 -> x1, other arithmetic: none -> 2.1 us  [body(): jnp.concatenate([hidden_in, masked], axis=1)]
  transfers between devices with their start and end apart: 5 -> 4, of which waited for: 5 -> 4; matrix products, arithmetic and copies ran while one was open for 15% -> 9% of each run, Pallas kernels for 0% -> 0%
where the time goes in v2:
time: 201 us
  waiting for transfers between devices  115 us (57%)
  matrix products  38.7 us (19%)
  starting transfers between devices  19.9 us (10%)
  between operations  14.3 us (7%)
  local copies, waits for them, and re-layouts  7.26 us (4%)
  other arithmetic  5.89 us (3%)
    all_gather x1, waiting for transfers between devices, body(): lax.all_gather(jnp.concatenate([hidden_in, masked], axis=1), 'dp', axis=0...  95.4 us
    all_to_all x2, starting transfers between devices, scatter_sum(): return jnp.sum(lax.all_to_all(blocks, ALL, 0, 0, tiled=False), axis=0)  12.7 us
    all_to_all x2, waiting for transfers between devices, scatter_sum(): return jnp.sum(lax.all_to_all(blocks, ALL, 0, 0, tiled=False), axis=0)  11.8 us
    all_to_all x1, waiting for transfers between devices, gather_rows(): got = lax.all_to_all(copies, ALL, 0, 0, tiled=False)  7.34 us
    dot_general x1, matrix products, through_layer(): gate_pre = jnp.dot(act_rows, gate_part, preferred_element_type=jnp.float32)  7.26 us
    all_to_all x1, starting transfers between devices, gather_rows(): got = lax.all_to_all(copies, ALL, 0, 0, tiled=False)  7.15 us
    dot_general x1, matrix products, body(): jnp.dot(cot_rows, down_out_proj, preferred_element_type=jnp.float32)  6.69 us
    dot_general x1, matrix products, body(): in_up = jnp.dot(act_rows, up_in_proj, preferred_element_type=jnp.float32)  5.69 us
  transfers between devices with their start and end apart: 4, of which 4 were waited for; matrix products, arithmetic and copies ran while one was open for 9% of the time, Pallas kernels for 0%

profile of v2, /device:TPU:1, one launch (start us, length us, event | category | flops | bytes accessed | tf_op | source)
XLA Modules:
  0.0 200.6 jit_solution(12197100085874266895)
XLA Ops:
  7.2 0.7 compare_convert_fusion
  8.0 1.1 broadcast_multiply_fusion
  9.1 2.1 %pad_maximum_fusion = bf16[32,16384]{1,0:T(8,128)(2,1)} fusion(bf16[32,8192]{1,0:T(8,128)(2,1)S(1)} %broadcast_multiply_fusion, bf16[32,8192]{1,0:T(8,128)(2,1)} %param.15), kind=kLoop, calls=%fused_computation.19 | loop fusion | flops 2097152 | bytes 2097152 | tf_op jit(solution)/shard_map/concatenate | solution.py:64
  11.2 95.4 %all-gather.2.cloned.1.call-done = bf16[512,16384]{1,0:T(8,128)(2,1)} async-done(((bf16[32,16384]{1,0:T(8,128)(2,1)}), bf16[512,16384]{1,0:T(8,128)(2,1)}) %all-gather.2.cloned.1.call-update) | async-done | bytes 16777232 | tf_op jit(solution)/shard_map/all_gather | solution.py:64
  106.6 7.3 %fusion.6 = f32[512,224]{0,1:T(8,128)S(1)} fusion(bf16[8192,224]{0,1:T(8,128)(2,1)} %param.17, bf16[512,16384]{1,0:T(8,128)(2,1)} %all-gather.2.cloned.1.call-done), kind=kOutput, calls=%fused_computation.6 | convolution fusion | flops 1879048192 | bytes 12517376 | tf_op jit(solution)/shard_map/dot_general | solution.py:12
  113.9 1.9 copy-done.3
  115.8 4.9 %fusion.2 = f32[512,224]{0,1:T(8,128)S(1)} fusion(bf16[224,8192]{1,0:T(8,128)(2,1)} %param.19, bf16[512,16384]{1,0:T(8,128)(2,1)S(1)} %copy-done.3), kind=kOutput, calls=%fused_computation.2 | convolution fusion | flops 1879048192 | bytes 12517376 | tf_op jit(solution)/shard_map/dot_general | solution.py:14
  121.0 2.7 %fusion.8 = f32[512,224]{0,1:T(8,128)S(1)} fusion(bf16[8192,224]{0,1:T(8,128)(2,1)S(1)} %copy-done.4, bf16[512,16384]{1,0:T(8,128)(2,1)S(1)} %copy-done.3), kind=kOutput, calls=%fused_computation.8 | convolution fusion | flops 1879048192 | bytes 12517376 | tf_op jit(solution)/shard_map/dot_general | solution.py:13
  124.5 1.0 reshape.37
  125.5 8.8 %all-to-all-start = ((f32[128,4,192]{2,1,0:T(4,128)}), f32[128,4,192]{2,1,0:T(4,128)S(1)}, u32[]{:S(2)}, u32[]{:S(2)}) async-start(f32[128,4,192]{2,1,0:T(4,128)} %reshape.37), calls=%async_computation | async-start | bytes 1048576 | tf_op jit(solution)/shard_map/all_to_all | solution.py:35
  134.3 5.7 %fusion.10 = f32[512,64]{1,0:T(8,128)S(1)} fusion(bf16[8192,64]{0,1:T(8,128)(2,1)S(1)} %copy-done, bf16[512,16384]{1,0:T(8,128)(2,1)} %all-gather.2.cloned.1.call-done), kind=kOutput, calls=%fused_computation.10 | convolution fusion | flops 536870912 | bytes 9568256 | tf_op jit(solution)/shard_map/dot_general | solution.py:72
  140.0 5.7 %fusion.4 = f32[512,64]{1,0:T(8,128)S(1)} fusion(bf16[8192,64]{0,1:T(8,128)(2,1)S(1)} %copy-done.5, bf16[512,16384]{1,0:T(8,128)(2,1)} %all-gather.2.cloned.1.call-done), kind=kOutput, calls=%fused_computation.4 | convolution fusion | flops 536870912 | bytes 9568256 | tf_op jit(solution)/shard_map/dot_general | solution.py:73
  145.7 2.6 %all-to-all-done = f32[128,4,192]{2,1,0:T(4,128)S(1)} async-done(((f32[128,4,192]{2,1,0:T(4,128)}), f32[128,4,192]{2,1,0:T(4,128)S(1)}, u32[]{:S(2)}, u32[]{:S(2)}) %all-to-all-start) | async-done | bytes 393248 | tf_op jit(solution)/shard_map/all_to_all | solution.py:35
  148.5 0.9 broadcast_in_dim.2
  149.4 7.2 %all-to-all-start.1 = ((f32[128,4,192]{2,1,0:T(4,128)}), f32[128,4,192]{2,1,0:T(4,128)S(1)}, u32[]{:S(2)}, u32[]{:S(2)}) async-start(f32[128,4,192]{2,1,0:T(4,128)} %broadcast_in_dim.2), calls=%async_computation.1 | async-start | bytes 1048576 | tf_op jit(solution)/shard_map/all_to_all | solution.py:40
  156.6 6.7 %fusion = f32[512,64]{1,0:T(8,128)} fusion(bf16[8192,64]{0,1:T(8,128)(2,1)} %param.22, bf16[512,16384]{1,0:T(8,128)(2,1)} %all-gather.2.cloned.1.call-done), kind=kOutput, calls=%fused_computation | convolution fusion | flops 536870912 | bytes 9568256 | tf_op jit(solution)/shard_map/dot_general | solution.py:74
  163.3 7.3 %all-to-all-done.1 = f32[128,4,192]{2,1,0:T(4,128)S(1)} async-done(((f32[128,4,192]{2,1,0:T(4,128)}), f32[128,4,192]{2,1,0:T(4,128)S(1)}, u32[]{:S(2)}, u32[]{:S(2)}) %all-to-all-start.1) | async-done | bytes 393248 | tf_op jit(solution)/shard_map/all_to_all | solution.py:40
  170.9 1.1 fusion.12
  172.0 1.1 fusion.13
  173.1 2.0 %fusion.14 = bf16[16,1,64,64]{3,2,0,1:T(8,128)(2,1)S(1)} fusion(f32[16,32,64]{2,1,0:T(8,128)S(1)} %bitcast.35, f32[16,32,64]{2,1,0:T(8,128)} %bitcast.40), kind=kOutput, calls=%fused_computation.18 | convolution fusion | flops 25231360 | bytes 393216 | tf_op jit(solution)/shard_map/dlr,dls->drs/dot_general | solution.py:80
  176.9 0.9 reshape.45
  177.7 3.9 %all-to-all-start.2 = ((f32[128,1,128]{2,1,0:T(1,128)}), f32[128,1,128]{2,1,0:T(1,128)S(1)}, u32[]{:S(2)}, u32[]{:S(2)}) async-start(f32[128,1,128]{2,1,0:T(1,128)} %reshape.45), calls=%async_computation.2 | async-start | bytes 131072 | tf_op jit(solution)/shard_map/all_to_all | solution.py:35
  182.3 9.2 %all-to-all-done.2 = f32[128,1,128]{2,1,0:T(1,128)S(1)} async-done(((f32[128,1,128]{2,1,0:T(1,128)}), f32[128,1,128]{2,1,0:T(1,128)S(1)}, u32[]{:S(2)}, u32[]{:S(2)}) %all-to-all-start.2) | async-done | bytes 65568 | tf_op jit(solution)/shard_map/all_to_all | solution.py:35
  192.1 0.8 reduce
  (36 shorter events, 5.5 us)
Async XLA Ops:
  7.2 127.2 %copy-start = (bf16[8192,64]{0,1:T(8,128)(2,1)S(1)}, bf16[8192,64]{0,1:T(8,128)(2,1)}, u32[]{:S(2)}) copy-start(bf16[8192,64]{0,1:T(8,128)(2,1)} %param.20) | copy-start | bytes 3145732
  7.2 99.4 %all-gather.2.cloned.1.call-start = ((), (), s32[]{:S(2)}) async-start(), calls=%async_computation.3 | async-start | bytes 17825792 | tf_op jit(solution)/shard_map/all_gather | solution.py:64
  106.6 9.2 %copy-start.3 = (bf16[512,16384]{1,0:T(8,128)(2,1)S(1)}, bf16[512,16384]{1,0:T(8,128)(2,1)}, u32[]{:S(2)}) copy-start(bf16[512,16384]{1,0:T(8,128)(2,1)} %all-gather.2.cloned.1.call-done) | copy-start | bytes 50331652
  115.8 4.9 %copy-start.6 = (bf16[224,64]{0,1:T(8,128)(2,1)S(1)}, bf16[224,64]{0,1:T(8,128)(2,1)}, u32[]{:S(2)}) copy-start(bf16[224,64]{0,1:T(8,128)(2,1)} %param.24) | copy-start | bytes 86020
  115.8 5.2 %copy-start.4 = (bf16[8192,224]{0,1:T(8,128)(2,1)S(1)}, bf16[8192,224]{0,1:T(8,128)(2,1)}, u32[]{:S(2)}) copy-start(bf16[8192,224]{0,1:T(8,128)(2,1)} %param.18) | copy-start | bytes 11010052
  121.0 2.7 %copy-start.7 = (bf16[224,64]{0,1:T(8,128)(2,1)S(1)}, bf16[224,64]{0,1:T(8,128)(2,1)}, u32[]{:S(2)}) copy-start(bf16[224,64]{0,1:T(8,128)(2,1)} %param.23) | copy-start | bytes 86020
  121.0 3.0 %copy-start.8 = (bf16[224,64]{0,1:T(8,128)(2,1)S(1)}, bf16[224,64]{0,1:T(8,128)(2,1)}, u32[]{:S(2)}) copy-start(bf16[224,64]{0,1:T(8,128)(2,1)} %param.25) | copy-start | bytes 86020
  124.5 15.5 %copy-start.5 = (bf16[8192,64]{0,1:T(8,128)(2,1)S(1)}, bf16[8192,64]{0,1:T(8,128)(2,1)}, u32[]{:S(2)}) copy-start(bf16[8192,64]{0,1:T(8,128)(2,1)} %param.21) | copy-start | bytes 3145732
  125.5 22.9 %all-to-all-start = ((f32[128,4,192]{2,1,0:T(4,128)}), f32[128,4,192]{2,1,0:T(4,128)S(1)}, u32[]{:S(2)}, u32[]{:S(2)}) async-start(f32[128,4,192]{2,1,0:T(4,128)} %reshape.37), calls=%async_computation | async-start | bytes 1048576 | tf_op jit(solution)/shard_map/all_to_all | solution.py:35
  149.4 21.2 %all-to-all-start.1 = ((f32[128,4,192]{2,1,0:T(4,128)}), f32[128,4,192]{2,1,0:T(4,128)S(1)}, u32[]{:S(2)}, u32[]{:S(2)}) async-start(f32[128,4,192]{2,1,0:T(4,128)} %broadcast_in_dim.2), calls=%async_computation.1 | async-start | bytes 1048576 | tf_op jit(solution)/shard_map/all_to_all | solution.py:40
  156.5 19.5 %copy-start.1 = (bf16[32,12288]{1,0:T(8,128)(2,1)S(1)}, bf16[32,12288]{1,0:T(8,128)(2,1)}, u32[]{:S(2)}) copy-start(bf16[32,12288]{1,0:T(8,128)(2,1)} %param.26) | copy-start | bytes 2359300
  163.2 13.1 %copy-start.2 = (s32[32]{0:T(128)S(1)}, s32[32]{0:T(128)}, u32[]{:S(2)}) copy-start(s32[32]{0:T(128)} %param.27) | copy-start | bytes 388
  177.7 13.8 %all-to-all-start.2 = ((f32[128,1,128]{2,1,0:T(1,128)}), f32[128,1,128]{2,1,0:T(1,128)S(1)}, u32[]{:S(2)}, u32[]{:S(2)}) async-start(f32[128,1,128]{2,1,0:T(1,128)} %reshape.45), calls=%async_computation.2 | async-start | bytes 131072 | tf_op jit(solution)/shard_map/all_to_all | solution.py:35
Sparse Core Ops, SparseCore 0:
  11.4 95.1 all-gather.1

commit v3 on v2

--- a/solution.py
+++ b/solution.py
@@ -3,31 +3,92 @@
 from jax import lax
 from jax.sharding import PartitionSpec as P
 
+from jax.experimental import pallas as pl
+from jax.experimental.pallas import tpu as pltpu
+
 LEN = 32
 EX_DEV = 8
 ALL = ("dp", "tensor")
 
-
-def through_layer(act_rows, cot_rows, gate_part, up_part, down_part):
-    gate_pre = jnp.dot(act_rows, gate_part, preferred_element_type=jnp.float32)
-    up_pre = jnp.dot(act_rows, up_part, preferred_element_type=jnp.float32)
-    back_pre = lax.dot_general(
-        cot_rows, down_part, (((1,), (1,)), ((), ())), preferred_element_type=jnp.float32
-    )
-    return (gate_pre, up_pre, back_pre)
+KC = 1024
 
 
-def project_rows(gate_pre, up_pre, back_pre, gate_out_proj, up_out_proj, down_in_proj):
-    squash = jax.nn.sigmoid(gate_pre)
-    hidden = (gate_pre * squash * up_pre).astype(jnp.bfloat16)
-    grad_up = (back_pre * gate_pre * squash).astype(jnp.bfloat16)
-    grad_gate = (back_pre * up_pre * squash * (1.0 + gate_pre * (1.0 - squash))).astype(
-        jnp.bfloat16
-    )
-    side_gate = jnp.dot(grad_gate, gate_out_proj, preferred_element_type=jnp.float32)
-    side_up = jnp.dot(grad_up, up_out_proj, preferred_element_type=jnp.float32)
-    side_down = jnp.dot(hidden, down_in_proj, preferred_element_type=jnp.float32)
-    return jnp.concatenate([side_gate, side_up, side_down], axis=1)
+def layer_kernel(act_ref, cot_ref, gw_ref, uw_ref, dw_ref, gi_ref, ui_ref, do_ref,
+                 go_ref, uo_ref, di_ref, side_ref, inp_ref, g_acc, u_acc, b_acc, i_acc):
+    k = pl.program_id(0)
+
+    @pl.when(k == 0)
+    def _():
+        g_acc[...] = jnp.zeros_like(g_acc)
+        u_acc[...] = jnp.zeros_like(u_acc)
+        b_acc[...] = jnp.zeros_like(b_acc)
+        i_acc[...] = jnp.zeros_like(i_acc)
+
+    a = act_ref[...]
+    c = cot_ref[...]
+    f32 = jnp.float32
+    g_acc[...] += jnp.dot(a, gw_ref[...], preferred_element_type=f32)
+    u_acc[...] += jnp.dot(a, uw_ref[...], preferred_element_type=f32)
+    b_acc[...] += lax.dot_general(c, dw_ref[...], (((1,), (1,)), ((), ())), preferred_element_type=f32)
+    r = gi_ref.shape[1]
+    i_acc[:, 0:r] += jnp.dot(a, gi_ref[...], preferred_element_type=f32)
+    i_acc[:, r:2 * r] += jnp.dot(a, ui_ref[...], preferred_element_type=f32)
+    i_acc[:, 2 * r:3 * r] += jnp.dot(c, do_ref[...], preferred_element_type=f32)
+
+    @pl.when(k == pl.num_programs(0) - 1)
+    def _():
+        g = g_acc[...]
+        u = u_acc[...]
+        b = b_acc[...]
+        s = jax.nn.sigmoid(g)
+        hidden = (g * s * u).astype(jnp.bfloat16)
+        grad_up = (b * g * s).astype(jnp.bfloat16)
+        grad_gate = (b * u * s * (1.0 + g * (1.0 - s))).astype(jnp.bfloat16)
+        side_ref[:, 0:r] = jnp.dot(grad_gate, go_ref[...], preferred_element_type=f32)
+        side_ref[:, r:2 * r] = jnp.dot(grad_up, uo_ref[...], preferred_element_type=f32)
+        side_ref[:, 2 * r:3 * r] = jnp.dot(hidden, di_ref[...], preferred_element_type=f32)
+        inp_ref[...] = i_acc[...]
+
+
+def layer_call(both, gw, uw, dw, gi, ui, do, go, uo, di):
+    rows, width = both.shape
+    d = width // 2
+    ff = gw.shape[1]
+    r = gi.shape[1]
+    nk = d // KC
+    f32 = jnp.float32
+    full = lambda shape: pl.BlockSpec(shape, lambda k: (0, 0))
+    return pl.pallas_call(
+        layer_kernel,
+        grid=(nk,),
+        in_specs=[
+            pl.BlockSpec((rows, KC), lambda k: (0, k)),
+            pl.BlockSpec((rows, KC), lambda k: (0, k + nk)),
+            pl.BlockSpec((KC, ff), lambda k: (k, 0)),
+            pl.BlockSpec((KC, ff), lambda k: (k, 0)),
+            pl.BlockSpec((ff, KC), lambda k: (0, k)),
+            pl.BlockSpec((KC, r), lambda k: (k, 0)),
+            pl.BlockSpec((KC, r), lambda k: (k, 0)),
+            pl.BlockSpec((KC, r), lambda k: (k, 0)),
+            full((ff, r)),
+            full((ff, r)),
+            full((ff, r)),
+        ],
+        out_specs=[full((rows, 3 * r)), full((rows, 3 * r))],
+        out_shape=[jax.ShapeDtypeStruct((rows, 3 * r), f32), jax.ShapeDtypeStruct((rows, 3 * r), f32)],
+        scratch_shapes=[
+            pltpu.VMEM((rows, ff), f32),
+            pltpu.VMEM((rows, ff), f32),
+            pltpu.VMEM((rows, ff), f32),
+            pltpu.VMEM((rows, 3 * r), f32),
+        ],
+        compiler_params=pltpu.CompilerParams(dimension_semantics=("arbitrary",)),
+        cost_estimate=pl.CostEstimate(
+            flops=2 * rows * d * (3 * ff + 3 * r) + 2 * rows * ff * 3 * r,
+            transcendentals=rows * ff,
+            bytes_accessed=2 * (rows * width + 3 * d * ff + 3 * d * r + 3 * ff * r) + 8 * rows * 3 * r,
+        ),
+    )(both, both, gw, uw, dw, gi, ui, do, go, uo, di)
 
 
 def scatter_sum(x, n):
@@ -62,17 +123,15 @@
     pad_mask = (token_ids != 0).astype(jnp.bfloat16)[:, None]
     masked = cotangent * pad_mask
     both = lax.all_gather(jnp.concatenate([hidden_in, masked], axis=1), "dp", axis=0, tiled=True)
-    act_rows = both[:, : hidden_in.shape[1]]
-    cot_rows = both[:, hidden_in.shape[1] :]
-    gate_pre, up_pre, back_pre = through_layer(
-        act_rows, cot_rows, gate_weight, up_weight, down_weight
+    block, inputs = layer_call(
+        both, gate_weight, up_weight, down_weight, gate_in_proj, up_in_proj, down_out_proj,
+        gate_out_proj, up_out_proj, down_in_proj,
     )
-    block = project_rows(gate_pre, up_pre, back_pre, gate_out_proj, up_out_proj, down_in_proj)
     summed = gather_rows(scatter_sum(block, n_all), n_all)
-    in_gate = jnp.dot(act_rows, gate_in_proj, preferred_element_type=jnp.float32)
-    in_up = jnp.dot(act_rows, up_in_proj, preferred_element_type=jnp.float32)
-    out_down = jnp.dot(cot_rows, down_out_proj, preferred_element_type=jnp.float32)
-    docs = act_rows.shape[0] // LEN
+    in_gate = inputs[:, :proj_rank]
+    in_up = inputs[:, proj_rank : 2 * proj_rank]
+    out_down = inputs[:, 2 * proj_rank :]
+    docs = both.shape[0] // LEN
 
     def doc_outer(left, right):
         left_docs = left.reshape(docs, LEN, proj_rank)

time: 201 us -> 200 us (level)
  matrix products: 38.7 us -> 4.02 us
  blocking collectives: 0 us -> 22.7 us
  Pallas kernels: 0 us -> 20.5 us
  local copies, waits for them, and re-layouts: 7.26 us -> 25.7 us
  waiting for transfers between devices: 115 us -> 98.3 us
  starting transfers between devices: 19.9 us -> 7.82 us
    dot_general x9 -> x0, matrix products: 33.7 us -> none  [the longest x1 7.26 us: through_layer(): gate_pre = jnp.dot(act_rows, gate_part, preferred_element_type=jnp.float32)]
    all_to_all x0 -> x1, blocking collectives: none -> 22.7 us  [scatter_sum(): return jnp.sum(lax.all_to_all(blocks, ALL, 0, 0, tiled=False), axis=0)]
    pallas_call x0 -> x1, Pallas kernels: none -> 20.5 us  [layer_call(): pl.pallas_call(layer_kernel, grid=(nk,), in_specs=[pl.BlockSpec((rows, KC...]
    all_gather x1, waiting for transfers between devices: 95.4 us -> 75.1 us  [body(): lax.all_gather(jnp.concatenate([hidden_in, masked], axis=1), 'dp', axis=0...]
    unnamed x20 -> x28, local copies, waits for them, and re-layouts: 3.02 us -> 21.3 us
    all_to_all x2 -> x1, starting transfers between devices: 12.7 us -> 3.89 us  [scatter_sum(): return jnp.sum(lax.all_to_all(blocks, ALL, 0, 0, tiled=False), axis=0)]
    all_to_all x1, waiting for transfers between devices: 7.34 us -> 13.9 us  [gather_rows(): got = lax.all_to_all(copies, ALL, 0, 0, tiled=False)]
    all_to_all x1, starting transfers between devices: 7.15 us -> 3.89 us  [gather_rows(): got = lax.all_to_all(copies, ALL, 0, 0, tiled=False)]
  transfers between devices with their start and end apart: 4 -> 3, of which waited for: 4 -> 3; matrix products, arithmetic and copies ran while one was open for 9% -> 11% of each run, Pallas kernels for 0% -> 0%
where the time goes in v3:
time: 200 us; the launch traced here: 199 us
  waiting for transfers between devices  98.3 us (49%)
  local copies, waits for them, and re-layouts  25.7 us (13%)
  blocking collectives  22.7 us (11%)
  Pallas kernels  20.5 us (10%)
  between operations  14.2 us (7%)
  starting transfers between devices  7.82 us (4%)
  other arithmetic  5.83 us (3%)
  matrix products  4.02 us (2%)
    all_gather x1, waiting for transfers between devices, body(): lax.all_gather(jnp.concatenate([hidden_in, masked], axis=1), 'dp', axis=0...  75.1 us
    all_to_all x1, blocking collectives, scatter_sum(): return jnp.sum(lax.all_to_all(blocks, ALL, 0, 0, tiled=False), axis=0)  22.7 us
    unnamed x28, local copies, waits for them, and re-layouts  21.3 us
    pallas_call x1, Pallas kernels, layer_call(): pl.pallas_call(layer_kernel, grid=(nk,), in_specs=[pl.BlockSpec((rows, KC...  20.5 us
    all_to_all x1, waiting for transfers between devices, gather_rows(): got = lax.all_to_all(copies, ALL, 0, 0, tiled=False)  13.9 us
    all_to_all x1, waiting for transfers between devices, scatter_sum(): return jnp.sum(lax.all_to_all(blocks, ALL, 0, 0, tiled=False), axis=0)  9.23 us
  transfers between devices with their start and end apart: 3, of which 3 were waited for; matrix products, arithmetic and copies ran while one was open for 11% of the time, Pallas kernels for 0%

profile of v3, /device:TPU:1, one launch (start us, length us, event | category | flops | bytes accessed | tf_op | source)
XLA Modules:
  0.0 199.1 jit_solution(18366205887179702799)
XLA Ops:
  7.9 1.1 broadcast_multiply_fusion
  9.1 2.1 %pad_maximum_fusion = bf16[32,16384]{1,0:T(8,128)(2,1)} fusion(bf16[32,8192]{1,0:T(8,128)(2,1)S(1)} %broadcast_multiply_fusion, bf16[32,8192]{1,0:T(8,128)(2,1)} %param.15), kind=kLoop, calls=%fused_computation.7 | loop fusion | flops 2097152 | bytes 2097152 | tf_op jit(solution)/shard_map/concatenate | solution.py:125
  11.2 6.2 %copy.24.gw_ref = bf16[8192,224]{1,0:T(8,128)(2,1)} copy(bf16[8192,224]{0,1:T(8,128)(2,1)} %param.17) | data formatting | bytes 7340032 | tf_op args[3]
  17.4 6.4 %copy.25.uw_ref = bf16[8192,224]{1,0:T(8,128)(2,1)} copy(bf16[8192,224]{0,1:T(8,128)(2,1)} %param.18) | data formatting | bytes 7340032 | tf_op args[4]
  23.9 1.8 copy.26.gi_ref
  25.7 1.8 copy.27.ui_ref
  27.5 1.8 copy.28.do_ref
  30.0 0.7 copy.30.uo_ref
  30.7 0.7 copy.31.di_ref
  31.5 75.1 %all-gather.2.cloned.1.call-done.act_ref.cot_ref = bf16[512,16384]{1,0:T(8,128)(2,1)} async-done(((bf16[32,16384]{1,0:T(8,128)(2,1)}), bf16[512,16384]{1,0:T(8,128)(2,1)}) %all-gather.2.cloned.1.call-update) | async-done | bytes 16777232 | tf_op jit(solution)/shard_map/all_gather | solution.py:125
  106.6 20.5 %shard_map.149 = (f32[512,192]{1,0:T(8,128)}, f32[512,192]{1,0:T(8,128)}) custom-call(bf16[512,16384]{1,0:T(8,128)(2,1)} %all-gather.2.cloned.1.call-done.act_ref.cot_ref, bf16[512,16384]{1,0:T(8,128)(2,1)} %all-gather.2.cloned.1.call-done.act_ref.cot_ref, bf16[8192,224]{1,0:T(8,128)(2,1)} %copy.24.gw_ref, bf16[8192,224]{1,0:T(8,128)(2,1)} %copy.25.uw_ref, ...), custom_call_target="tpu_custom_call" | custom-call | flops 7291797504 | bytes 31805440 | tf_op jit(solution)/shard_map/pallas_call | solution.py:61
  127.1 1.2 reshape.37
  128.4 22.7 %all_to_all.15 = f32[128,4,192]{2,1,0:T(4,128)S(1)} all-to-all(f32[128,4,192]{2,1,0:T(4,128)S(1)} %reshape.37), channel_id=1, replica_groups=mesh['dp'=16,'tensor'=8] {'dp','tensor'}, dimensions={0} | all-to-all | bytes 786432 | tf_op jit(solution)/shard_map/all_to_all | solution.py:96
  151.2 0.9 broadcast_in_dim.2
  152.1 3.9 %all-to-all-start.1 = ((f32[128,4,192]{2,1,0:T(4,128)}), f32[128,4,192]{2,1,0:T(4,128)S(1)}, u32[]{:S(2)}, u32[]{:S(2)}) async-start(f32[128,4,192]{2,1,0:T(4,128)} %broadcast_in_dim.2), calls=%async_computation.1 | async-start | bytes 1048576 | tf_op jit(solution)/shard_map/all_to_all | solution.py:101
  156.1 13.9 %all-to-all-done.1 = f32[128,4,192]{2,1,0:T(4,128)S(1)} async-done(((f32[128,4,192]{2,1,0:T(4,128)}), f32[128,4,192]{2,1,0:T(4,128)S(1)}, u32[]{:S(2)}, u32[]{:S(2)}) %all-to-all-start.1) | async-done | bytes 393248 | tf_op jit(solution)/shard_map/all_to_all | solution.py:101
  170.4 1.1 fusion
  171.4 1.1 fusion.1
  172.5 1.1 fusion.2
  175.3 0.9 reshape.45
  176.2 3.9 %all-to-all-start.2 = ((f32[128,1,128]{2,1,0:T(1,128)}), f32[128,1,128]{2,1,0:T(1,128)S(1)}, u32[]{:S(2)}, u32[]{:S(2)}) async-start(f32[128,1,128]{2,1,0:T(1,128)} %reshape.45), calls=%async_computation.2 | async-start | bytes 131072 | tf_op jit(solution)/shard_map/all_to_all | solution.py:96
  180.8 9.2 %all-to-all-done.2 = f32[128,1,128]{2,1,0:T(1,128)S(1)} async-done(((f32[128,1,128]{2,1,0:T(1,128)}), f32[128,1,128]{2,1,0:T(1,128)S(1)}, u32[]{:S(2)}, u32[]{:S(2)}) %all-to-all-start.2) | async-done | bytes 65568 | tf_op jit(solution)/shard_map/all_to_all | solution.py:96
  190.5 0.8 reduce
  191.5 0.7 reduce_sum.19
  (34 shorter events, 5.2 us)
Async XLA Ops:
  7.2 167.3 %copy-start = (bf16[32,12288]{1,0:T(8,128)(2,1)S(1)}, bf16[32,12288]{1,0:T(8,128)(2,1)}, u32[]{:S(2)}) copy-start(bf16[32,12288]{1,0:T(8,128)(2,1)} %param.26) | copy-start | bytes 2359300
  7.2 99.4 %all-gather.2.cloned.1.call-start = ((), (), s32[]{:S(2)}) async-start(), calls=%async_computation.3 | async-start | bytes 17825792 | tf_op jit(solution)/shard_map/all_gather | solution.py:125
  17.4 6.5 %copy-start.2 = (bf16[8192,64]{0,1:T(8,128)(2,1)S(1)}, bf16[8192,64]{0,1:T(8,128)(2,1)}, u32[]{:S(2)}) copy-start(bf16[8192,64]{0,1:T(8,128)(2,1)} %param.20) | copy-start | bytes 3145732
  17.4 8.2 %copy-start.3 = (bf16[8192,64]{0,1:T(8,128)(2,1)S(1)}, bf16[8192,64]{0,1:T(8,128)(2,1)}, u32[]{:S(2)}) copy-start(bf16[8192,64]{0,1:T(8,128)(2,1)} %param.21) | copy-start | bytes 3145732
  25.7 1.8 copy-start.4
  25.7 3.6 %copy-start.5 = (bf16[224,64]{0,1:T(8,128)(2,1)S(1)}, bf16[224,64]{0,1:T(8,128)(2,1)}, u32[]{:S(2)}) copy-start(bf16[224,64]{0,1:T(8,128)(2,1)} %param.23) | copy-start | bytes 86020
  25.7 4.3 %copy-start.6 = (bf16[224,64]{0,1:T(8,128)(2,1)S(1)}, bf16[224,64]{0,1:T(8,128)(2,1)}, u32[]{:S(2)}) copy-start(bf16[224,64]{0,1:T(8,128)(2,1)} %param.24) | copy-start | bytes 86020
  25.7 5.0 %copy-start.7 = (bf16[224,64]{0,1:T(8,128)(2,1)S(1)}, bf16[224,64]{0,1:T(8,128)(2,1)}, u32[]{:S(2)}) copy-start(bf16[224,64]{0,1:T(8,128)(2,1)} %param.25) | copy-start | bytes 86020
  127.1 28.9 %copy-start.1 = (f32[512,192]{1,0:T(8,128)S(1)}, f32[512,192]{1,0:T(8,128)}, u32[]{:S(2)}) copy-start(f32[512,192]{1,0:T(8,128)} %get-tuple-element.4) | copy-start | bytes 1179652
  152.1 17.9 %all-to-all-start.1 = ((f32[128,4,192]{2,1,0:T(4,128)}), f32[128,4,192]{2,1,0:T(4,128)S(1)}, u32[]{:S(2)}, u32[]{:S(2)}) async-start(f32[128,4,192]{2,1,0:T(4,128)} %broadcast_in_dim.2), calls=%async_computation.1 | async-start | bytes 1048576 | tf_op jit(solution)/shard_map/all_to_all | solution.py:101
  171.4 3.4 %copy-start.8 = (s32[32]{0:T(128)S(1)}, s32[32]{0:T(128)}, u32[]{:S(2)}) copy-start(s32[32]{0:T(128)} %param.27) | copy-start | bytes 388
  176.2 13.8 %all-to-all-start.2 = ((f32[128,1,128]{2,1,0:T(1,128)}), f32[128,1,128]{2,1,0:T(1,128)S(1)}, u32[]{:S(2)}, u32[]{:S(2)}) async-start(f32[128,1,128]{2,1,0:T(1,128)} %reshape.45), calls=%async_computation.2 | async-start | bytes 131072 | tf_op jit(solution)/shard_map/all_to_all | solution.py:96
Sparse Core Ops, SparseCore 0:
  11.3 95.1 all-gather.1

commit v4 on v3

--- a/solution.py
+++ b/solution.py
@@ -10,44 +10,42 @@
 EX_DEV = 8
 ALL = ("dp", "tensor")
 
-KC = 1024
+KC = 2048
+LANE = 128
 
 
-def layer_kernel(act_ref, cot_ref, gw_ref, uw_ref, dw_ref, gi_ref, ui_ref, do_ref,
-                 go_ref, uo_ref, di_ref, side_ref, inp_ref, g_acc, u_acc, b_acc, i_acc):
+def pad_to(x, cols):
+    return jnp.pad(x, ((0, 0), (0, cols - x.shape[1])))
+
+
+def layer_kernel(act_ref, cot_ref, wa_ref, wc_ref, go_ref, uo_ref, di_ref, side_ref, inp_ref, a_acc, c_acc):
     k = pl.program_id(0)
 
     @pl.when(k == 0)
     def _():
-        g_acc[...] = jnp.zeros_like(g_acc)
-        u_acc[...] = jnp.zeros_like(u_acc)
-        b_acc[...] = jnp.zeros_like(b_acc)
-        i_acc[...] = jnp.zeros_like(i_acc)
+        a_acc[...] = jnp.zeros_like(a_acc)
+        c_acc[...] = jnp.zeros_like(c_acc)
 
-    a = act_ref[...]
-    c = cot_ref[...]
     f32 = jnp.float32
-    g_acc[...] += jnp.dot(a, gw_ref[...], preferred_element_type=f32)
-    u_acc[...] += jnp.dot(a, uw_ref[...], preferred_element_type=f32)
-    b_acc[...] += lax.dot_general(c, dw_ref[...], (((1,), (1,)), ((), ())), preferred_element_type=f32)
-    r = gi_ref.shape[1]
-    i_acc[:, 0:r] += jnp.dot(a, gi_ref[...], preferred_element_type=f32)
-    i_acc[:, r:2 * r] += jnp.dot(a, ui_ref[...], preferred_element_type=f32)
-    i_acc[:, 2 * r:3 * r] += jnp.dot(c, do_ref[...], preferred_element_type=f32)
+    a_acc[...] += jnp.dot(act_ref[...], wa_ref[...], preferred_element_type=f32)
+    c_acc[...] += jnp.dot(cot_ref[...], wc_ref[...], preferred_element_type=f32)
 
     @pl.when(k == pl.num_programs(0) - 1)
     def _():
-        g = g_acc[...]
-        u = u_acc[...]
-        b = b_acc[...]
+        ff, r = go_ref.shape
+        fp = -(-ff // LANE) * LANE
+        g = a_acc[:, 0:ff]
+        u = a_acc[:, fp : fp + ff]
+        b = c_acc[:, 0:ff]
         s = jax.nn.sigmoid(g)
         hidden = (g * s * u).astype(jnp.bfloat16)
         grad_up = (b * g * s).astype(jnp.bfloat16)
         grad_gate = (b * u * s * (1.0 + g * (1.0 - s))).astype(jnp.bfloat16)
         side_ref[:, 0:r] = jnp.dot(grad_gate, go_ref[...], preferred_element_type=f32)
-        side_ref[:, r:2 * r] = jnp.dot(grad_up, uo_ref[...], preferred_element_type=f32)
-        side_ref[:, 2 * r:3 * r] = jnp.dot(hidden, di_ref[...], preferred_element_type=f32)
-        inp_ref[...] = i_acc[...]
+        side_ref[:, r : 2 * r] = jnp.dot(grad_up, uo_ref[...], preferred_element_type=f32)
+        side_ref[:, 2 * r : 3 * r] = jnp.dot(hidden, di_ref[...], preferred_element_type=f32)
+        inp_ref[:, 0 : 2 * r] = a_acc[:, 2 * fp : 2 * fp + 2 * r]
+        inp_ref[:, 2 * r : 3 * r] = c_acc[:, fp : fp + r]
 
 
 def layer_call(both, gw, uw, dw, gi, ui, do, go, uo, di):
@@ -55,6 +53,9 @@
     d = width // 2
     ff = gw.shape[1]
     r = gi.shape[1]
+    fp = -(-ff // LANE) * LANE
+    wa = jnp.concatenate([pad_to(gw, fp), pad_to(uw, fp), pad_to(jnp.concatenate([gi, ui], 1), LANE)], 1)
+    wc = jnp.concatenate([pad_to(dw.T, fp), pad_to(do, LANE)], 1)
     nk = d // KC
     f32 = jnp.float32
     full = lambda shape: pl.BlockSpec(shape, lambda k: (0, 0))
@@ -64,12 +65,8 @@
         in_specs=[
             pl.BlockSpec((rows, KC), lambda k: (0, k)),
             pl.BlockSpec((rows, KC), lambda k: (0, k + nk)),
-            pl.BlockSpec((KC, ff), lambda k: (k, 0)),
-            pl.BlockSpec((KC, ff), lambda k: (k, 0)),
-            pl.BlockSpec((ff, KC), lambda k: (0, k)),
-            pl.BlockSpec((KC, r), lambda k: (k, 0)),
-            pl.BlockSpec((KC, r), lambda k: (k, 0)),
-            pl.BlockSpec((KC, r), lambda k: (k, 0)),
+            pl.BlockSpec((KC, wa.shape[1]), lambda k: (k, 0)),
+            pl.BlockSpec((KC, wc.shape[1]), lambda k: (k, 0)),
             full((ff, r)),
             full((ff, r)),
             full((ff, r)),
@@ -77,18 +74,18 @@
         out_specs=[full((rows, 3 * r)), full((rows, 3 * r))],
         out_shape=[jax.ShapeDtypeStruct((rows, 3 * r), f32), jax.ShapeDtypeStruct((rows, 3 * r), f32)],
         scratch_shapes=[
-            pltpu.VMEM((rows, ff), f32),
-            pltpu.VMEM((rows, ff), f32),
-            pltpu.VMEM((rows, ff), f32),
-            pltpu.VMEM((rows, 3 * r), f32),
+            pltpu.VMEM((rows, wa.shape[1]), f32),
+            pltpu.VMEM((rows, wc.shape[1]), f32),
         ],
-        compiler_params=pltpu.CompilerParams(dimension_semantics=("arbitrary",)),
+        compiler_params=pltpu.CompilerParams(
+            dimension_semantics=("arbitrary",), vmem_limit_bytes=48 * 1024 * 1024
+        ),
         cost_estimate=pl.CostEstimate(
             flops=2 * rows * d * (3 * ff + 3 * r) + 2 * rows * ff * 3 * r,
             transcendentals=rows * ff,
-            bytes_accessed=2 * (rows * width + 3 * d * ff + 3 * d * r + 3 * ff * r) + 8 * rows * 3 * r,
+            bytes_accessed=2 * (rows * width + d * (wa.shape[1] + wc.shape[1]) + 3 * ff * r) + 8 * rows * 3 * r,
         ),
-    )(both, both, gw, uw, dw, gi, ui, do, go, uo, di)
+    )(both, both, wa, wc, go, uo, di)
 
 
 def scatter_sum(x, n):

time: 200 us -> 194 us (0.970)
  waiting for transfers between devices: 98.3 us -> 78 us
  other arithmetic: 5.83 us -> 20.3 us
  local copies, waits for them, and re-layouts: 25.7 us -> 30.4 us
  Pallas kernels: 20.5 us -> 16.3 us
    all_gather x1, waiting for transfers between devices: 75.1 us -> 54.9 us  [body(): lax.all_gather(jnp.concatenate([hidden_in, masked], axis=1), 'dp', axis=0...]
    concatenate x0 -> x2, other arithmetic: none -> 14.5 us  [the longest x1 7.85 us: layer_call(): wc = jnp.concatenate([pad_to(dw.T, fp), pad_to(do, LANE)], 1)]
    unnamed x28 -> x35, local copies, waits for them, and re-layouts: 21.3 us -> 27 us
    pallas_call x1, Pallas kernels: 20.5 us -> 16.3 us  [layer_call(): pl.pallas_call(layer_kernel, grid=(nk,), in_specs=[pl.BlockSpec((rows, KC...]
  transfers between devices with their start and end apart: 3 -> 3, of which waited for: 3 -> 3; matrix products, arithmetic and copies ran while one was open for 11% -> 21% of each run, Pallas kernels for 0% -> 0%
where the time goes in v4:
time: 194 us
  waiting for transfers between devices  78 us (40%)
  local copies, waits for them, and re-layouts  30.4 us (16%)
  blocking collectives  22.7 us (12%)
  other arithmetic  20.3 us (10%)
  Pallas kernels  16.3 us (8%)
  between operations  14.3 us (7%)
  starting transfers between devices  7.83 us (4%)
  matrix products  4.04 us (2%)
    all_gather x1, waiting for transfers between devices, body(): lax.all_gather(jnp.concatenate([hidden_in, masked], axis=1), 'dp', axis=0...  54.9 us
    unnamed x35, local copies, waits for them, and re-layouts  27 us
    all_to_all x1, blocking collectives, scatter_sum(): return jnp.sum(lax.all_to_all(blocks, ALL, 0, 0, tiled=False), axis=0)  22.7 us
    pallas_call x1, Pallas kernels, layer_call(): pl.pallas_call(layer_kernel, grid=(nk,), in_specs=[pl.BlockSpec((rows, KC...  16.3 us
    all_to_all x1, waiting for transfers between devices, gather_rows(): got = lax.all_to_all(copies, ALL, 0, 0, tiled=False)  13.9 us
    all_to_all x1, waiting for transfers between devices, scatter_sum(): return jnp.sum(lax.all_to_all(blocks, ALL, 0, 0, tiled=False), axis=0)  9.23 us
    concatenate x1, other arithmetic, layer_call(): wc = jnp.concatenate([pad_to(dw.T, fp), pad_to(do, LANE)], 1)  7.85 us
    concatenate x1, other arithmetic, layer_call(): jnp.concatenate([pad_to(gw, fp), pad_to(uw, fp), pad_to(jnp.concatenate([...  6.6 us
  transfers between devices with their start and end apart: 3, of which 3 were waited for; matrix products, arithmetic and copies ran while one was open for 21% of the time, Pallas kernels for 0%

profile of v4, /device:TPU:1, one launch (start us, length us, event | category | flops | bytes accessed | tf_op | source)
XLA Modules:
  0.0 193.7 jit_solution(764039294119359939)
XLA Ops:
  7.9 1.1 broadcast_multiply_fusion
  9.1 2.1 %pad_maximum_fusion = bf16[32,16384]{1,0:T(8,128)(2,1)} fusion(bf16[32,8192]{1,0:T(8,128)(2,1)S(1)} %broadcast_multiply_fusion, bf16[32,8192]{1,0:T(8,128)(2,1)} %param.15), kind=kLoop, calls=%fused_computation.21 | loop fusion | flops 2097152 | bytes 2097152 | tf_op jit(solution)/shard_map/concatenate | solution.py:122
  11.2 6.4 %copy.25 = bf16[8192,224]{1,0:T(8,128)(2,1)} copy(bf16[8192,224]{0,1:T(8,128)(2,1)} %param.17) | data formatting | bytes 7340032 | tf_op args[3]
  17.6 6.3 %copy.26 = bf16[8192,224]{1,0:T(8,128)(2,1)} copy(bf16[8192,224]{0,1:T(8,128)(2,1)} %param.18) | data formatting | bytes 7340032 | tf_op args[4]
  23.9 1.7 copy.27
  25.7 1.8 copy.28
  27.5 6.3 %copy.29 = bf16[224,8192]{0,1:T(8,128)(2,1)} copy(bf16[224,8192]{1,0:T(8,128)(2,1)} %param.19) | data formatting | bytes 7340032 | tf_op args[5]
  33.8 1.8 copy.30
  36.0 7.9 %fusion.8.wc_ref = bf16[8192,384]{1,0:T(8,128)(2,1)} fusion(bf16[8192,64]{1,0:T(8,128)(2,1)} %copy.30, bf16[8192,224]{1,0:T(8,128)(2,1)} %bitcast.27), kind=kLoop, calls=%fused_computation.13 | loop fusion | flops 25165824 | bytes 11010048 | tf_op jit(solution)/shard_map/concatenate | solution.py:58
  43.9 1.2 copy-done.4
  45.1 6.6 %fusion.7.wa_ref = bf16[8192,640]{1,0:T(8,128)(2,1)} fusion(bf16[8192,224]{1,0:T(8,128)(2,1)S(1)} %copy-done.2, bf16[8192,224]{1,0:T(8,128)(2,1)S(1)} %copy-done.1, bf16[8192,64]{1,0:T(8,128)(2,1)S(1)} %copy-done.4, bf16[8192,64]{1,0:T(8,128)(2,1)S(1)} %copy-done.3), kind=kLoop, calls=%fused_computation.12 | loop fusion | flops 73400320 | bytes 19922944 | tf_op jit(solution)/shard_map/concatenate | solution.py:57
  51.7 54.9 %all-gather.2.cloned.1.call-done.act_ref.cot_ref = bf16[512,16384]{1,0:T(8,128)(2,1)} async-done(((bf16[32,16384]{1,0:T(8,128)(2,1)}), bf16[512,16384]{1,0:T(8,128)(2,1)}) %all-gather.2.cloned.1.call-update) | async-done | bytes 16777232 | tf_op jit(solution)/shard_map/all_gather | solution.py:122
  106.6 16.3 %shard_map.149 = (f32[512,192]{1,0:T(8,128)S(1)}, f32[512,192]{1,0:T(8,128)S(1)}) custom-call(bf16[512,16384]{1,0:T(8,128)(2,1)} %all-gather.2.cloned.1.call-done.act_ref.cot_ref, bf16[512,16384]{1,0:T(8,128)(2,1)} %all-gather.2.cloned.1.call-done.act_ref.cot_ref, bf16[8192,640]{1,0:T(8,128)(2,1)} %fusion.7.wa_ref, bf16[8192,384]{1,0:T(8,128)(2,1)} %fusion.8.wc_ref, ...), custom_call_target="tpu_custom_call" | custom-call | flops 7291797504 | bytes 34426880 | tf_op jit(solution)/shard_map/pallas_call | solution.py:62
  123.0 22.7 %all_to_all.15 = f32[128,4,192]{2,1,0:T(4,128)S(1)} all-to-all(f32[128,4,192]{2,1,0:T(4,128)S(1)} %reshape.37), channel_id=1, replica_groups=mesh['dp'=16,'tensor'=8] {'dp','tensor'}, dimensions={0} | all-to-all | bytes 786432 | tf_op jit(solution)/shard_map/all_to_all | solution.py:93
  145.8 0.9 broadcast_in_dim.2
  146.7 3.9 %all-to-all-start.1 = ((f32[128,4,192]{2,1,0:T(4,128)}), f32[128,4,192]{2,1,0:T(4,128)S(1)}, u32[]{:S(2)}, u32[]{:S(2)}) async-start(f32[128,4,192]{2,1,0:T(4,128)} %broadcast_in_dim.2), calls=%async_computation.1 | async-start | bytes 1048576 | tf_op jit(solution)/shard_map/all_to_all | solution.py:98
  150.8 13.9 %all-to-all-done.1 = f32[128,4,192]{2,1,0:T(4,128)S(1)} async-done(((f32[128,4,192]{2,1,0:T(4,128)}), f32[128,4,192]{2,1,0:T(4,128)S(1)}, u32[]{:S(2)}, u32[]{:S(2)}) %all-to-all-start.1) | async-done | bytes 393248 | tf_op jit(solution)/shard_map/all_to_all | solution.py:98
  165.0 1.1 fusion.9
  166.1 1.1 fusion.10
  167.1 1.1 fusion.11
  170.0 0.9 reshape.45
  170.8 3.9 %all-to-all-start.2 = ((f32[128,1,128]{2,1,0:T(1,128)}), f32[128,1,128]{2,1,0:T(1,128)S(1)}, u32[]{:S(2)}, u32[]{:S(2)}) async-start(f32[128,1,128]{2,1,0:T(1,128)} %reshape.45), calls=%async_computation.2 | async-start | bytes 131072 | tf_op jit(solution)/shard_map/all_to_all | solution.py:93
  175.4 9.2 %all-to-all-done.2 = f32[128,1,128]{2,1,0:T(1,128)S(1)} async-done(((f32[128,1,128]{2,1,0:T(1,128)}), f32[128,1,128]{2,1,0:T(1,128)S(1)}, u32[]{:S(2)}, u32[]{:S(2)}) %all-to-all-start.2) | async-done | bytes 65568 | tf_op jit(solution)/shard_map/all_to_all | solution.py:93
  185.1 0.8 reduce
  (43 shorter events, 5.8 us)
Async XLA Ops:
  7.2 162.0 %copy-start = (bf16[32,12288]{1,0:T(8,128)(2,1)S(1)}, bf16[32,12288]{1,0:T(8,128)(2,1)}, u32[]{:S(2)}) copy-start(bf16[32,12288]{1,0:T(8,128)(2,1)} %param.26) | copy-start | bytes 2359300
  7.2 99.4 %all-gather.2.cloned.1.call-start = ((), (), s32[]{:S(2)}) async-start(), calls=%async_computation.3 | async-start | bytes 17825792 | tf_op jit(solution)/shard_map/all_gather | solution.py:122
  11.2 12.7 %copy-start.5 = (bf16[8192,64]{0,1:T(8,128)(2,1)S(1)}, bf16[8192,64]{0,1:T(8,128)(2,1)}, u32[]{:S(2)}) copy-start(bf16[8192,64]{0,1:T(8,128)(2,1)} %param.20) | copy-start | bytes 3145732
  17.6 8.1 %copy-start.6 = (bf16[8192,64]{0,1:T(8,128)(2,1)S(1)}, bf16[8192,64]{0,1:T(8,128)(2,1)}, u32[]{:S(2)}) copy-start(bf16[8192,64]{0,1:T(8,128)(2,1)} %param.21) | copy-start | bytes 3145732
  25.7 8.2 %copy-start.7 = (bf16[8192,64]{0,1:T(8,128)(2,1)S(1)}, bf16[8192,64]{0,1:T(8,128)(2,1)}, u32[]{:S(2)}) copy-start(bf16[8192,64]{0,1:T(8,128)(2,1)} %param.22) | copy-start | bytes 3145732
  25.7 10.0 %copy-start.8 = (bf16[224,64]{0,1:T(8,128)(2,1)S(1)}, bf16[224,64]{0,1:T(8,128)(2,1)}, u32[]{:S(2)}) copy-start(bf16[224,64]{0,1:T(8,128)(2,1)} %param.23) | copy-start | bytes 86020
  27.5 8.3 %copy-start.9 = (bf16[224,64]{0,1:T(8,128)(2,1)S(1)}, bf16[224,64]{0,1:T(8,128)(2,1)}, u32[]{:S(2)}) copy-start(bf16[224,64]{0,1:T(8,128)(2,1)} %param.24) | copy-start | bytes 86020
  27.5 8.4 %copy-start.10 = (bf16[224,64]{0,1:T(8,128)(2,1)S(1)}, bf16[224,64]{0,1:T(8,128)(2,1)}, u32[]{:S(2)}) copy-start(bf16[224,64]{0,1:T(8,128)(2,1)} %param.25) | copy-start | bytes 86020
  36.0 7.9 %copy-start.1 = (bf16[8192,224]{1,0:T(8,128)(2,1)S(1)}, bf16[8192,224]{1,0:T(8,128)(2,1)}, u32[]{:S(2)}) copy-start(bf16[8192,224]{1,0:T(8,128)(2,1)} %copy.25) | copy-start | bytes 11010052
  36.0 7.9 %copy-start.2 = (bf16[8192,224]{1,0:T(8,128)(2,1)S(1)}, bf16[8192,224]{1,0:T(8,128)(2,1)}, u32[]{:S(2)}) copy-start(bf16[8192,224]{1,0:T(8,128)(2,1)} %copy.26) | copy-start | bytes 11010052
  36.0 7.9 %copy-start.3 = (bf16[8192,64]{1,0:T(8,128)(2,1)S(1)}, bf16[8192,64]{1,0:T(8,128)(2,1)}, u32[]{:S(2)}) copy-start(bf16[8192,64]{1,0:T(8,128)(2,1)} %copy.27) | copy-start | bytes 3145732
  36.0 9.1 %copy-start.4 = (bf16[8192,64]{1,0:T(8,128)(2,1)S(1)}, bf16[8192,64]{1,0:T(8,128)(2,1)}, u32[]{:S(2)}) copy-start(bf16[8192,64]{1,0:T(8,128)(2,1)} %copy.28) | copy-start | bytes 3145732
  146.7 17.9 %all-to-all-start.1 = ((f32[128,4,192]{2,1,0:T(4,128)}), f32[128,4,192]{2,1,0:T(4,128)S(1)}, u32[]{:S(2)}, u32[]{:S(2)}) async-start(f32[128,4,192]{2,1,0:T(4,128)} %broadcast_in_dim.2), calls=%async_computation.1 | async-start | bytes 1048576 | tf_op jit(solution)/shard_map/all_to_all | solution.py:98
  150.6 18.8 %copy-start.11 = (s32[32]{0:T(128)S(1)}, s32[32]{0:T(128)}, u32[]{:S(2)}) copy-start(s32[32]{0:T(128)} %param.27) | copy-start | bytes 388
  170.8 13.8 %all-to-all-start.2 = ((f32[128,1,128]{2,1,0:T(1,128)}), f32[128,1,128]{2,1,0:T(1,128)S(1)}, u32[]{:S(2)}, u32[]{:S(2)}) async-start(f32[128,1,128]{2,1,0:T(1,128)} %reshape.45), calls=%async_computation.2 | async-start | bytes 131072 | tf_op jit(solution)/shard_map/all_to_all | solution.py:93
Sparse Core Ops, SparseCore 0:
  11.3 95.1 all-gather.1

commit v5 on v4

--- a/solution.py
+++ b/solution.py
@@ -18,7 +18,7 @@
     return jnp.pad(x, ((0, 0), (0, cols - x.shape[1])))
 
 
-def layer_kernel(act_ref, cot_ref, wa_ref, wc_ref, go_ref, uo_ref, di_ref, side_ref, inp_ref, a_acc, c_acc):
+def layer_kernel(act_ref, cot_ref, wa_ref, wc_ref, go_ref, uo_ref, di_ref, side_ref, a_acc, c_acc):
     k = pl.program_id(0)
 
     @pl.when(k == 0)
@@ -44,18 +44,16 @@
         side_ref[:, 0:r] = jnp.dot(grad_gate, go_ref[...], preferred_element_type=f32)
         side_ref[:, r : 2 * r] = jnp.dot(grad_up, uo_ref[...], preferred_element_type=f32)
         side_ref[:, 2 * r : 3 * r] = jnp.dot(hidden, di_ref[...], preferred_element_type=f32)
-        inp_ref[:, 0 : 2 * r] = a_acc[:, 2 * fp : 2 * fp + 2 * r]
-        inp_ref[:, 2 * r : 3 * r] = c_acc[:, fp : fp + r]
 
 
-def layer_call(both, gw, uw, dw, gi, ui, do, go, uo, di):
+def layer_call(both, gw, uw, dw, go, uo, di):
     rows, width = both.shape
     d = width // 2
     ff = gw.shape[1]
-    r = gi.shape[1]
+    r = go.shape[1]
     fp = -(-ff // LANE) * LANE
-    wa = jnp.concatenate([pad_to(gw, fp), pad_to(uw, fp), pad_to(jnp.concatenate([gi, ui], 1), LANE)], 1)
-    wc = jnp.concatenate([pad_to(dw.T, fp), pad_to(do, LANE)], 1)
+    wa = jnp.concatenate([pad_to(gw, fp), pad_to(uw, fp)], 1)
+    wc = pad_to(dw.T, fp)
     nk = d // KC
     f32 = jnp.float32
     full = lambda shape: pl.BlockSpec(shape, lambda k: (0, 0))
@@ -71,8 +69,8 @@
             full((ff, r)),
             full((ff, r)),
         ],
-        out_specs=[full((rows, 3 * r)), full((rows, 3 * r))],
-        out_shape=[jax.ShapeDtypeStruct((rows, 3 * r), f32), jax.ShapeDtypeStruct((rows, 3 * r), f32)],
+        out_specs=full((rows, 3 * r)),
+        out_shape=jax.ShapeDtypeStruct((rows, 3 * r), f32),
         scratch_shapes=[
             pltpu.VMEM((rows, wa.shape[1]), f32),
             pltpu.VMEM((rows, wc.shape[1]), f32),
@@ -81,9 +79,9 @@
             dimension_semantics=("arbitrary",), vmem_limit_bytes=48 * 1024 * 1024
         ),
         cost_estimate=pl.CostEstimate(
-            flops=2 * rows * d * (3 * ff + 3 * r) + 2 * rows * ff * 3 * r,
+            flops=2 * rows * d * 3 * ff + 2 * rows * ff * 3 * r,
             transcendentals=rows * ff,
-            bytes_accessed=2 * (rows * width + d * (wa.shape[1] + wc.shape[1]) + 3 * ff * r) + 8 * rows * 3 * r,
+            bytes_accessed=2 * (rows * width + d * (wa.shape[1] + wc.shape[1]) + 3 * ff * r) + 4 * rows * 3 * r,
         ),
     )(both, both, wa, wc, go, uo, di)
 
@@ -120,14 +118,25 @@
     pad_mask = (token_ids != 0).astype(jnp.bfloat16)[:, None]
     masked = cotangent * pad_mask
     both = lax.all_gather(jnp.concatenate([hidden_in, masked], axis=1), "dp", axis=0, tiled=True)
-    block, inputs = layer_call(
-        both, gate_weight, up_weight, down_weight, gate_in_proj, up_in_proj, down_out_proj,
-        gate_out_proj, up_out_proj, down_in_proj,
+    f32 = jnp.float32
+    own_inputs = jnp.concatenate(
+        [
+            jnp.dot(hidden_in, gate_in_proj, preferred_element_type=f32),
+            jnp.dot(hidden_in, up_in_proj, preferred_element_type=f32),
+            jnp.dot(masked, down_out_proj, preferred_element_type=f32),
+        ],
+        axis=1,
     )
-    summed = gather_rows(scatter_sum(block, n_all), n_all)
-    in_gate = inputs[:, :proj_rank]
-    in_up = inputs[:, proj_rank : 2 * proj_rank]
-    out_down = inputs[:, 2 * proj_rank :]
+    block = layer_call(both, gate_weight, up_weight, down_weight, gate_out_proj, up_out_proj, down_in_proj)
+    part_rows = block.shape[0] // n_all
+    my_inputs = lax.dynamic_slice_in_dim(own_inputs, lax.axis_index("tensor") * part_rows, part_rows, 0)
+    summed_part = scatter_sum(block, n_all)
+    gathered = gather_rows(jnp.concatenate([summed_part, my_inputs], axis=1), n_all)
+    width = 3 * proj_rank
+    summed = gathered[:, :width]
+    in_gate = gathered[:, width : width + proj_rank]
+    in_up = gathered[:, width + proj_rank : width + 2 * proj_rank]
+    out_down = gathered[:, width + 2 * proj_rank :]
     docs = both.shape[0] // LEN
 
     def doc_outer(left, right):

time: 194 us -> 196 us (1.010)
  waiting for transfers between devices: 78 us -> 103 us
  blocking collectives: 22.7 us -> 0 us
  other arithmetic: 20.3 us -> 10.1 us
  starting transfers between devices: 7.83 us -> 16.4 us
  Pallas kernels: 16.3 us -> 12.1 us
  matrix products: 4.04 us -> 6.51 us
  local copies, waits for them, and re-layouts: 30.4 us -> 32.8 us
    all_to_all x1 -> x0, blocking collectives: 22.7 us -> none  [scatter_sum(): return jnp.sum(lax.all_to_all(blocks, ALL, 0, 0, tiled=False), axis=0)]
    all_to_all x1 -> x2, waiting for transfers between devices: 9.23 us -> 21 us  [scatter_sum(): return jnp.sum(lax.all_to_all(blocks, ALL, 0, 0, tiled=False), axis=0)]
    all_gather x1, waiting for transfers between devices: 54.9 us -> 65.6 us  [body(): lax.all_gather(jnp.concatenate([hidden_in, masked], axis=1), 'dp', axis=0...]
    concatenate x2 -> x3, other arithmetic: 14.5 us -> 4.24 us  [the longest x1 4.07 us: layer_call(): wa = jnp.concatenate([pad_to(gw, fp), pad_to(uw, fp)], 1)]
    all_to_all x1 -> x2, starting transfers between devices: 3.89 us -> 12.5 us  [scatter_sum(): return jnp.sum(lax.all_to_all(blocks, ALL, 0, 0, tiled=False), axis=0)]
    pad x0 -> x1, local copies, waits for them, and re-layouts: none -> 5.29 us  [pad_to(): return jnp.pad(x, ((0, 0), (0, cols - x.shape[1])))]
    pallas_call x1, Pallas kernels: 16.3 us -> 12.1 us  [layer_call(): pl.pallas_call(layer_kernel, grid=(nk,), in_specs=[pl.BlockSpec((rows, KC...]
    unnamed x35 -> x32, local copies, waits for them, and re-layouts: 27 us -> 23.2 us
  transfers between devices with their start and end apart: 3 -> 4, of which waited for: 3 -> 4; matrix products, arithmetic and copies ran while one was open for 21% -> 16% of each run, Pallas kernels for 0% -> 0%
where the time goes in v5:
time: 196 us
  waiting for transfers between devices  103 us (53%)
  local copies, waits for them, and re-layouts  32.8 us (17%)
  starting transfers between devices  16.4 us (8%)
  between operations  14.3 us (7%)
  Pallas kernels  12.1 us (6%)
  other arithmetic  10.1 us (5%)
  matrix products  6.51 us (3%)
    all_gather x1, waiting for transfers between devices, body(): lax.all_gather(jnp.concatenate([hidden_in, masked], axis=1), 'dp', axis=0...  65.6 us
    unnamed x32, local copies, waits for them, and re-layouts  23.2 us
    all_to_all x2, waiting for transfers between devices, scatter_sum(): return jnp.sum(lax.all_to_all(blocks, ALL, 0, 0, tiled=False), axis=0)  21 us
    all_to_all x1, waiting for transfers between devices, gather_rows(): got = lax.all_to_all(copies, ALL, 0, 0, tiled=False)  16.8 us
    all_to_all x2, starting transfers between devices, scatter_sum(): return jnp.sum(lax.all_to_all(blocks, ALL, 0, 0, tiled=False), axis=0)  12.5 us
    pallas_call x1, Pallas kernels, layer_call(): pl.pallas_call(layer_kernel, grid=(nk,), in_specs=[pl.BlockSpec((rows, KC...  12.1 us
    pad x1, local copies, waits for them, and re-layouts, pad_to(): return jnp.pad(x, ((0, 0), (0, cols - x.shape[1])))  5.29 us
    concatenate x1, other arithmetic, layer_call(): wa = jnp.concatenate([pad_to(gw, fp), pad_to(uw, fp)], 1)  4.07 us
  transfers between devices with their start and end apart: 4, of which 4 were waited for; matrix products, arithmetic and copies ran while one was open for 16% of the time, Pallas kernels for 0%

profile of v5, /device:TPU:1, one launch (start us, length us, event | category | flops | bytes accessed | tf_op | source)
XLA Modules:
  0.0 195.7 jit_solution(18067694286213961282)
XLA Ops:
  8.0 1.1 broadcast_multiply_fusion
  9.1 2.1 %pad_maximum_fusion = bf16[32,16384]{1,0:T(8,128)(2,1)} fusion(bf16[32,8192]{1,0:T(8,128)(2,1)S(1)} %broadcast_multiply_fusion, bf16[32,8192]{1,0:T(8,128)(2,1)} %param.15), kind=kLoop, calls=%fused_computation.12 | loop fusion | flops 2097152 | bytes 2097152 | tf_op jit(solution)/shard_map/concatenate | solution.py:120
  11.3 6.3 %copy.22 = bf16[8192,224]{1,0:T(8,128)(2,1)} copy(bf16[8192,224]{0,1:T(8,128)(2,1)} %param.17) | data formatting | bytes 7340032 | tf_op args[3]
  17.5 6.3 %copy.23 = bf16[8192,224]{1,0:T(8,128)(2,1)} copy(bf16[8192,224]{0,1:T(8,128)(2,1)} %param.18) | data formatting | bytes 7340032 | tf_op args[4]
  23.8 6.3 %copy.24 = bf16[224,8192]{0,1:T(8,128)(2,1)} copy(bf16[224,8192]{1,0:T(8,128)(2,1)} %param.19) | data formatting | bytes 7340032 | tf_op args[5]
  30.5 5.3 %pad.12.wc_ref = bf16[8192,256]{1,0:T(8,128)(2,1)} pad(bf16[8192,224]{1,0:T(8,128)(2,1)} %bitcast.33, bf16[]{:T(256)} %constant.5.clone.1), padding=0_0x0_32 | pad | bytes 7864322 | tf_op jit(solution)/shard_map/jit(_pad)/pad | solution.py:18
  36.9 4.1 %fusion.2.wa_ref = bf16[8192,512]{1,0:T(8,128)(2,1)} fusion(bf16[8192,224]{1,0:T(8,128)(2,1)S(1)} %copy-done.4, bf16[8192,224]{1,0:T(8,128)(2,1)S(1)} %copy-done.3), kind=kLoop, calls=%fused_computation.4 | loop fusion | flops 33554432 | bytes 15728640 | tf_op jit(solution)/shard_map/concatenate | solution.py:55
  41.0 65.6 %all-gather.2.cloned.1.call-done.act_ref.cot_ref = bf16[512,16384]{1,0:T(8,128)(2,1)} async-done(((bf16[32,16384]{1,0:T(8,128)(2,1)}), bf16[512,16384]{1,0:T(8,128)(2,1)}) %all-gather.2.cloned.1.call-update) | async-done | bytes 16777232 | tf_op jit(solution)/shard_map/all_gather | solution.py:120
  106.6 2.2 %copy-done.2 = bf16[8192,256]{1,0:T(8,128)(2,1)S(1)} copy-done((bf16[8192,256]{1,0:T(8,128)(2,1)S(1)}, bf16[8192,256]{1,0:T(8,128)(2,1)}, u32[]{:S(2)}) %copy-start.2) | copy-done | bytes 4194328
  108.8 12.1 %shard_map.149 = f32[512,192]{1,0:T(8,128)S(1)} custom-call(bf16[512,16384]{1,0:T(8,128)(2,1)} %all-gather.2.cloned.1.call-done.act_ref.cot_ref, bf16[512,16384]{1,0:T(8,128)(2,1)} %all-gather.2.cloned.1.call-done.act_ref.cot_ref, bf16[8192,512]{1,0:T(8,128)(2,1)} %fusion.2.wa_ref, bf16[8192,256]{1,0:T(8,128)(2,1)S(1)} %copy-done.2, ...), custom_call_target="tpu_custom_call" | custom-call | flops 5681184768 | bytes 29839360 | tf_op jit(solution)/shard_map/pallas_call | solution.py:60
  120.9 0.9 reshape.36
  121.8 8.8 %all-to-all-start = ((f32[128,4,192]{2,1,0:T(4,128)}), f32[128,4,192]{2,1,0:T(4,128)S(1)}, u32[]{:S(2)}, u32[]{:S(2)}) async-start(f32[128,4,192]{2,1,0:T(4,128)} %reshape.36), calls=%async_computation | async-start | bytes 1048576 | tf_op jit(solution)/shard_map/all_to_all | solution.py:91
  131.1 1.7 fusion.13
  132.9 11.8 %all-to-all-done = f32[128,4,192]{2,1,0:T(4,128)S(1)} async-done(((f32[128,4,192]{2,1,0:T(4,128)}), f32[128,4,192]{2,1,0:T(4,128)S(1)}, u32[]{:S(2)}, u32[]{:S(2)}) %all-to-all-start) | async-done | bytes 393248 | tf_op jit(solution)/shard_map/all_to_all | solution.py:91
  145.0 1.0 broadcast_in_dim.2
  146.0 3.9 %all-to-all-start.1 = ((f32[128,4,384]{2,1,0:T(4,128)}), f32[128,4,384]{2,1,0:T(4,128)S(1)}, u32[]{:S(2)}, u32[]{:S(2)}) async-start(f32[128,4,384]{2,1,0:T(4,128)} %broadcast_in_dim.2), calls=%async_computation.1 | async-start | bytes 1572864 | tf_op jit(solution)/shard_map/all_to_all | solution.py:96
  149.9 16.8 %all-to-all-done.1 = f32[128,4,384]{2,1,0:T(4,128)S(1)} async-done(((f32[128,4,384]{2,1,0:T(4,128)}), f32[128,4,384]{2,1,0:T(4,128)S(1)}, u32[]{:S(2)}, u32[]{:S(2)}) %all-to-all-start.1) | async-done | bytes 786464 | tf_op jit(solution)/shard_map/all_to_all | solution.py:96
  167.2 1.1 fusion.3
  168.3 1.1 fusion.4
  169.4 1.1 fusion.5
  172.2 0.9 reshape.45
  173.1 3.6 %all-to-all-start.2 = ((f32[128,1,128]{2,1,0:T(1,128)}), f32[128,1,128]{2,1,0:T(1,128)S(1)}, u32[]{:S(2)}, u32[]{:S(2)}) async-start(f32[128,1,128]{2,1,0:T(1,128)} %reshape.45), calls=%async_computation.2 | async-start | bytes 131072 | tf_op jit(solution)/shard_map/all_to_all | solution.py:91
  177.4 9.2 %all-to-all-done.2 = f32[128,1,128]{2,1,0:T(1,128)S(1)} async-done(((f32[128,1,128]{2,1,0:T(1,128)}), f32[128,1,128]{2,1,0:T(1,128)S(1)}, u32[]{:S(2)}, u32[]{:S(2)}) %all-to-all-start.2) | async-done | bytes 65568 | tf_op jit(solution)/shard_map/all_to_all | solution.py:91
  187.1 0.8 reduce
  (45 shorter events, 7.4 us)
Async XLA Ops:
  7.2 28.6 %copy-start = (bf16[8192,64]{0,1:T(8,128)(2,1)S(1)}, bf16[8192,64]{0,1:T(8,128)(2,1)}, u32[]{:S(2)}) copy-start(bf16[8192,64]{0,1:T(8,128)(2,1)} %param.22) | copy-start | bytes 3145732
  7.2 99.4 %all-gather.2.cloned.1.call-start = ((), (), s32[]{:S(2)}) async-start(), calls=%async_computation.3 | async-start | bytes 17825792 | tf_op jit(solution)/shard_map/all_gather | solution.py:120
  17.5 12.6 %copy-start.8 = (bf16[224,64]{0,1:T(8,128)(2,1)S(1)}, bf16[224,64]{0,1:T(8,128)(2,1)}, u32[]{:S(2)}) copy-start(bf16[224,64]{0,1:T(8,128)(2,1)} %param.23) | copy-start | bytes 86020
  17.5 12.7 %copy-start.9 = (bf16[224,64]{0,1:T(8,128)(2,1)S(1)}, bf16[224,64]{0,1:T(8,128)(2,1)}, u32[]{:S(2)}) copy-start(bf16[224,64]{0,1:T(8,128)(2,1)} %param.24) | copy-start | bytes 86020
  17.5 12.8 %copy-start.10 = (bf16[224,64]{0,1:T(8,128)(2,1)S(1)}, bf16[224,64]{0,1:T(8,128)(2,1)}, u32[]{:S(2)}) copy-start(bf16[224,64]{0,1:T(8,128)(2,1)} %param.25) | copy-start | bytes 86020
  30.5 5.7 %copy-start.3 = (bf16[8192,224]{1,0:T(8,128)(2,1)S(1)}, bf16[8192,224]{1,0:T(8,128)(2,1)}, u32[]{:S(2)}) copy-start(bf16[8192,224]{1,0:T(8,128)(2,1)} %copy.22) | copy-start | bytes 11010052
  30.5 6.4 %copy-start.4 = (bf16[8192,224]{1,0:T(8,128)(2,1)S(1)}, bf16[8192,224]{1,0:T(8,128)(2,1)}, u32[]{:S(2)}) copy-start(bf16[8192,224]{1,0:T(8,128)(2,1)} %copy.23) | copy-start | bytes 11010052
  106.6 2.2 %copy-start.2 = (bf16[8192,256]{1,0:T(8,128)(2,1)S(1)}, bf16[8192,256]{1,0:T(8,128)(2,1)}, u32[]{:S(2)}) copy-start(bf16[8192,256]{1,0:T(8,128)(2,1)} %pad.12.wc_ref) | copy-start | bytes 12582916
  108.8 21.9 %copy-start.5 = (bf16[32,8192]{1,0:T(8,128)(2,1)S(1)}, bf16[32,8192]{1,0:T(8,128)(2,1)}, u32[]{:S(2)}) copy-start(bf16[32,8192]{1,0:T(8,128)(2,1)} %param.15) | copy-start | bytes 1572868
  108.8 21.9 %copy-start.6 = (bf16[8192,64]{0,1:T(8,128)(2,1)S(1)}, bf16[8192,64]{0,1:T(8,128)(2,1)}, u32[]{:S(2)}) copy-start(bf16[8192,64]{0,1:T(8,128)(2,1)} %param.20) | copy-start | bytes 3145732
  121.8 22.9 %all-to-all-start = ((f32[128,4,192]{2,1,0:T(4,128)}), f32[128,4,192]{2,1,0:T(4,128)S(1)}, u32[]{:S(2)}, u32[]{:S(2)}) async-start(f32[128,4,192]{2,1,0:T(4,128)} %reshape.36), calls=%async_computation | async-start | bytes 1048576 | tf_op jit(solution)/shard_map/all_to_all | solution.py:91
  131.1 40.2 %copy-start.7 = (bf16[32,12288]{1,0:T(8,128)(2,1)S(1)}, bf16[32,12288]{1,0:T(8,128)(2,1)}, u32[]{:S(2)}) copy-start(bf16[32,12288]{1,0:T(8,128)(2,1)} %param.26) | copy-start | bytes 2359300
  131.1 40.6 %copy-start.11 = (s32[32]{0:T(128)S(1)}, s32[32]{0:T(128)}, u32[]{:S(2)}) copy-start(s32[32]{0:T(128)} %param.27) | copy-start | bytes 388
  145.0 43.9 %copy-start.1 = (bf16[8192,64]{0,1:T(8,128)(2,1)S(1)}, bf16[8192,64]{0,1:T(8,128)(2,1)}, u32[]{:S(2)}) copy-start(bf16[8192,64]{0,1:T(8,128)(2,1)} %param.22) | copy-start | bytes 3145732
  146.0 20.7 %all-to-all-start.1 = ((f32[128,4,384]{2,1,0:T(4,128)}), f32[128,4,384]{2,1,0:T(4,128)S(1)}, u32[]{:S(2)}, u32[]{:S(2)}) async-start(f32[128,4,384]{2,1,0:T(4,128)} %broadcast_in_dim.2), calls=%async_computation.1 | async-start | bytes 1572864 | tf_op jit(solution)/shard_map/all_to_all | solution.py:96
  173.1 13.6 %all-to-all-start.2 = ((f32[128,1,128]{2,1,0:T(1,128)}), f32[128,1,128]{2,1,0:T(1,128)S(1)}, u32[]{:S(2)}, u32[]{:S(2)}) async-start(f32[128,1,128]{2,1,0:T(1,128)} %reshape.45), calls=%async_computation.2 | async-start | bytes 131072 | tf_op jit(solution)/shard_map/all_to_all | solution.py:91
Sparse Core Ops, SparseCore 0:
  11.4 95.1 all-gather.1

commit v6 on v5

--- a/solution.py
+++ b/solution.py
@@ -76,7 +76,7 @@
             pltpu.VMEM((rows, wc.shape[1]), f32),
         ],
         compiler_params=pltpu.CompilerParams(
-            dimension_semantics=("arbitrary",), vmem_limit_bytes=48 * 1024 * 1024
+            dimension_semantics=("arbitrary",), vmem_limit_bytes=62 * 1024 * 1024
         ),
         cost_estimate=pl.CostEstimate(
             flops=2 * rows * d * 3 * ff + 2 * rows * ff * 3 * r,
@@ -119,24 +119,15 @@
     masked = cotangent * pad_mask
     both = lax.all_gather(jnp.concatenate([hidden_in, masked], axis=1), "dp", axis=0, tiled=True)
     f32 = jnp.float32
-    own_inputs = jnp.concatenate(
-        [
-            jnp.dot(hidden_in, gate_in_proj, preferred_element_type=f32),
-            jnp.dot(hidden_in, up_in_proj, preferred_element_type=f32),
-            jnp.dot(masked, down_out_proj, preferred_element_type=f32),
-        ],
-        axis=1,
+    block = layer_call(both, gate_weight, up_weight, down_weight, gate_out_proj, up_out_proj, down_in_proj)
+    summed = gather_rows(scatter_sum(block, n_all), n_all)
+    d_model = hidden_in.shape[1]
+    in_both = jnp.dot(
+        both[:, :d_model], jnp.concatenate([gate_in_proj, up_in_proj], axis=1), preferred_element_type=f32
     )
-    block = layer_call(both, gate_weight, up_weight, down_weight, gate_out_proj, up_out_proj, down_in_proj)
-    part_rows = block.shape[0] // n_all
-    my_inputs = lax.dynamic_slice_in_dim(own_inputs, lax.axis_index("tensor") * part_rows, part_rows, 0)
-    summed_part = scatter_sum(block, n_all)
-    gathered = gather_rows(jnp.concatenate([summed_part, my_inputs], axis=1), n_all)
-    width = 3 * proj_rank
-    summed = gathered[:, :width]
-    in_gate = gathered[:, width : width + proj_rank]
-    in_up = gathered[:, width + proj_rank : width + 2 * proj_rank]
-    out_down = gathered[:, width + 2 * proj_rank :]
+    in_gate = in_both[:, :proj_rank]
+    in_up = in_both[:, proj_rank:]
+    out_down = jnp.dot(both[:, d_model:], down_out_proj, preferred_element_type=f32)
     docs = both.shape[0] // LEN
 
     def doc_outer(left, right):

time: 196 us -> 195 us (level)
  waiting for transfers between devices: 103 us -> 85.6 us
  matrix products: 6.51 us -> 18.3 us
  other arithmetic: 10.1 us -> 13.5 us
    dot_general x3 -> x2, matrix products: 2.49 us -> 13.3 us  [the longest x1 6.83 us: body(): jnp.dot(both[:, :d_model], jnp.concatenate([gate_in_proj, up_in_proj], ax...]
    all_to_all x1, waiting for transfers between devices: 16.8 us -> 7.54 us  [gather_rows(): got = lax.all_to_all(copies, ALL, 0, 0, tiled=False)]
    all_to_all x2, waiting for transfers between devices: 21 us -> 16.1 us  [scatter_sum(): return jnp.sum(lax.all_to_all(blocks, ALL, 0, 0, tiled=False), axis=0)]
    all_gather x1, waiting for transfers between devices: 65.6 us -> 61.9 us  [body(): lax.all_gather(jnp.concatenate([hidden_in, masked], axis=1), 'dp', axis=0...]
    concatenate x1, other arithmetic: 4.07 us -> 7.61 us  [layer_call(): wa = jnp.concatenate([pad_to(gw, fp), pad_to(uw, fp)], 1)]
    unnamed x32 -> x20, local copies, waits for them, and re-layouts: 23.2 us -> 22.1 us
  transfers between devices with their start and end apart: 4 -> 4, of which waited for: 4 -> 4; matrix products, arithmetic and copies ran while one was open for 16% -> 25% of each run, Pallas kernels for 0% -> 0%
where the time goes in v6:
time: 195 us
  waiting for transfers between devices  85.6 us (44%)
  local copies, waits for them, and re-layouts  32.3 us (17%)
  matrix products  18.3 us (9%)
  starting transfers between devices  16.7 us (9%)
  between operations  14.2 us (7%)
  Pallas kernels  14 us (7%)
  other arithmetic  13.5 us (7%)
    all_gather x1, waiting for transfers between devices, body(): lax.all_gather(jnp.concatenate([hidden_in, masked], axis=1), 'dp', axis=0...  61.9 us
    unnamed x20, local copies, waits for them, and re-layouts  22.1 us
    all_to_all x2, waiting for transfers between devices, scatter_sum(): return jnp.sum(lax.all_to_all(blocks, ALL, 0, 0, tiled=False), axis=0)  16.1 us
    pallas_call x1, Pallas kernels, layer_call(): pl.pallas_call(layer_kernel, grid=(nk,), in_specs=[pl.BlockSpec((rows, KC...  14 us
    all_to_all x2, starting transfers between devices, scatter_sum(): return jnp.sum(lax.all_to_all(blocks, ALL, 0, 0, tiled=False), axis=0)  12.7 us
    concatenate x1, other arithmetic, layer_call(): wa = jnp.concatenate([pad_to(gw, fp), pad_to(uw, fp)], 1)  7.61 us
    all_to_all x1, waiting for transfers between devices, gather_rows(): got = lax.all_to_all(copies, ALL, 0, 0, tiled=False)  7.54 us
    dot_general x1, matrix products, body(): jnp.dot(both[:, :d_model], jnp.concatenate([gate_in_proj, up_in_proj], ax...  6.83 us
  transfers between devices with their start and end apart: 4, of which 4 were waited for; matrix products, arithmetic and copies ran while one was open for 25% of the time, Pallas kernels for 0%

profile of v6, /device:TPU:1, one launch (start us, length us, event | category | flops | bytes accessed | tf_op | source)
XLA Modules:
  0.0 194.5 jit_solution(11785306960912526227)
XLA Ops:
  8.0 1.1 broadcast_multiply_fusion
  9.1 2.1 %pad_maximum_fusion = bf16[32,16384]{1,0:T(8,128)(2,1)} fusion(bf16[32,8192]{1,0:T(8,128)(2,1)S(1)} %broadcast_multiply_fusion, bf16[32,8192]{1,0:T(8,128)(2,1)} %param.15), kind=kLoop, calls=%fused_computation.19 | loop fusion | flops 2097152 | bytes 2097152 | tf_op jit(solution)/shard_map/concatenate | solution.py:120
  11.2 6.3 %copy.26 = bf16[8192,224]{1,0:T(8,128)(2,1)} copy(bf16[8192,224]{0,1:T(8,128)(2,1)} %param.17) | data formatting | bytes 7340032 | tf_op args[3]
  17.5 6.3 %copy.27 = bf16[8192,224]{1,0:T(8,128)(2,1)} copy(bf16[8192,224]{0,1:T(8,128)(2,1)} %param.18) | data formatting | bytes 7340032 | tf_op args[4]
  23.8 6.3 %copy.28 = bf16[224,8192]{0,1:T(8,128)(2,1)} copy(bf16[224,8192]{1,0:T(8,128)(2,1)} %param.19) | data formatting | bytes 7340032 | tf_op args[5]
  32.2 4.9 %pad.12.wc_ref = bf16[8192,256]{1,0:T(8,128)(2,1)} pad(bf16[8192,224]{1,0:T(8,128)(2,1)} %bitcast.28, bf16[]{:T(256)} %constant.4.clone.1), padding=0_0x0_32 | pad | bytes 7864322 | tf_op jit(solution)/shard_map/jit(_pad)/pad | solution.py:18
  37.1 7.6 %fusion.2.wa_ref = bf16[8192,512]{1,0:T(8,128)(2,1)} fusion(bf16[8192,224]{1,0:T(8,128)(2,1)} %copy.27, bf16[8192,224]{1,0:T(8,128)(2,1)} %copy.26), kind=kLoop, calls=%fused_computation.4 | loop fusion | flops 33554432 | bytes 15728640 | tf_op jit(solution)/shard_map/concatenate | solution.py:55
  44.7 61.9 %all-gather.2.cloned.1.call-done.act_ref.cot_ref = bf16[512,16384]{1,0:T(8,128)(2,1)} async-done(((bf16[32,16384]{1,0:T(8,128)(2,1)}), bf16[512,16384]{1,0:T(8,128)(2,1)}) %all-gather.2.cloned.1.call-update) | async-done | bytes 16777232 | tf_op jit(solution)/shard_map/all_gather | solution.py:120
  106.6 14.0 %shard_map.149 = f32[512,192]{1,0:T(8,128)} custom-call(bf16[512,16384]{1,0:T(8,128)(2,1)} %all-gather.2.cloned.1.call-done.act_ref.cot_ref, bf16[512,16384]{1,0:T(8,128)(2,1)} %all-gather.2.cloned.1.call-done.act_ref.cot_ref, bf16[8192,512]{1,0:T(8,128)(2,1)} %fusion.2.wa_ref, bf16[8192,256]{1,0:T(8,128)(2,1)} %pad.12.wc_ref, bf16[224,64]{1,0:T(8,128)(2,1)} %copy.29.go_ref, ...), custom_call_target="tpu_custom_call" | custom-call | flops 5681184768 | bytes 29839360 | tf_op jit(solution)/shard_map/pallas_call | solution.py:60
  120.6 2.0 %reshape.37 = f32[128,4,192]{2,1,0:T(4,128)} reshape(f32[512,192]{1,0:T(8,128)} %shard_map.149) | data formatting | bytes 786432 | tf_op jit(solution)/shard_map/reshape | solution.py:90
  122.6 8.8 %all-to-all-start = ((f32[128,4,192]{2,1,0:T(4,128)}), f32[128,4,192]{2,1,0:T(4,128)S(1)}, u32[]{:S(2)}, u32[]{:S(2)}) async-start(f32[128,4,192]{2,1,0:T(4,128)} %reshape.37), calls=%async_computation | async-start | bytes 1048576 | tf_op jit(solution)/shard_map/all_to_all | solution.py:91
  131.5 6.8 %fusion.5 = f32[512,128]{0,1:T(8,128)S(1)} fusion(bf16[512,16384]{1,0:T(8,128)(2,1)} %all-gather.2.cloned.1.call-done.act_ref.cot_ref, bf16[8192,64]{0,1:T(8,128)(2,1)} %param.21, bf16[8192,64]{0,1:T(8,128)(2,1)} %param.20), kind=kOutput, calls=%fused_computation.7 | convolution fusion | flops 1077936128 | bytes 10747904 | tf_op jit(solution)/shard_map/dot_general | solution.py:125
  138.6 6.9 %all-to-all-done = f32[128,4,192]{2,1,0:T(4,128)S(1)} async-done(((f32[128,4,192]{2,1,0:T(4,128)}), f32[128,4,192]{2,1,0:T(4,128)S(1)}, u32[]{:S(2)}, u32[]{:S(2)}) %all-to-all-start) | async-done | bytes 393248 | tf_op jit(solution)/shard_map/all_to_all | solution.py:91
  145.7 0.9 broadcast_in_dim.2
  146.5 3.9 %all-to-all-start.1 = ((f32[128,4,192]{2,1,0:T(4,128)}), f32[128,4,192]{2,1,0:T(4,128)S(1)}, u32[]{:S(2)}, u32[]{:S(2)}) async-start(f32[128,4,192]{2,1,0:T(4,128)} %broadcast_in_dim.2), calls=%async_computation.1 | async-start | bytes 1048576 | tf_op jit(solution)/shard_map/all_to_all | solution.py:96
  150.5 6.5 %fusion.3 = f32[512,64]{1,0:T(8,128)} fusion(bf16[8192,64]{0,1:T(8,128)(2,1)S(1)} %copy-done, bf16[512,16384]{1,0:T(8,128)(2,1)} %all-gather.2.cloned.1.call-done.act_ref.cot_ref), kind=kOutput, calls=%fused_computation.5 | convolution fusion | flops 536870912 | bytes 9568256 | tf_op jit(solution)/shard_map/dot_general | solution.py:130
  156.9 7.5 %all-to-all-done.1 = f32[128,4,192]{2,1,0:T(4,128)S(1)} async-done(((f32[128,4,192]{2,1,0:T(4,128)}), f32[128,4,192]{2,1,0:T(4,128)S(1)}, u32[]{:S(2)}, u32[]{:S(2)}) %all-to-all-start.1) | async-done | bytes 393248 | tf_op jit(solution)/shard_map/all_to_all | solution.py:96
  164.8 1.1 fusion.10
  165.9 1.1 fusion.11
  167.0 2.0 %fusion.12 = bf16[16,1,64,64]{3,2,0,1:T(8,128)(2,1)S(1)} fusion(f32[16,32,64]{2,1,0:T(8,128)S(1)} %bitcast.31, f32[16,32,64]{2,1,0:T(8,128)} %bitcast.34), kind=kOutput, calls=%fused_computation.18 | convolution fusion | flops 25231360 | bytes 393216 | tf_op jit(solution)/shard_map/dlr,dls->drs/dot_general | solution.py:136
  170.8 0.9 reshape.45
  171.6 3.9 %all-to-all-start.2 = ((f32[128,1,128]{2,1,0:T(1,128)}), f32[128,1,128]{2,1,0:T(1,128)S(1)}, u32[]{:S(2)}, u32[]{:S(2)}) async-start(f32[128,1,128]{2,1,0:T(1,128)} %reshape.45), calls=%async_computation.2 | async-start | bytes 131072 | tf_op jit(solution)/shard_map/all_to_all | solution.py:91
  176.2 9.2 %all-to-all-done.2 = f32[128,1,128]{2,1,0:T(1,128)S(1)} async-done(((f32[128,1,128]{2,1,0:T(1,128)}), f32[128,1,128]{2,1,0:T(1,128)S(1)}, u32[]{:S(2)}, u32[]{:S(2)}) %all-to-all-start.2) | async-done | bytes 65568 | tf_op jit(solution)/shard_map/all_to_all | solution.py:91
  185.9 0.8 reduce
  (33 shorter events, 7.5 us)
Async XLA Ops:
  7.2 143.3 %copy-start = (bf16[8192,64]{0,1:T(8,128)(2,1)S(1)}, bf16[8192,64]{0,1:T(8,128)(2,1)}, u32[]{:S(2)}) copy-start(bf16[8192,64]{0,1:T(8,128)(2,1)} %param.22) | copy-start | bytes 3145732
  7.2 99.4 %all-gather.2.cloned.1.call-start = ((), (), s32[]{:S(2)}) async-start(), calls=%async_computation.3 | async-start | bytes 17825792 | tf_op jit(solution)/shard_map/all_gather | solution.py:120
  17.5 12.6 %copy-start.2 = (bf16[224,64]{0,1:T(8,128)(2,1)S(1)}, bf16[224,64]{0,1:T(8,128)(2,1)}, u32[]{:S(2)}) copy-start(bf16[224,64]{0,1:T(8,128)(2,1)} %param.23) | copy-start | bytes 86020
  17.5 13.3 %copy-start.3 = (bf16[224,64]{0,1:T(8,128)(2,1)S(1)}, bf16[224,64]{0,1:T(8,128)(2,1)}, u32[]{:S(2)}) copy-start(bf16[224,64]{0,1:T(8,128)(2,1)} %param.24) | copy-start | bytes 86020
  17.5 14.0 %copy-start.4 = (bf16[224,64]{0,1:T(8,128)(2,1)S(1)}, bf16[224,64]{0,1:T(8,128)(2,1)}, u32[]{:S(2)}) copy-start(bf16[224,64]{0,1:T(8,128)(2,1)} %param.25) | copy-start | bytes 86020
  122.6 22.9 %all-to-all-start = ((f32[128,4,192]{2,1,0:T(4,128)}), f32[128,4,192]{2,1,0:T(4,128)S(1)}, u32[]{:S(2)}, u32[]{:S(2)}) async-start(f32[128,4,192]{2,1,0:T(4,128)} %reshape.37), calls=%async_computation | async-start | bytes 1048576 | tf_op jit(solution)/shard_map/all_to_all | solution.py:91
  146.5 17.9 %all-to-all-start.1 = ((f32[128,4,192]{2,1,0:T(4,128)}), f32[128,4,192]{2,1,0:T(4,128)S(1)}, u32[]{:S(2)}, u32[]{:S(2)}) async-start(f32[128,4,192]{2,1,0:T(4,128)} %broadcast_in_dim.2), calls=%async_computation.1 | async-start | bytes 1048576 | tf_op jit(solution)/shard_map/all_to_all | solution.py:96
  150.5 19.4 %copy-start.1 = (bf16[32,12288]{1,0:T(8,128)(2,1)S(1)}, bf16[32,12288]{1,0:T(8,128)(2,1)}, u32[]{:S(2)}) copy-start(bf16[32,12288]{1,0:T(8,128)(2,1)} %param.26) | copy-start | bytes 2359300
  156.9 13.3 %copy-start.5 = (s32[32]{0:T(128)S(1)}, s32[32]{0:T(128)}, u32[]{:S(2)}) copy-start(s32[32]{0:T(128)} %param.27) | copy-start | bytes 388
  171.6 13.8 %all-to-all-start.2 = ((f32[128,1,128]{2,1,0:T(1,128)}), f32[128,1,128]{2,1,0:T(1,128)S(1)}, u32[]{:S(2)}, u32[]{:S(2)}) async-start(f32[128,1,128]{2,1,0:T(1,128)} %reshape.45), calls=%async_computation.2 | async-start | bytes 131072 | tf_op jit(solution)/shard_map/all_to_all | solution.py:91
Sparse Core Ops, SparseCore 0:
  11.3 95.1 all-gather.1

commit v7 on v6

--- a/solution.py
+++ b/solution.py
@@ -130,18 +130,13 @@
     out_down = jnp.dot(both[:, d_model:], down_out_proj, preferred_element_type=f32)
     docs = both.shape[0] // LEN
 
-    def doc_outer(left, right):
-        left_docs = left.reshape(docs, LEN, proj_rank)
-        right_docs = right.reshape(docs, LEN, proj_rank)
-        return jnp.einsum("dlr,dls->drs", left_docs, right_docs, precision=lax.Precision.HIGHEST)
-
     side_gate = summed[:, :proj_rank]
     side_up = summed[:, proj_rank : 2 * proj_rank]
     side_down = summed[:, 2 * proj_rank :]
-    blocks = jnp.stack(
-        [doc_outer(in_gate, side_gate), doc_outer(in_up, side_up), doc_outer(side_down, out_down)],
-        axis=1,
-    )
+    shape = (3, docs, LEN, proj_rank)
+    lefts = jnp.stack([in_gate, in_up, side_down]).reshape(shape)
+    rights = jnp.stack([side_gate, side_up, out_down]).reshape(shape)
+    blocks = jnp.einsum("bdlr,bdls->dbrs", lefts, rights, precision=lax.Precision.HIGHEST)
     all_docs = blocks.reshape(docs, 3 * proj_rank * proj_rank).astype(jnp.bfloat16)
     docs_here = hidden_in.shape[0] // LEN
     doc_grads = lax.dynamic_slice_in_dim(all_docs, lax.axis_index("dp") * docs_here, docs_here, 0)

time: 195 us -> 195 us (level)
    dot_general x3 -> x1, matrix products: 4.16 us -> 3.73 us  [body(): jnp.einsum('bdlr,bdls->dbrs', lefts, rights, precision=lax.Precision.HIGH...]
where the time goes in v7:
time: 195 us; the launch traced here: 194 us
  waiting for transfers between devices  85.6 us (44%)
  local copies, waits for them, and re-layouts  32.2 us (17%)
  matrix products  17.9 us (9%)
  starting transfers between devices  16.7 us (9%)
  between operations  14.2 us (7%)
  Pallas kernels  14 us (7%)
  other arithmetic  13.3 us (7%)
    all_gather x1, waiting for transfers between devices, body(): lax.all_gather(jnp.concatenate([hidden_in, masked], axis=1), 'dp', axis=0...  61.9 us
    unnamed x20, local copies, waits for them, and re-layouts  22.1 us
    all_to_all x2, waiting for transfers between devices, scatter_sum(): return jnp.sum(lax.all_to_all(blocks, ALL, 0, 0, tiled=False), axis=0)  16.1 us
    pallas_call x1, Pallas kernels, layer_call(): pl.pallas_call(layer_kernel, grid=(nk,), in_specs=[pl.BlockSpec((rows, KC...  14 us
    all_to_all x2, starting transfers between devices, scatter_sum(): return jnp.sum(lax.all_to_all(blocks, ALL, 0, 0, tiled=False), axis=0)  12.7 us
    concatenate x1, other arithmetic, layer_call(): wa = jnp.concatenate([pad_to(gw, fp), pad_to(uw, fp)], 1)  7.61 us
    all_to_all x1, waiting for transfers between devices, gather_rows(): got = lax.all_to_all(copies, ALL, 0, 0, tiled=False)  7.54 us
    dot_general x1, matrix products, body(): jnp.dot(both[:, :d_model], jnp.concatenate([gate_in_proj, up_in_proj], ax...  6.83 us
  transfers between devices with their start and end apart: 4, of which 4 were waited for; matrix products, arithmetic and copies ran while one was open for 25% of the time, Pallas kernels for 0%

profile of v7, /device:TPU:1, one launch (start us, length us, event | category | flops | bytes accessed | tf_op | source)
XLA Modules:
  0.0 193.8 jit_solution(14208596549013964893)
XLA Ops:
  7.2 0.7 compare_convert_fusion
  8.0 1.1 broadcast_multiply_fusion
  9.1 2.1 %pad_maximum_fusion = bf16[32,16384]{1,0:T(8,128)(2,1)} fusion(bf16[32,8192]{1,0:T(8,128)(2,1)S(1)} %broadcast_multiply_fusion, bf16[32,8192]{1,0:T(8,128)(2,1)} %param.15), kind=kLoop, calls=%fused_computation.14 | loop fusion | flops 2097152 | bytes 2097152 | tf_op jit(solution)/shard_map/concatenate | solution.py:120
  11.2 6.3 %copy.27 = bf16[8192,224]{1,0:T(8,128)(2,1)} copy(bf16[8192,224]{0,1:T(8,128)(2,1)} %param.17) | data formatting | bytes 7340032 | tf_op args[3]
  17.5 6.3 %copy.28 = bf16[8192,224]{1,0:T(8,128)(2,1)} copy(bf16[8192,224]{0,1:T(8,128)(2,1)} %param.18) | data formatting | bytes 7340032 | tf_op args[4]
  23.8 6.3 %copy.29 = bf16[224,8192]{0,1:T(8,128)(2,1)} copy(bf16[224,8192]{1,0:T(8,128)(2,1)} %param.19) | data formatting | bytes 7340032 | tf_op args[5]
  32.2 4.9 %pad.12.wc_ref = bf16[8192,256]{1,0:T(8,128)(2,1)} pad(bf16[8192,224]{1,0:T(8,128)(2,1)} %bitcast.22, bf16[]{:T(256)} %constant.4.clone.1), padding=0_0x0_32 | pad | bytes 7864322 | tf_op jit(solution)/shard_map/jit(_pad)/pad | solution.py:18
  37.1 7.6 %fusion.2.wa_ref = bf16[8192,512]{1,0:T(8,128)(2,1)} fusion(bf16[8192,224]{1,0:T(8,128)(2,1)} %copy.28, bf16[8192,224]{1,0:T(8,128)(2,1)} %copy.27), kind=kLoop, calls=%fused_computation.4 | loop fusion | flops 33554432 | bytes 15728640 | tf_op jit(solution)/shard_map/concatenate | solution.py:55
  44.7 61.9 %all-gather.2.cloned.1.call-done.act_ref.cot_ref = bf16[512,16384]{1,0:T(8,128)(2,1)} async-done(((bf16[32,16384]{1,0:T(8,128)(2,1)}), bf16[512,16384]{1,0:T(8,128)(2,1)}) %all-gather.2.cloned.1.call-update) | async-done | bytes 16777232 | tf_op jit(solution)/shard_map/all_gather | solution.py:120
  106.6 14.0 %shard_map.149 = f32[512,192]{1,0:T(8,128)} custom-call(bf16[512,16384]{1,0:T(8,128)(2,1)} %all-gather.2.cloned.1.call-done.act_ref.cot_ref, bf16[512,16384]{1,0:T(8,128)(2,1)} %all-gather.2.cloned.1.call-done.act_ref.cot_ref, bf16[8192,512]{1,0:T(8,128)(2,1)} %fusion.2.wa_ref, bf16[8192,256]{1,0:T(8,128)(2,1)} %pad.12.wc_ref, bf16[224,64]{1,0:T(8,128)(2,1)} %copy.30.go_ref, ...), custom_call_target="tpu_custom_call" | custom-call | flops 5681184768 | bytes 29839360 | tf_op jit(solution)/shard_map/pallas_call | solution.py:60
  120.6 2.0 %reshape.32 = f32[128,4,192]{2,1,0:T(4,128)} reshape(f32[512,192]{1,0:T(8,128)} %shard_map.149) | data formatting | bytes 786432 | tf_op jit(solution)/shard_map/reshape | solution.py:90
  122.6 8.8 %all-to-all-start = ((f32[128,4,192]{2,1,0:T(4,128)}), f32[128,4,192]{2,1,0:T(4,128)S(1)}, u32[]{:S(2)}, u32[]{:S(2)}) async-start(f32[128,4,192]{2,1,0:T(4,128)} %reshape.32), calls=%async_computation | async-start | bytes 1048576 | tf_op jit(solution)/shard_map/all_to_all | solution.py:91
  131.5 6.8 %fusion.5 = f32[512,128]{0,1:T(8,128)S(1)} fusion(bf16[512,16384]{1,0:T(8,128)(2,1)} %all-gather.2.cloned.1.call-done.act_ref.cot_ref, bf16[8192,64]{0,1:T(8,128)(2,1)} %param.21, bf16[8192,64]{0,1:T(8,128)(2,1)} %param.20), kind=kOutput, calls=%fused_computation.7 | convolution fusion | flops 1077936128 | bytes 10747904 | tf_op jit(solution)/shard_map/dot_general | solution.py:125
  138.6 6.9 %all-to-all-done = f32[128,4,192]{2,1,0:T(4,128)S(1)} async-done(((f32[128,4,192]{2,1,0:T(4,128)}), f32[128,4,192]{2,1,0:T(4,128)S(1)}, u32[]{:S(2)}, u32[]{:S(2)}) %all-to-all-start) | async-done | bytes 393248 | tf_op jit(solution)/shard_map/all_to_all | solution.py:91
  145.7 0.9 broadcast_in_dim.2
  146.5 3.9 %all-to-all-start.1 = ((f32[128,4,192]{2,1,0:T(4,128)}), f32[128,4,192]{2,1,0:T(4,128)S(1)}, u32[]{:S(2)}, u32[]{:S(2)}) async-start(f32[128,4,192]{2,1,0:T(4,128)} %broadcast_in_dim.2), calls=%async_computation.1 | async-start | bytes 1048576 | tf_op jit(solution)/shard_map/all_to_all | solution.py:96
  150.5 6.5 %fusion.3 = f32[512,64]{1,0:T(8,128)} fusion(bf16[8192,64]{0,1:T(8,128)(2,1)S(1)} %copy-done, bf16[512,16384]{1,0:T(8,128)(2,1)} %all-gather.2.cloned.1.call-done.act_ref.cot_ref), kind=kOutput, calls=%fused_computation.5 | convolution fusion | flops 536870912 | bytes 9568256 | tf_op jit(solution)/shard_map/dot_general | solution.py:130
  157.0 7.5 %all-to-all-done.1 = f32[128,4,192]{2,1,0:T(4,128)S(1)} async-done(((f32[128,4,192]{2,1,0:T(4,128)}), f32[128,4,192]{2,1,0:T(4,128)S(1)}, u32[]{:S(2)}, u32[]{:S(2)}) %all-to-all-start.1) | async-done | bytes 393248 | tf_op jit(solution)/shard_map/all_to_all | solution.py:96
  164.8 3.7 %convolution_convert_fusion = bf16[16,3,64,64]{3,2,1,0:T(8,128)(2,1)S(1)} fusion(f32[1,16,32,64]{3,2,0,1:T(8,128)S(1)} %bitcast.27, f32[1,16,32,64]{3,2,0,1:T(8,128)S(1)} %bitcast.24, f32[1,16,32,64]{3,2,0,1:T(8,128)S(1)} %bitcast.23, f32[1,16,32,64]{3,2,0,1:T(8,128)} %bitcast.28, f32[1,16,32,64]{3,2,0,1:T(8,128)S(1)} %bitcast.26, ...), kind=kOutput, calls=%fused_computation.12 | convolution fusion | flops 76087296 | bytes 1179648 | tf_op jit(solution)/shard_map/bdlr,bdls->dbrs/dot_general | solution.py:139
  170.0 0.9 reshape.35
  170.9 3.9 %all-to-all-start.2 = ((f32[128,1,128]{2,1,0:T(1,128)}), f32[128,1,128]{2,1,0:T(1,128)S(1)}, u32[]{:S(2)}, u32[]{:S(2)}) async-start(f32[128,1,128]{2,1,0:T(1,128)} %reshape.35), calls=%async_computation.2 | async-start | bytes 131072 | tf_op jit(solution)/shard_map/all_to_all | solution.py:91
  175.5 9.2 %all-to-all-done.2 = f32[128,1,128]{2,1,0:T(1,128)S(1)} async-done(((f32[128,1,128]{2,1,0:T(1,128)}), f32[128,1,128]{2,1,0:T(1,128)S(1)}, u32[]{:S(2)}, u32[]{:S(2)}) %all-to-all-start.2) | async-done | bytes 65568 | tf_op jit(solution)/shard_map/all_to_all | solution.py:91
  185.2 0.8 reduce
  186.2 0.7 reduce_sum.19
  (29 shorter events, 5.8 us)
Async XLA Ops:
  7.2 143.3 %copy-start = (bf16[8192,64]{0,1:T(8,128)(2,1)S(1)}, bf16[8192,64]{0,1:T(8,128)(2,1)}, u32[]{:S(2)}) copy-start(bf16[8192,64]{0,1:T(8,128)(2,1)} %param.22) | copy-start | bytes 3145732
  7.2 99.4 %all-gather.2.cloned.1.call-start = ((), (), s32[]{:S(2)}) async-start(), calls=%async_computation.3 | async-start | bytes 17825792 | tf_op jit(solution)/shard_map/all_gather | solution.py:120
  17.5 12.6 %copy-start.2 = (bf16[224,64]{0,1:T(8,128)(2,1)S(1)}, bf16[224,64]{0,1:T(8,128)(2,1)}, u32[]{:S(2)}) copy-start(bf16[224,64]{0,1:T(8,128)(2,1)} %param.23) | copy-start | bytes 86020
  17.5 13.3 %copy-start.3 = (bf16[224,64]{0,1:T(8,128)(2,1)S(1)}, bf16[224,64]{0,1:T(8,128)(2,1)}, u32[]{:S(2)}) copy-start(bf16[224,64]{0,1:T(8,128)(2,1)} %param.24) | copy-start | bytes 86020
  17.5 14.0 %copy-start.4 = (bf16[224,64]{0,1:T(8,128)(2,1)S(1)}, bf16[224,64]{0,1:T(8,128)(2,1)}, u32[]{:S(2)}) copy-start(bf16[224,64]{0,1:T(8,128)(2,1)} %param.25) | copy-start | bytes 86020
  122.6 22.9 %all-to-all-start = ((f32[128,4,192]{2,1,0:T(4,128)}), f32[128,4,192]{2,1,0:T(4,128)S(1)}, u32[]{:S(2)}, u32[]{:S(2)}) async-start(f32[128,4,192]{2,1,0:T(4,128)} %reshape.32), calls=%async_computation | async-start | bytes 1048576 | tf_op jit(solution)/shard_map/all_to_all | solution.py:91
  146.5 17.9 %all-to-all-start.1 = ((f32[128,4,192]{2,1,0:T(4,128)}), f32[128,4,192]{2,1,0:T(4,128)S(1)}, u32[]{:S(2)}, u32[]{:S(2)}) async-start(f32[128,4,192]{2,1,0:T(4,128)} %broadcast_in_dim.2), calls=%async_computation.1 | async-start | bytes 1048576 | tf_op jit(solution)/shard_map/all_to_all | solution.py:96
  150.5 18.7 %copy-start.1 = (bf16[32,12288]{1,0:T(8,128)(2,1)S(1)}, bf16[32,12288]{1,0:T(8,128)(2,1)}, u32[]{:S(2)}) copy-start(bf16[32,12288]{1,0:T(8,128)(2,1)} %param.26) | copy-start | bytes 2359300
  150.5 19.1 %copy-start.5 = (s32[32]{0:T(128)S(1)}, s32[32]{0:T(128)}, u32[]{:S(2)}) copy-start(s32[32]{0:T(128)} %param.27) | copy-start | bytes 388
  170.9 13.8 %all-to-all-start.2 = ((f32[128,1,128]{2,1,0:T(1,128)}), f32[128,1,128]{2,1,0:T(1,128)S(1)}, u32[]{:S(2)}, u32[]{:S(2)}) async-start(f32[128,1,128]{2,1,0:T(1,128)} %reshape.35), calls=%async_computation.2 | async-start | bytes 131072 | tf_op jit(solution)/shard_map/all_to_all | solution.py:91
Sparse Core Ops, SparseCore 0:
  11.3 95.1 all-gather.1

commit v8 on v7

--- a/solution.py
+++ b/solution.py
@@ -10,7 +10,7 @@
 EX_DEV = 8
 ALL = ("dp", "tensor")
 
-KC = 2048
+KC = 1024
 LANE = 128
 
 

time: 195 us -> 196 us (level)
  transfers between devices with their start and end apart: 4 -> 4, of which waited for: 4 -> 4; matrix products, arithmetic and copies ran while one was open for 25% -> 24% of each run, Pallas kernels for 0% -> 0%
where the time goes in v8:
time: 196 us; the launch traced here: 195 us
  waiting for transfers between devices  85.6 us (44%)
  local copies, waits for them, and re-layouts  32.2 us (16%)
  matrix products  17.9 us (9%)
  starting transfers between devices  16.7 us (9%)
  Pallas kernels  15.3 us (8%)
  between operations  14.2 us (7%)
  other arithmetic  13.3 us (7%)
    all_gather x1, waiting for transfers between devices, body(): lax.all_gather(jnp.concatenate([hidden_in, masked], axis=1), 'dp', axis=0...  61.9 us
    unnamed x20, local copies, waits for them, and re-layouts  22.1 us
    all_to_all x2, waiting for transfers between devices, scatter_sum(): return jnp.sum(lax.all_to_all(blocks, ALL, 0, 0, tiled=False), axis=0)  16.1 us
    pallas_call x1, Pallas kernels, layer_call(): pl.pallas_call(layer_kernel, grid=(nk,), in_specs=[pl.BlockSpec((rows, KC...  15.3 us
    all_to_all x2, starting transfers between devices, scatter_sum(): return jnp.sum(lax.all_to_all(blocks, ALL, 0, 0, tiled=False), axis=0)  12.7 us
    concatenate x1, other arithmetic, layer_call(): wa = jnp.concatenate([pad_to(gw, fp), pad_to(uw, fp)], 1)  7.61 us
    all_to_all x1, waiting for transfers between devices, gather_rows(): got = lax.all_to_all(copies, ALL, 0, 0, tiled=False)  7.54 us
    dot_general x1, matrix products, body(): jnp.dot(both[:, :d_model], jnp.concatenate([gate_in_proj, up_in_proj], ax...  6.83 us
  transfers between devices with their start and end apart: 4, of which 4 were waited for; matrix products, arithmetic and copies ran while one was open for 24% of the time, Pallas kernels for 0%

profile of v8, /device:TPU:1, one launch (start us, length us, event | category | flops | bytes accessed | tf_op | source)
XLA Modules:
  0.0 195.1 jit_solution(8445907117163817238)
XLA Ops:
  7.2 0.7 compare_convert_fusion
  8.0 1.1 broadcast_multiply_fusion
  9.1 2.1 %pad_maximum_fusion = bf16[32,16384]{1,0:T(8,128)(2,1)} fusion(bf16[32,8192]{1,0:T(8,128)(2,1)S(1)} %broadcast_multiply_fusion, bf16[32,8192]{1,0:T(8,128)(2,1)} %param.15), kind=kLoop, calls=%fused_computation.14 | loop fusion | flops 2097152 | bytes 2097152 | tf_op jit(solution)/shard_map/concatenate | solution.py:120
  11.2 6.3 %copy.27 = bf16[8192,224]{1,0:T(8,128)(2,1)} copy(bf16[8192,224]{0,1:T(8,128)(2,1)} %param.17) | data formatting | bytes 7340032 | tf_op args[3]
  17.5 6.3 %copy.28 = bf16[8192,224]{1,0:T(8,128)(2,1)} copy(bf16[8192,224]{0,1:T(8,128)(2,1)} %param.18) | data formatting | bytes 7340032 | tf_op args[4]
  23.8 6.3 %copy.29 = bf16[224,8192]{0,1:T(8,128)(2,1)} copy(bf16[224,8192]{1,0:T(8,128)(2,1)} %param.19) | data formatting | bytes 7340032 | tf_op args[5]
  32.2 4.9 %pad.12.wc_ref = bf16[8192,256]{1,0:T(8,128)(2,1)} pad(bf16[8192,224]{1,0:T(8,128)(2,1)} %bitcast.22, bf16[]{:T(256)} %constant.4.clone.1), padding=0_0x0_32 | pad | bytes 7864322 | tf_op jit(solution)/shard_map/jit(_pad)/pad | solution.py:18
  37.1 7.6 %fusion.2.wa_ref = bf16[8192,512]{1,0:T(8,128)(2,1)} fusion(bf16[8192,224]{1,0:T(8,128)(2,1)} %copy.28, bf16[8192,224]{1,0:T(8,128)(2,1)} %copy.27), kind=kLoop, calls=%fused_computation.4 | loop fusion | flops 33554432 | bytes 15728640 | tf_op jit(solution)/shard_map/concatenate | solution.py:55
  44.7 61.9 %all-gather.2.cloned.1.call-done.act_ref.cot_ref = bf16[512,16384]{1,0:T(8,128)(2,1)} async-done(((bf16[32,16384]{1,0:T(8,128)(2,1)}), bf16[512,16384]{1,0:T(8,128)(2,1)}) %all-gather.2.cloned.1.call-update) | async-done | bytes 16777232 | tf_op jit(solution)/shard_map/all_gather | solution.py:120
  106.6 15.3 %shard_map.149 = f32[512,192]{1,0:T(8,128)} custom-call(bf16[512,16384]{1,0:T(8,128)(2,1)} %all-gather.2.cloned.1.call-done.act_ref.cot_ref, bf16[512,16384]{1,0:T(8,128)(2,1)} %all-gather.2.cloned.1.call-done.act_ref.cot_ref, bf16[8192,512]{1,0:T(8,128)(2,1)} %fusion.2.wa_ref, bf16[8192,256]{1,0:T(8,128)(2,1)} %pad.12.wc_ref, bf16[224,64]{1,0:T(8,128)(2,1)} %copy.30.go_ref, ...), custom_call_target="tpu_custom_call" | custom-call | flops 5681184768 | bytes 29839360 | tf_op jit(solution)/shard_map/pallas_call | solution.py:60
  121.9 2.0 %reshape.32 = f32[128,4,192]{2,1,0:T(4,128)} reshape(f32[512,192]{1,0:T(8,128)} %shard_map.149) | data formatting | bytes 786432 | tf_op jit(solution)/shard_map/reshape | solution.py:90
  123.9 8.8 %all-to-all-start = ((f32[128,4,192]{2,1,0:T(4,128)}), f32[128,4,192]{2,1,0:T(4,128)S(1)}, u32[]{:S(2)}, u32[]{:S(2)}) async-start(f32[128,4,192]{2,1,0:T(4,128)} %reshape.32), calls=%async_computation | async-start | bytes 1048576 | tf_op jit(solution)/shard_map/all_to_all | solution.py:91
  132.7 6.8 %fusion.5 = f32[512,128]{0,1:T(8,128)S(1)} fusion(bf16[512,16384]{1,0:T(8,128)(2,1)} %all-gather.2.cloned.1.call-done.act_ref.cot_ref, bf16[8192,64]{0,1:T(8,128)(2,1)} %param.21, bf16[8192,64]{0,1:T(8,128)(2,1)} %param.20), kind=kOutput, calls=%fused_computation.7 | convolution fusion | flops 1077936128 | bytes 10747904 | tf_op jit(solution)/shard_map/dot_general | solution.py:125
  139.9 6.9 %all-to-all-done = f32[128,4,192]{2,1,0:T(4,128)S(1)} async-done(((f32[128,4,192]{2,1,0:T(4,128)}), f32[128,4,192]{2,1,0:T(4,128)S(1)}, u32[]{:S(2)}, u32[]{:S(2)}) %all-to-all-start) | async-done | bytes 393248 | tf_op jit(solution)/shard_map/all_to_all | solution.py:91
  146.9 0.9 broadcast_in_dim.2
  147.8 3.9 %all-to-all-start.1 = ((f32[128,4,192]{2,1,0:T(4,128)}), f32[128,4,192]{2,1,0:T(4,128)S(1)}, u32[]{:S(2)}, u32[]{:S(2)}) async-start(f32[128,4,192]{2,1,0:T(4,128)} %broadcast_in_dim.2), calls=%async_computation.1 | async-start | bytes 1048576 | tf_op jit(solution)/shard_map/all_to_all | solution.py:96
  151.8 6.5 %fusion.3 = f32[512,64]{1,0:T(8,128)} fusion(bf16[8192,64]{0,1:T(8,128)(2,1)S(1)} %copy-done, bf16[512,16384]{1,0:T(8,128)(2,1)} %all-gather.2.cloned.1.call-done.act_ref.cot_ref), kind=kOutput, calls=%fused_computation.5 | convolution fusion | flops 536870912 | bytes 9568256 | tf_op jit(solution)/shard_map/dot_general | solution.py:130
  158.2 7.5 %all-to-all-done.1 = f32[128,4,192]{2,1,0:T(4,128)S(1)} async-done(((f32[128,4,192]{2,1,0:T(4,128)}), f32[128,4,192]{2,1,0:T(4,128)S(1)}, u32[]{:S(2)}, u32[]{:S(2)}) %all-to-all-start.1) | async-done | bytes 393248 | tf_op jit(solution)/shard_map/all_to_all | solution.py:96
  166.1 3.7 %convolution_convert_fusion = bf16[16,3,64,64]{3,2,1,0:T(8,128)(2,1)S(1)} fusion(f32[1,16,32,64]{3,2,0,1:T(8,128)S(1)} %bitcast.27, f32[1,16,32,64]{3,2,0,1:T(8,128)S(1)} %bitcast.24, f32[1,16,32,64]{3,2,0,1:T(8,128)S(1)} %bitcast.23, f32[1,16,32,64]{3,2,0,1:T(8,128)} %bitcast.28, f32[1,16,32,64]{3,2,0,1:T(8,128)S(1)} %bitcast.26, ...), kind=kOutput, calls=%fused_computation.12 | convolution fusion | flops 76087296 | bytes 1179648 | tf_op jit(solution)/shard_map/bdlr,bdls->dbrs/dot_general | solution.py:139
  171.3 0.9 reshape.35
  172.2 3.9 %all-to-all-start.2 = ((f32[128,1,128]{2,1,0:T(1,128)}), f32[128,1,128]{2,1,0:T(1,128)S(1)}, u32[]{:S(2)}, u32[]{:S(2)}) async-start(f32[128,1,128]{2,1,0:T(1,128)} %reshape.35), calls=%async_computation.2 | async-start | bytes 131072 | tf_op jit(solution)/shard_map/all_to_all | solution.py:91
  176.8 9.2 %all-to-all-done.2 = f32[128,1,128]{2,1,0:T(1,128)S(1)} async-done(((f32[128,1,128]{2,1,0:T(1,128)}), f32[128,1,128]{2,1,0:T(1,128)S(1)}, u32[]{:S(2)}, u32[]{:S(2)}) %all-to-all-start.2) | async-done | bytes 65568 | tf_op jit(solution)/shard_map/all_to_all | solution.py:91
  186.5 0.8 reduce
  187.5 0.7 reduce_sum.19
  (29 shorter events, 5.8 us)
Async XLA Ops:
  7.2 144.6 %copy-start = (bf16[8192,64]{0,1:T(8,128)(2,1)S(1)}, bf16[8192,64]{0,1:T(8,128)(2,1)}, u32[]{:S(2)}) copy-start(bf16[8192,64]{0,1:T(8,128)(2,1)} %param.22) | copy-start | bytes 3145732
  7.2 99.4 %all-gather.2.cloned.1.call-start = ((), (), s32[]{:S(2)}) async-start(), calls=%async_computation.3 | async-start | bytes 17825792 | tf_op jit(solution)/shard_map/all_gather | solution.py:120
  17.5 12.6 %copy-start.2 = (bf16[224,64]{0,1:T(8,128)(2,1)S(1)}, bf16[224,64]{0,1:T(8,128)(2,1)}, u32[]{:S(2)}) copy-start(bf16[224,64]{0,1:T(8,128)(2,1)} %param.23) | copy-start | bytes 86020
  17.5 13.3 %copy-start.3 = (bf16[224,64]{0,1:T(8,128)(2,1)S(1)}, bf16[224,64]{0,1:T(8,128)(2,1)}, u32[]{:S(2)}) copy-start(bf16[224,64]{0,1:T(8,128)(2,1)} %param.24) | copy-start | bytes 86020
  17.5 14.0 %copy-start.4 = (bf16[224,64]{0,1:T(8,128)(2,1)S(1)}, bf16[224,64]{0,1:T(8,128)(2,1)}, u32[]{:S(2)}) copy-start(bf16[224,64]{0,1:T(8,128)(2,1)} %param.25) | copy-start | bytes 86020
  123.9 22.9 %all-to-all-start = ((f32[128,4,192]{2,1,0:T(4,128)}), f32[128,4,192]{2,1,0:T(4,128)S(1)}, u32[]{:S(2)}, u32[]{:S(2)}) async-start(f32[128,4,192]{2,1,0:T(4,128)} %reshape.32), calls=%async_computation | async-start | bytes 1048576 | tf_op jit(solution)/shard_map/all_to_all | solution.py:91
  147.8 17.9 %all-to-all-start.1 = ((f32[128,4,192]{2,1,0:T(4,128)}), f32[128,4,192]{2,1,0:T(4,128)S(1)}, u32[]{:S(2)}, u32[]{:S(2)}) async-start(f32[128,4,192]{2,1,0:T(4,128)} %broadcast_in_dim.2), calls=%async_computation.1 | async-start | bytes 1048576 | tf_op jit(solution)/shard_map/all_to_all | solution.py:96
  151.7 18.7 %copy-start.1 = (bf16[32,12288]{1,0:T(8,128)(2,1)S(1)}, bf16[32,12288]{1,0:T(8,128)(2,1)}, u32[]{:S(2)}) copy-start(bf16[32,12288]{1,0:T(8,128)(2,1)} %param.26) | copy-start | bytes 2359300
  151.7 19.1 %copy-start.5 = (s32[32]{0:T(128)S(1)}, s32[32]{0:T(128)}, u32[]{:S(2)}) copy-start(s32[32]{0:T(128)} %param.27) | copy-start | bytes 388
  172.2 13.8 %all-to-all-start.2 = ((f32[128,1,128]{2,1,0:T(1,128)}), f32[128,1,128]{2,1,0:T(1,128)S(1)}, u32[]{:S(2)}, u32[]{:S(2)}) async-start(f32[128,1,128]{2,1,0:T(1,128)} %reshape.35), calls=%async_computation.2 | async-start | bytes 131072 | tf_op jit(solution)/shard_map/all_to_all | solution.py:91
Sparse Core Ops, SparseCore 0:
  11.3 95.1 all-gather.1

commit v9 on v7

--- a/solution.py
+++ b/solution.py
@@ -86,6 +86,42 @@
     )(both, both, wa, wc, go, uo, di)
 
 
+def ring_perm(n, f):
+    return [(i, f(i) % n) for i in range(n)]
+
+
+def shared_gather(x, n):
+    pp = lambda v, p: lax.ppermute(v, "dp", p)
+    zp = ring_perm(n, lambda i: i + 4)
+    zm = ring_perm(n, lambda i: i - 4)
+    yy = ring_perm(n, lambda i: i ^ 2)
+    cc = ring_perm(n, lambda i: i ^ 1)
+    half = x.shape[0] // 2
+    from_zm = pp(x, zp)
+    from_zp = pp(x, zm)
+    from_y = pp(x, yy)
+    o_own = pp(x, cc)
+    b_z2 = pp(from_zp, zm)
+    b_zm_y = pp(from_y, zp)
+    b_zp_y = pp(from_zp, yy)
+    o_b = pp(jnp.stack([from_zm, from_zp, from_y]), cc)
+    c_z2_y = jnp.concatenate([pp(b_z2[:half], yy), pp(b_zp_y[half:], zm)], axis=0)
+    o_c = pp(jnp.stack([b_z2, b_zm_y, b_zp_y]), cc)
+    o_d = pp(c_z2_y, cc)
+    slots = [x, from_zm, from_zp, from_y, b_z2, b_zm_y, b_zp_y, c_z2_y,
+             o_own, o_b[0], o_b[1], o_b[2], o_c[0], o_c[1], o_c[2], o_d]
+    d = lax.axis_index("dp")
+    mine = [d, d - 4, d + 4, d ^ 2, d + 8, (d - 4) % n ^ 2, (d ^ 2) + 4, (d ^ 2) + 8]
+    ids = jnp.stack([m % n for m in mine] + [(m % n) ^ 1 for m in mine])
+    return jnp.concatenate(slots, axis=0), jnp.argsort(ids)
+
+
+def to_dp_order(x, order):
+    n = order.shape[0]
+    blocks = x.reshape((n, x.shape[0] // n) + x.shape[1:])
+    return jnp.take(blocks, order, axis=0).reshape(x.shape)
+
+
 def scatter_sum(x, n):
     blocks = x.reshape((n, x.shape[0] // n) + x.shape[1:])
     return jnp.sum(lax.all_to_all(blocks, ALL, 0, 0, tiled=False), axis=0)
@@ -117,17 +153,18 @@
     proj_rank = gate_in_proj.shape[1]
     pad_mask = (token_ids != 0).astype(jnp.bfloat16)[:, None]
     masked = cotangent * pad_mask
-    both = lax.all_gather(jnp.concatenate([hidden_in, masked], axis=1), "dp", axis=0, tiled=True)
+    both, order = shared_gather(jnp.concatenate([hidden_in, masked], axis=1), lax.axis_size("dp"))
     f32 = jnp.float32
     block = layer_call(both, gate_weight, up_weight, down_weight, gate_out_proj, up_out_proj, down_in_proj)
-    summed = gather_rows(scatter_sum(block, n_all), n_all)
+    summed = gather_rows(scatter_sum(to_dp_order(block, order), n_all), n_all)
     d_model = hidden_in.shape[1]
     in_both = jnp.dot(
         both[:, :d_model], jnp.concatenate([gate_in_proj, up_in_proj], axis=1), preferred_element_type=f32
     )
+    in_both = to_dp_order(in_both, order)
     in_gate = in_both[:, :proj_rank]
     in_up = in_both[:, proj_rank:]
-    out_down = jnp.dot(both[:, d_model:], down_out_proj, preferred_element_type=f32)
+    out_down = to_dp_order(jnp.dot(both[:, d_model:], down_out_proj, preferred_element_type=f32), order)
     docs = both.shape[0] // LEN
 
     side_gate = summed[:, :proj_rank]

time: 195 us -> 188 us (0.964)
  waiting for transfers between devices: 85.6 us -> 47.7 us
  local copies, waits for them, and re-layouts: 32.2 us -> 54.7 us
  starting transfers between devices: 16.7 us -> 38.2 us
  between operations: 14.2 us -> 0.9 us
  other arithmetic: 13.3 us -> 18 us
  matrix products: 17.9 us -> 13.4 us
    all_gather x1 -> x0, waiting for transfers between devices: 61.9 us -> none  [body(): lax.all_gather(jnp.concatenate([hidden_in, masked], axis=1), 'dp', axis=0...]
    ppermute x0 -> x12, waiting for transfers between devices: none -> 23 us  [shared_gather(): pp = lambda v, p: lax.ppermute(v, 'dp', p)]
    unnamed x20 -> x35, local copies, waits for them, and re-layouts: 22.1 us -> 42.3 us
    ppermute x0 -> x12, starting transfers between devices: none -> 16.8 us  [shared_gather(): pp = lambda v, p: lax.ppermute(v, 'dp', p)]
    all_to_all x1, waiting for transfers between devices: 7.54 us -> 13.8 us  [gather_rows(): got = lax.all_to_all(copies, ALL, 0, 0, tiled=False)]
    all_to_all x2, waiting for transfers between devices: 16.1 us -> 11 us  [scatter_sum(): return jnp.sum(lax.all_to_all(blocks, ALL, 0, 0, tiled=False), axis=0)]
    dot_general x1, matrix products: 6.47 us -> 2.31 us  [body(): jnp.dot(both[:, d_model:], down_out_proj, preferred_element_type=f32)]
    all_to_all x1, starting transfers between devices: 3.9 us -> 8.04 us  [gather_rows(): got = lax.all_to_all(copies, ALL, 0, 0, tiled=False)]
  transfers between devices with their start and end apart: 4 -> 15, of which waited for: 4 -> 7; matrix products, arithmetic and copies ran while one was open for 25% -> 35% of each run, Pallas kernels for 0% -> 0%
where the time goes in v9:
time: 188 us; the launch traced here: 187 us
  local copies, waits for them, and re-layouts  54.7 us (29%)
  waiting for transfers between devices  47.7 us (25%)
  starting transfers between devices  38.2 us (20%)
  other arithmetic  18 us (10%)
  Pallas kernels  14 us (7%)
  matrix products  13.4 us (7%)
    unnamed x35, local copies, waits for them, and re-layouts  42.3 us
    ppermute x12, waiting for transfers between devices, shared_gather(): pp = lambda v, p: lax.ppermute(v, 'dp', p)  23 us
    ppermute x12, starting transfers between devices, shared_gather(): pp = lambda v, p: lax.ppermute(v, 'dp', p)  16.8 us
    pallas_call x1, Pallas kernels, layer_call(): pl.pallas_call(layer_kernel, grid=(nk,), in_specs=[pl.BlockSpec((rows, KC...  14 us
    all_to_all x1, waiting for transfers between devices, gather_rows(): got = lax.all_to_all(copies, ALL, 0, 0, tiled=False)  13.8 us
    all_to_all x2, starting transfers between devices, scatter_sum(): return jnp.sum(lax.all_to_all(blocks, ALL, 0, 0, tiled=False), axis=0)  13.4 us
    all_to_all x2, waiting for transfers between devices, scatter_sum(): return jnp.sum(lax.all_to_all(blocks, ALL, 0, 0, tiled=False), axis=0)  11 us
    all_to_all x1, starting transfers between devices, gather_rows(): got = lax.all_to_all(copies, ALL, 0, 0, tiled=False)  8.04 us
  transfers between devices with their start and end apart: 15, of which 7 were waited for; matrix products, arithmetic and copies ran while one was open for 35% of the time, Pallas kernels for 0%

profile of v9, /device:TPU:1, one launch (start us, length us, event | category | flops | bytes accessed | tf_op | source)
XLA Modules:
  0.0 186.9 jit_solution(13924083832304429026)
XLA Ops:
  2.6 2.5 %pad_maximum_fusion.3 = (bf16[32,16384]{1,0:T(8,128)(2,1)}, bf16[512,16384]{1,0:T(8,128)(2,1)}) fusion(bf16[32,8192]{1,0:T(8,128)(2,1)S(1)} %broadcast_multiply_fusion, bf16[32,8192]{1,0:T(8,128)(2,1)} %param.15), kind=kLoop, calls=%fused_computation.32 | loop fusion | flops 2097151 | bytes 3145728 | tf_op jit(solution)/shard_map/concatenate | solution.py:156
  5.1 2.5 %collective-permute-start = (bf16[32,16384]{1,0:T(8,128)(2,1)}, bf16[32,16384]{1,0:T(8,128)(2,1)}, u32[]{:S(2)}, u32[]{:S(2)}) collective-permute-start(bf16[32,16384]{1,0:T(8,128)(2,1)} %get-tuple-element.4), channel_id=1, source_target_pairs={{0,32},{8,40},{16,48},{24,56},{32,64},{40,72},{48,80},{56,88},{64,... | collective-permute-start | bytes 3145736 | tf_op jit(solution)/shard_map/ppermute | solution.py:94
  13.6 6.2 %copy.23 = bf16[8192,224]{1,0:T(8,128)(2,1)} copy(bf16[8192,224]{0,1:T(8,128)(2,1)} %param.18) | data formatting | bytes 7340032 | tf_op args[4]
  19.8 6.3 %copy.22 = bf16[8192,224]{1,0:T(8,128)(2,1)} copy(bf16[8192,224]{0,1:T(8,128)(2,1)} %param.17) | data formatting | bytes 7340032 | tf_op args[3]
  26.1 6.2 %copy.24 = bf16[224,8192]{0,1:T(8,128)(2,1)} copy(bf16[224,8192]{1,0:T(8,128)(2,1)} %param.19) | data formatting | bytes 7340032 | tf_op args[5]
  34.8 4.8 %pad.12.wc_ref = bf16[8192,256]{1,0:T(8,128)(2,1)} pad(bf16[8192,224]{1,0:T(8,128)(2,1)} %bitcast.68, bf16[]{:T(256)} %constant.116.clone.1), padding=0_0x0_32 | pad | bytes 7864322 | tf_op jit(solution)/shard_map/jit(_pad)/pad | solution.py:18
  39.6 7.4 %fusion.2.wa_ref = bf16[8192,512]{1,0:T(8,128)(2,1)} fusion(bf16[8192,224]{1,0:T(8,128)(2,1)} %copy.23, bf16[8192,224]{1,0:T(8,128)(2,1)} %copy.22), kind=kLoop, calls=%fused_computation.7 | loop fusion | flops 33554432 | bytes 15728640 | tf_op jit(solution)/shard_map/concatenate | solution.py:55
  50.7 2.3 %constant_dynamic-update-slice_fusion.9 = bf16[512,16384]{1,0:T(8,128)(2,1)} fusion(bf16[512,16384]{1,0:T(8,128)(2,1)} %get-tuple-element.5, bf16[32,16384]{1,0:T(8,128)(2,1)} %collective-permute-done), kind=kLoop, calls=%fused_computation.59 | loop fusion | bytes 2097152
  55.1 17.9 %collective-permute-done.3 = bf16[32,16384]{1,0:T(8,128)(2,1)S(1)} collective-permute-done((bf16[32,16384]{1,0:T(8,128)(2,1)S(1)}, bf16[32,16384]{1,0:T(8,128)(2,1)S(1)}, u32[]{:S(2)}, u32[]{:S(2)}) %collective-permute-start.3) | collective-permute-done | bytes 1048608 | tf_op jit(solution)/shard_map/ppermute | solution.py:94
  74.6 2.5 %collective-permute-start.7 = (bf16[16,16384]{1,0:T(8,128)(2,1)S(1)}, bf16[16,16384]{1,0:T(8,128)(2,1)S(1)}, u32[]{:S(2)}, u32[]{:S(2)}) collective-permute-start(bf16[16,16384]{1,0:T(8,128)(2,1)S(1)} %slice.67), channel_id=1, source_target_pairs={{0,96},{8,104},{16,112},{24,120},{32,0},{40,8},{48,16},{56,24},{64... | collective-permute-start | bytes 1572872 | tf_op jit(solution)/shard_map/ppermute | solution.py:94
  77.4 2.2 %collective-permute-start.10 = (bf16[3,32,16384]{2,1,0:T(8,128)(2,1)S(1)}, bf16[3,32,16384]{2,1,0:T(8,128)(2,1)S(1)}, u32[]{:S(2)}, u32[]{:S(2)}) collective-permute-start(bf16[3,32,16384]{2,1,0:T(8,128)(2,1)S(1)} %pad_maximum_fusion.1), channel_id=1, source_target_pairs={{0,8},{8,0},{16,24},{24,16},{32,40},{40,32},{48,56},{56,48},{64,72... | collective-permute-start | bytes 9437192 | tf_op jit(solution)/shard_map/ppermute | solution.py:94
  82.8 2.6 %collective-permute-done.6 = bf16[16,16384]{1,0:T(8,128)(2,1)S(1)} collective-permute-done((bf16[16,16384]{1,0:T(8,128)(2,1)S(1)}, bf16[16,16384]{1,0:T(8,128)(2,1)S(1)}, u32[]{:S(2)}, u32[]{:S(2)}) %collective-permute-start.6) | collective-permute-done | bytes 524320 | tf_op jit(solution)/shard_map/ppermute | solution.py:94
  86.6 2.7 %collective-permute-start.11 = (bf16[32,16384]{1,0:T(8,128)(2,1)S(1)}, bf16[32,16384]{1,0:T(8,128)(2,1)S(1)}, u32[]{:S(2)}, u32[]{:S(2)}) collective-permute-start(bf16[32,16384]{1,0:T(8,128)(2,1)S(1)} %pad_maximum_fusion.2), channel_id=1, source_target_pairs={{0,8},{8,0},{16,24},{24,16},{32,40},{40,32},{48,56},{56,48},{64,72... | collective-permute-start | bytes 3145736 | tf_op jit(solution)/shard_map/ppermute | solution.py:94
  91.1 2.4 %constant_dynamic-update-slice_fusion.1 = bf16[512,16384]{1,0:T(8,128)(2,1)} fusion(bf16[512,16384]{1,0:T(8,128)(2,1)} %constant_dynamic-update-slice_fusion.2, bf16[32,16384]{1,0:T(8,128)(2,1)} %collective-permute-done.8), kind=kLoop, calls=%fused_computation.51 | loop fusion | bytes 2097152
  100.8 14.0 %shard_map.149 = f32[512,192]{1,0:T(8,128)} custom-call(bf16[512,16384]{1,0:T(8,128)(2,1)} %constant_dynamic-update-slice_fusion.act_ref.cot_ref, bf16[512,16384]{1,0:T(8,128)(2,1)} %constant_dynamic-update-slice_fusion.act_ref.cot_ref, bf16[8192,512]{1,0:T(8,128)(2,1)} %fusion.2.wa_ref, bf16[8192,256]{1,0:T(8,128)(2,1)} %pad.12.wc_ref, ...), custom_call_target="tpu_custom_call" | custom-call | flops 5681184768 | bytes 29839360 | tf_op jit(solution)/shard_map/pallas_call | solution.py:60
  117.6 9.5 %all-to-all-start = ((f32[128,4,192]{2,1,0:T(4,128)}), f32[128,4,192]{2,1,0:T(4,128)S(1)}, u32[]{:S(2)}, u32[]{:S(2)}) async-start(f32[128,4,192]{2,1,0:T(4,128)} %broadcast_select_fusion), calls=%async_computation | async-start | bytes 1048576 | tf_op jit(solution)/shard_map/all_to_all | solution.py:127
  127.1 6.4 %fusion.5 = f32[512,128]{1,0:T(8,128)S(1)} fusion(bf16[512,16384]{1,0:T(8,128)(2,1)} %constant_dynamic-update-slice_fusion.act_ref.cot_ref, bf16[8192,64]{0,1:T(8,128)(2,1)} %param.21, bf16[8192,64]{0,1:T(8,128)(2,1)} %param.20), kind=kOutput, calls=%fused_computation.10 | convolution fusion | flops 1077936128 | bytes 10747904 | tf_op jit(solution)/shard_map/dot_general | solution.py:161
  133.5 2.3 %copy-done.1 = bf16[512,16384]{1,0:T(8,128)(2,1)S(1)} copy-done((bf16[512,16384]{1,0:T(8,128)(2,1)S(1)}, bf16[512,16384]{1,0:T(8,128)(2,1)}, u32[]{:S(2)}) %copy-start.1) | copy-done | bytes 16777240
  135.9 2.3 %fusion.3 = f32[512,64]{1,0:T(8,128)S(1)} fusion(bf16[8192,64]{0,1:T(8,128)(2,1)S(1)} %copy-done, bf16[512,16384]{1,0:T(8,128)(2,1)S(1)} %copy-done.1), kind=kOutput, calls=%fused_computation.8 | convolution fusion | flops 536870912 | bytes 9568256 | tf_op jit(solution)/shard_map/dot_general | solution.py:167
  142.2 8.0 %all-to-all-start.1 = ((f32[128,4,192]{2,1,0:T(4,128)}), f32[128,4,192]{2,1,0:T(4,128)S(1)}, u32[]{:S(2)}, u32[]{:S(2)}) async-start(f32[128,4,192]{2,1,0:T(4,128)} %broadcast_in_dim.58), calls=%async_computation.1 | async-start | bytes 1048576 | tf_op jit(solution)/shard_map/all_to_all | solution.py:132
  150.5 13.8 %all-to-all-done.1 = f32[128,4,192]{2,1,0:T(4,128)S(1)} async-done(((f32[128,4,192]{2,1,0:T(4,128)}), f32[128,4,192]{2,1,0:T(4,128)S(1)}, u32[]{:S(2)}, u32[]{:S(2)}) %all-to-all-start.1) | async-done | bytes 393248 | tf_op jit(solution)/shard_map/all_to_all | solution.py:132
  164.6 2.8 %convolution_convert_fusion = bf16[16,3,64,64]{3,2,1,0:T(8,128)(2,1)S(1)} fusion(f32[1,16,32,64]{3,2,0,1:T(8,128)S(1)} %bitcast.79, f32[1,16,32,64]{3,2,0,1:T(8,128)S(1)} %bitcast.76, f32[1,16,32,64]{3,2,0,1:T(8,128)S(1)} %bitcast.75, f32[1,16,32,64]{3,2,0,1:T(8,128)S(1)} %bitcast_select_fusion, f32[1,16,32,64]{3,2,0,1:T(8,128)S(1)} %bitcast.78, ...), kind=kOutput, calls=%fused_computation.17 | convolution fusion | flops 76087296 | bytes 1179648 | tf_op jit(solution)/shard_map/bdlr,bdls->dbrs/dot_general | solution.py:176
  170.9 3.9 %all-to-all-start.2 = ((f32[128,1,128]{2,1,0:T(1,128)}), f32[128,1,128]{2,1,0:T(1,128)S(1)}, u32[]{:S(2)}, u32[]{:S(2)}) async-start(f32[128,1,128]{2,1,0:T(1,128)} %reshape.90), calls=%async_computation.2 | async-start | bytes 131072 | tf_op jit(solution)/shard_map/all_to_all | solution.py:127
  175.4 9.2 %all-to-all-done.2 = f32[128,1,128]{2,1,0:T(1,128)S(1)} async-done(((f32[128,1,128]{2,1,0:T(1,128)}), f32[128,1,128]{2,1,0:T(1,128)S(1)}, u32[]{:S(2)}, u32[]{:S(2)}) %all-to-all-start.2) | async-done | bytes 65568 | tf_op jit(solution)/shard_map/all_to_all | solution.py:127
  (85 shorter events, 45.2 us)
Async XLA Ops:
  0.6 132.9 %copy-start = (bf16[8192,64]{0,1:T(8,128)(2,1)S(1)}, bf16[8192,64]{0,1:T(8,128)(2,1)}, u32[]{:S(2)}) copy-start(bf16[8192,64]{0,1:T(8,128)(2,1)} %param.22) | copy-start | bytes 3145732
  0.6 31.6 %copy-start.2 = (bf16[224,64]{0,1:T(8,128)(2,1)S(1)}, bf16[224,64]{0,1:T(8,128)(2,1)}, u32[]{:S(2)}) copy-start(bf16[224,64]{0,1:T(8,128)(2,1)} %param.23) | copy-start | bytes 86020
  0.7 32.3 %copy-start.3 = (bf16[224,64]{0,1:T(8,128)(2,1)S(1)}, bf16[224,64]{0,1:T(8,128)(2,1)}, u32[]{:S(2)}) copy-start(bf16[224,64]{0,1:T(8,128)(2,1)} %param.24) | copy-start | bytes 86020
  0.7 33.1 %copy-start.4 = (bf16[224,64]{0,1:T(8,128)(2,1)S(1)}, bf16[224,64]{0,1:T(8,128)(2,1)}, u32[]{:S(2)}) copy-start(bf16[224,64]{0,1:T(8,128)(2,1)} %param.25) | copy-start | bytes 86020
  5.1 41.9 %collective-permute-start = (bf16[32,16384]{1,0:T(8,128)(2,1)}, bf16[32,16384]{1,0:T(8,128)(2,1)}, u32[]{:S(2)}, u32[]{:S(2)}) collective-permute-start(bf16[32,16384]{1,0:T(8,128)(2,1)} %get-tuple-element.4), channel_id=1, source_target_pairs={{0,32},{8,40},{16,48},{24,56},{32,64},{40,72},{48,80},{56,88},{64,... | collective-permute-start | bytes 3145736 | tf_op jit(solution)/shard_map/ppermute | solution.py:94
  7.5 39.5 %collective-permute-start.1 = (bf16[32,16384]{1,0:T(8,128)(2,1)}, bf16[32,16384]{1,0:T(8,128)(2,1)S(1)}, u32[]{:S(2)}, u32[]{:S(2)}) collective-permute-start(bf16[32,16384]{1,0:T(8,128)(2,1)} %get-tuple-element.4), channel_id=1, source_target_pairs={{0,96},{8,104},{16,112},{24,120},{32,0},{40,8},{48,16},{56,24},{64... | collective-permute-start | bytes 3145736 | tf_op jit(solution)/shard_map/ppermute | solution.py:94
  9.7 37.4 %collective-permute-start.2 = (bf16[32,16384]{1,0:T(8,128)(2,1)}, bf16[32,16384]{1,0:T(8,128)(2,1)S(1)}, u32[]{:S(2)}, u32[]{:S(2)}) collective-permute-start(bf16[32,16384]{1,0:T(8,128)(2,1)} %get-tuple-element.4), channel_id=1, source_target_pairs={{0,16},{8,24},{16,0},{24,8},{32,48},{40,56},{48,32},{56,40},{64,80... | collective-permute-start | bytes 3145736 | tf_op jit(solution)/shard_map/ppermute | solution.py:94
  11.0 80.1 %collective-permute-start.8 = (bf16[32,16384]{1,0:T(8,128)(2,1)}, bf16[32,16384]{1,0:T(8,128)(2,1)}, u32[]{:S(2)}, u32[]{:S(2)}) collective-permute-start(bf16[32,16384]{1,0:T(8,128)(2,1)} %get-tuple-element.4), channel_id=1, source_target_pairs={{0,8},{8,0},{16,24},{24,16},{32,40},{40,32},{48,56},{56,48},{64,72... | collective-permute-start | bytes 3145736 | tf_op jit(solution)/shard_map/ppermute | solution.py:94
  48.6 44.8 %collective-permute-start.9 = (bf16[3,32,16384]{2,1,0:T(8,128)(2,1)S(1)}, bf16[3,32,16384]{2,1,0:T(8,128)(2,1)S(1)}, u32[]{:S(2)}, u32[]{:S(2)}) collective-permute-start(bf16[3,32,16384]{2,1,0:T(8,128)(2,1)S(1)} %pad_maximum_fusion), channel_id=1, source_target_pairs={{0,8},{8,0},{16,24},{24,16},{32,40},{40,32},{48,56},{56,48},{64,72... | collective-permute-start | bytes 9437192 | tf_op jit(solution)/shard_map/ppermute | solution.py:94
  48.7 24.4 %collective-permute-start.3 = (bf16[32,16384]{1,0:T(8,128)(2,1)S(1)}, bf16[32,16384]{1,0:T(8,128)(2,1)S(1)}, u32[]{:S(2)}, u32[]{:S(2)}) collective-permute-start(bf16[32,16384]{1,0:T(8,128)(2,1)S(1)} %collective-permute-done.1), channel_id=1, source_target_pairs={{0,96},{8,104},{16,112},{24,120},{32,0},{40,8},{48,16},{56,24},{64... | collective-permute-start | bytes 3145736 | tf_op jit(solution)/shard_map/ppermute | solution.py:94
  50.5 26.5 %collective-permute-start.4 = (bf16[32,16384]{1,0:T(8,128)(2,1)S(1)}, bf16[32,16384]{1,0:T(8,128)(2,1)S(1)}, u32[]{:S(2)}, u32[]{:S(2)}) collective-permute-start(bf16[32,16384]{1,0:T(8,128)(2,1)S(1)} %collective-permute-done.2), channel_id=1, source_target_pairs={{0,32},{8,40},{16,48},{24,56},{32,64},{40,72},{48,80},{56,88},{64,... | collective-permute-start | bytes 3145736 | tf_op jit(solution)/shard_map/ppermute | solution.py:94
  50.5 24.0 %collective-permute-start.5 = (bf16[32,16384]{1,0:T(8,128)(2,1)S(1)}, bf16[32,16384]{1,0:T(8,128)(2,1)S(1)}, u32[]{:S(2)}, u32[]{:S(2)}) collective-permute-start(bf16[32,16384]{1,0:T(8,128)(2,1)S(1)} %collective-permute-done.1), channel_id=1, source_target_pairs={{0,16},{8,24},{16,0},{24,8},{32,48},{40,56},{48,32},{56,40},{64,80... | collective-permute-start | bytes 3145736 | tf_op jit(solution)/shard_map/ppermute | solution.py:94
  73.1 12.3 %collective-permute-start.6 = (bf16[16,16384]{1,0:T(8,128)(2,1)S(1)}, bf16[16,16384]{1,0:T(8,128)(2,1)S(1)}, u32[]{:S(2)}, u32[]{:S(2)}) collective-permute-start(bf16[16,16384]{1,0:T(8,128)(2,1)S(1)} %slice.66), channel_id=1, source_target_pairs={{0,16},{8,24},{16,0},{24,8},{32,48},{40,56},{48,32},{56,40},{64,80... | collective-permute-start | bytes 1572872 | tf_op jit(solution)/shard_map/ppermute | solution.py:94
  74.6 12.0 %collective-permute-start.7 = (bf16[16,16384]{1,0:T(8,128)(2,1)S(1)}, bf16[16,16384]{1,0:T(8,128)(2,1)S(1)}, u32[]{:S(2)}, u32[]{:S(2)}) collective-permute-start(bf16[16,16384]{1,0:T(8,128)(2,1)S(1)} %slice.67), channel_id=1, source_target_pairs={{0,96},{8,104},{16,112},{24,120},{32,0},{40,8},{48,16},{56,24},{64... | collective-permute-start | bytes 1572872 | tf_op jit(solution)/shard_map/ppermute | solution.py:94
  77.4 19.2 %collective-permute-start.10 = (bf16[3,32,16384]{2,1,0:T(8,128)(2,1)S(1)}, bf16[3,32,16384]{2,1,0:T(8,128)(2,1)S(1)}, u32[]{:S(2)}, u32[]{:S(2)}) collective-permute-start(bf16[3,32,16384]{2,1,0:T(8,128)(2,1)S(1)} %pad_maximum_fusion.1), channel_id=1, source_target_pairs={{0,8},{8,0},{16,24},{24,16},{32,40},{40,32},{48,56},{56,48},{64,72... | collective-permute-start | bytes 9437192 | tf_op jit(solution)/shard_map/ppermute | solution.py:94
  86.6 13.1 %collective-permute-start.11 = (bf16[32,16384]{1,0:T(8,128)(2,1)S(1)}, bf16[32,16384]{1,0:T(8,128)(2,1)S(1)}, u32[]{:S(2)}, u32[]{:S(2)}) collective-permute-start(bf16[32,16384]{1,0:T(8,128)(2,1)S(1)} %pad_maximum_fusion.2), channel_id=1, source_target_pairs={{0,8},{8,0},{16,24},{24,16},{32,40},{40,32},{48,56},{56,48},{64,72... | collective-permute-start | bytes 3145736 | tf_op jit(solution)/shard_map/ppermute | solution.py:94
  117.6 23.5 %all-to-all-start = ((f32[128,4,192]{2,1,0:T(4,128)}), f32[128,4,192]{2,1,0:T(4,128)S(1)}, u32[]{:S(2)}, u32[]{:S(2)}) async-start(f32[128,4,192]{2,1,0:T(4,128)} %broadcast_select_fusion), calls=%async_computation | async-start | bytes 1048576 | tf_op jit(solution)/shard_map/all_to_all | solution.py:127
  127.1 8.8 %copy-start.1 = (bf16[512,16384]{1,0:T(8,128)(2,1)S(1)}, bf16[512,16384]{1,0:T(8,128)(2,1)}, u32[]{:S(2)}) copy-start(bf16[512,16384]{1,0:T(8,128)(2,1)} %constant_dynamic-update-slice_fusion.act_ref.cot_ref) | copy-start | bytes 50331652
  135.9 33.6 %copy-start.5 = (s32[32]{0:T(128)S(1)}, s32[32]{0:T(128)}, u32[]{:S(2)}) copy-start(s32[32]{0:T(128)} %param.27) | copy-start | bytes 388
  142.2 22.1 %all-to-all-start.1 = ((f32[128,4,192]{2,1,0:T(4,128)}), f32[128,4,192]{2,1,0:T(4,128)S(1)}, u32[]{:S(2)}, u32[]{:S(2)}) async-start(f32[128,4,192]{2,1,0:T(4,128)} %broadcast_in_dim.58), calls=%async_computation.1 | async-start | bytes 1048576 | tf_op jit(solution)/shard_map/all_to_all | solution.py:132
  170.9 13.8 %all-to-all-start.2 = ((f32[128,1,128]{2,1,0:T(1,128)}), f32[128,1,128]{2,1,0:T(1,128)S(1)}, u32[]{:S(2)}, u32[]{:S(2)}) async-start(f32[128,1,128]{2,1,0:T(1,128)} %reshape.90), calls=%async_computation.2 | async-start | bytes 131072 | tf_op jit(solution)/shard_map/all_to_all | solution.py:127

commit v10 on v9

--- a/solution.py
+++ b/solution.py
@@ -14,29 +14,28 @@
 LANE = 128
 
 
-def pad_to(x, cols):
-    return jnp.pad(x, ((0, 0), (0, cols - x.shape[1])))
-
-
-def layer_kernel(act_ref, cot_ref, wa_ref, wc_ref, go_ref, uo_ref, di_ref, side_ref, a_acc, c_acc):
+def layer_kernel(act_ref, cot_ref, gw_ref, uw_ref, dw_ref, go_ref, uo_ref, di_ref, side_ref, g_acc, u_acc, b_acc):
     k = pl.program_id(0)
 
     @pl.when(k == 0)
     def _():
-        a_acc[...] = jnp.zeros_like(a_acc)
-        c_acc[...] = jnp.zeros_like(c_acc)
+        g_acc[...] = jnp.zeros_like(g_acc)
+        u_acc[...] = jnp.zeros_like(u_acc)
+        b_acc[...] = jnp.zeros_like(b_acc)
 
     f32 = jnp.float32
-    a_acc[...] += jnp.dot(act_ref[...], wa_ref[...], preferred_element_type=f32)
-    c_acc[...] += jnp.dot(cot_ref[...], wc_ref[...], preferred_element_type=f32)
+    nt = (((1,), (1,)), ((), ()))
+    a = act_ref[...]
+    g_acc[...] += lax.dot_general(a, gw_ref[...], nt, preferred_element_type=f32)
+    u_acc[...] += lax.dot_general(a, uw_ref[...], nt, preferred_element_type=f32)
+    b_acc[...] += lax.dot_general(cot_ref[...], dw_ref[...], nt, preferred_element_type=f32)
 
     @pl.when(k == pl.num_programs(0) - 1)
     def _():
-        ff, r = go_ref.shape
-        fp = -(-ff // LANE) * LANE
-        g = a_acc[:, 0:ff]
-        u = a_acc[:, fp : fp + ff]
-        b = c_acc[:, 0:ff]
+        r = go_ref.shape[1]
+        g = g_acc[...]
+        u = u_acc[...]
+        b = b_acc[...]
         s = jax.nn.sigmoid(g)
         hidden = (g * s * u).astype(jnp.bfloat16)
         grad_up = (b * g * s).astype(jnp.bfloat16)
@@ -49,11 +48,7 @@
 def layer_call(both, gw, uw, dw, go, uo, di):
     rows, width = both.shape
     d = width // 2
-    ff = gw.shape[1]
-    r = go.shape[1]
-    fp = -(-ff // LANE) * LANE
-    wa = jnp.concatenate([pad_to(gw, fp), pad_to(uw, fp)], 1)
-    wc = pad_to(dw.T, fp)
+    ff, r = go.shape
     nk = d // KC
     f32 = jnp.float32
     full = lambda shape: pl.BlockSpec(shape, lambda k: (0, 0))
@@ -63,27 +58,25 @@
         in_specs=[
             pl.BlockSpec((rows, KC), lambda k: (0, k)),
             pl.BlockSpec((rows, KC), lambda k: (0, k + nk)),
-            pl.BlockSpec((KC, wa.shape[1]), lambda k: (k, 0)),
-            pl.BlockSpec((KC, wc.shape[1]), lambda k: (k, 0)),
+            pl.BlockSpec((ff, KC), lambda k: (0, k)),
+            pl.BlockSpec((ff, KC), lambda k: (0, k)),
+            pl.BlockSpec((ff, KC), lambda k: (0, k)),
             full((ff, r)),
             full((ff, r)),
             full((ff, r)),
         ],
         out_specs=full((rows, 3 * r)),
         out_shape=jax.ShapeDtypeStruct((rows, 3 * r), f32),
-        scratch_shapes=[
-            pltpu.VMEM((rows, wa.shape[1]), f32),
-            pltpu.VMEM((rows, wc.shape[1]), f32),
-        ],
+        scratch_shapes=[pltpu.VMEM((rows, ff), f32) for _ in range(3)],
         compiler_params=pltpu.CompilerParams(
             dimension_semantics=("arbitrary",), vmem_limit_bytes=62 * 1024 * 1024
         ),
         cost_estimate=pl.CostEstimate(
             flops=2 * rows * d * 3 * ff + 2 * rows * ff * 3 * r,
             transcendentals=rows * ff,
-            bytes_accessed=2 * (rows * width + d * (wa.shape[1] + wc.shape[1]) + 3 * ff * r) + 4 * rows * 3 * r,
+            bytes_accessed=2 * (rows * width + 3 * d * ff + 3 * ff * r) + 4 * rows * 3 * r,
         ),
-    )(both, both, wa, wc, go, uo, di)
+    )(both, both, gw.T, uw.T, dw, go, uo, di)
 
 
 def ring_perm(n, f):

time: 188 us -> 177 us (0.941)
  local copies, waits for them, and re-layouts: 54.7 us -> 31.1 us
  waiting for transfers between devices: 47.7 us -> 61.6 us
  other arithmetic: 18 us -> 10.6 us
  starting transfers between devices: 38.2 us -> 41.9 us
  matrix products: 13.4 us -> 16.7 us
    unnamed x35 -> x24, local copies, waits for them, and re-layouts: 42.3 us -> 23.5 us
    ppermute x12, waiting for transfers between devices: 23 us -> 37.7 us  [shared_gather(): pp = lambda v, p: lax.ppermute(v, 'dp', p)]
    concatenate x1 -> x0, other arithmetic: 7.39 us -> none  [layer_call(): wa = jnp.concatenate([pad_to(gw, fp), pad_to(uw, fp)], 1)]
    pad x1 -> x0, local copies, waits for them, and re-layouts: 4.84 us -> none  [pad_to(): return jnp.pad(x, ((0, 0), (0, cols - x.shape[1])))]
    dot_general x1, matrix products: 2.31 us -> 5.7 us  [body(): jnp.dot(both[:, d_model:], down_out_proj, preferred_element_type=f32)]
    ppermute x12, starting transfers between devices: 16.8 us -> 19.6 us  [shared_gather(): pp = lambda v, p: lax.ppermute(v, 'dp', p)]
  transfers between devices with their start and end apart: 15 -> 15, of which waited for: 7 -> 8; matrix products, arithmetic and copies ran while one was open for 35% -> 23% of each run, Pallas kernels for 0% -> 0%
where the time goes in v10:
time: 177 us
  waiting for transfers between devices  61.6 us (35%)
  starting transfers between devices  41.9 us (24%)
  local copies, waits for them, and re-layouts  31.1 us (18%)
  matrix products  16.7 us (9%)
  Pallas kernels  14 us (8%)
  other arithmetic  10.6 us (6%)
    ppermute x12, waiting for transfers between devices, shared_gather(): pp = lambda v, p: lax.ppermute(v, 'dp', p)  37.7 us
    unnamed x24, local copies, waits for them, and re-layouts  23.5 us
    ppermute x12, starting transfers between devices, shared_gather(): pp = lambda v, p: lax.ppermute(v, 'dp', p)  19.6 us
    pallas_call x1, Pallas kernels, layer_call(): pl.pallas_call(layer_kernel, grid=(nk,), in_specs=[pl.BlockSpec((rows, KC...  14 us
    all_to_all x1, waiting for transfers between devices, gather_rows(): got = lax.all_to_all(copies, ALL, 0, 0, tiled=False)  13.8 us
    all_to_all x2, starting transfers between devices, scatter_sum(): return jnp.sum(lax.all_to_all(blocks, ALL, 0, 0, tiled=False), axis=0)  13.4 us
    all_to_all x2, waiting for transfers between devices, scatter_sum(): return jnp.sum(lax.all_to_all(blocks, ALL, 0, 0, tiled=False), axis=0)  10.1 us
    all_to_all x1, starting transfers between devices, gather_rows(): got = lax.all_to_all(copies, ALL, 0, 0, tiled=False)  8.95 us
  transfers between devices with their start and end apart: 15, of which 8 were waited for; matrix products, arithmetic and copies ran while one was open for 23% of the time, Pallas kernels for 0%

profile of v10, /device:TPU:1, one launch (start us, length us, event | category | flops | bytes accessed | tf_op | source)
XLA Modules:
  0.0 176.7 jit_solution(11623160019237111636)
XLA Ops:
  2.5 2.6 %pad_maximum_fusion.3 = (bf16[32,16384]{1,0:T(8,128)(2,1)}, bf16[512,16384]{1,0:T(8,128)(2,1)}) fusion(bf16[32,8192]{1,0:T(8,128)(2,1)S(1)} %broadcast_multiply_fusion, bf16[32,8192]{1,0:T(8,128)(2,1)} %param.15), kind=kLoop, calls=%fused_computation.27 | loop fusion | flops 2097151 | bytes 3145728 | tf_op jit(solution)/shard_map/concatenate | solution.py:149
  5.1 2.5 %collective-permute-start = (bf16[32,16384]{1,0:T(8,128)(2,1)}, bf16[32,16384]{1,0:T(8,128)(2,1)}, u32[]{:S(2)}, u32[]{:S(2)}) collective-permute-start(bf16[32,16384]{1,0:T(8,128)(2,1)} %get-tuple-element.4), channel_id=1, source_target_pairs={{0,32},{8,40},{16,48},{24,56},{32,64},{40,72},{48,80},{56,88},{64,... | collective-permute-start | bytes 3145736 | tf_op jit(solution)/shard_map/ppermute | solution.py:87
  7.6 2.1 %collective-permute-start.1 = (bf16[32,16384]{1,0:T(8,128)(2,1)}, bf16[32,16384]{1,0:T(8,128)(2,1)S(1)}, u32[]{:S(2)}, u32[]{:S(2)}) collective-permute-start(bf16[32,16384]{1,0:T(8,128)(2,1)} %get-tuple-element.4), channel_id=1, source_target_pairs={{0,96},{8,104},{16,112},{24,120},{32,0},{40,8},{48,16},{56,24},{64... | collective-permute-start | bytes 3145736 | tf_op jit(solution)/shard_map/ppermute | solution.py:87
  18.4 14.5 %collective-permute-done = bf16[32,16384]{1,0:T(8,128)(2,1)} collective-permute-done((bf16[32,16384]{1,0:T(8,128)(2,1)}, bf16[32,16384]{1,0:T(8,128)(2,1)}, u32[]{:S(2)}, u32[]{:S(2)}) %collective-permute-start) | collective-permute-done | bytes 1048608 | tf_op jit(solution)/shard_map/ppermute | solution.py:87
  33.7 1.6 pad_maximum_fusion
  35.3 1.8 %collective-permute-start.9 = (bf16[3,32,16384]{2,1,0:T(8,128)(2,1)S(1)}, bf16[3,32,16384]{2,1,0:T(8,128)(2,1)S(1)}, u32[]{:S(2)}, u32[]{:S(2)}) collective-permute-start(bf16[3,32,16384]{2,1,0:T(8,128)(2,1)S(1)} %pad_maximum_fusion), channel_id=1, source_target_pairs={{0,8},{8,0},{16,24},{24,16},{32,40},{40,32},{48,56},{56,48},{64,72... | collective-permute-start | bytes 9437192 | tf_op jit(solution)/shard_map/ppermute | solution.py:87
  39.9 2.3 %constant_dynamic-update-slice_fusion.9 = bf16[512,16384]{1,0:T(8,128)(2,1)} fusion(bf16[512,16384]{1,0:T(8,128)(2,1)} %get-tuple-element.5, bf16[32,16384]{1,0:T(8,128)(2,1)} %collective-permute-done), kind=kLoop, calls=%fused_computation.54 | loop fusion | bytes 2097152
  44.3 17.4 %collective-permute-done.3 = bf16[32,16384]{1,0:T(8,128)(2,1)S(1)} collective-permute-done((bf16[32,16384]{1,0:T(8,128)(2,1)S(1)}, bf16[32,16384]{1,0:T(8,128)(2,1)S(1)}, u32[]{:S(2)}, u32[]{:S(2)}) %collective-permute-start.3) | collective-permute-done | bytes 1048608 | tf_op jit(solution)/shard_map/ppermute | solution.py:87
  63.2 2.7 %collective-permute-start.7 = (bf16[16,16384]{1,0:T(8,128)(2,1)S(1)}, bf16[16,16384]{1,0:T(8,128)(2,1)S(1)}, u32[]{:S(2)}, u32[]{:S(2)}) collective-permute-start(bf16[16,16384]{1,0:T(8,128)(2,1)S(1)} %slice.67), channel_id=1, source_target_pairs={{0,96},{8,104},{16,112},{24,120},{32,0},{40,8},{48,16},{56,24},{64... | collective-permute-start | bytes 1572872 | tf_op jit(solution)/shard_map/ppermute | solution.py:87
  66.3 1.6 collective-permute-start.10
  71.0 3.4 %collective-permute-done.6 = bf16[16,16384]{1,0:T(8,128)(2,1)S(1)} collective-permute-done((bf16[16,16384]{1,0:T(8,128)(2,1)S(1)}, bf16[16,16384]{1,0:T(8,128)(2,1)S(1)}, u32[]{:S(2)}, u32[]{:S(2)}) %collective-permute-start.6) | collective-permute-done | bytes 524320 | tf_op jit(solution)/shard_map/ppermute | solution.py:87
  74.4 1.6 collective-permute-done.7
  76.1 2.2 %collective-permute-start.11 = (bf16[32,16384]{1,0:T(8,128)(2,1)S(1)}, bf16[32,16384]{1,0:T(8,128)(2,1)S(1)}, u32[]{:S(2)}, u32[]{:S(2)}) collective-permute-start(bf16[32,16384]{1,0:T(8,128)(2,1)S(1)} %pad_maximum_fusion.2), channel_id=1, source_target_pairs={{0,8},{8,0},{16,24},{24,16},{32,40},{40,32},{48,56},{56,48},{64,72... | collective-permute-start | bytes 3145736 | tf_op jit(solution)/shard_map/ppermute | solution.py:87
  79.9 2.3 %constant_dynamic-update-slice_fusion.1 = bf16[512,16384]{1,0:T(8,128)(2,1)} fusion(bf16[512,16384]{1,0:T(8,128)(2,1)} %constant_dynamic-update-slice_fusion.2, bf16[32,16384]{1,0:T(8,128)(2,1)} %collective-permute-done.8), kind=kLoop, calls=%fused_computation.46 | loop fusion | bytes 2097152
  89.7 14.0 %shard_map.149 = f32[512,192]{1,0:T(8,128)} custom-call(bf16[512,16384]{1,0:T(8,128)(2,1)} %constant_dynamic-update-slice_fusion.act_ref.cot_ref, bf16[512,16384]{1,0:T(8,128)(2,1)} %constant_dynamic-update-slice_fusion.act_ref.cot_ref, bf16[224,8192]{1,0:T(8,128)(2,1)} %bitcast.74, bf16[224,8192]{1,0:T(8,128)(2,1)} %bitcast.75, bf16[224,8192]{1,0:T(8,128)(2,1)} %dw_ref.1, ...), custom_call_target="tpu_custom_call" | custom-call | flops 5681184768 | bytes 28266496 | tf_op jit(solution)/shard_map/pallas_call | solution.py:55
  103.7 1.6 gather_fusion.1
  106.5 9.5 %all-to-all-start = ((f32[128,4,192]{2,1,0:T(4,128)}), f32[128,4,192]{2,1,0:T(4,128)S(1)}, u32[]{:S(2)}, u32[]{:S(2)}) async-start(f32[128,4,192]{2,1,0:T(4,128)} %broadcast_select_fusion), calls=%async_computation | async-start | bytes 1048576 | tf_op jit(solution)/shard_map/all_to_all | solution.py:120
  116.0 6.2 %fusion.2 = f32[512,128]{1,0:T(8,128)S(1)} fusion(bf16[512,16384]{1,0:T(8,128)(2,1)} %constant_dynamic-update-slice_fusion.act_ref.cot_ref, bf16[8192,64]{0,1:T(8,128)(2,1)} %param.21, bf16[8192,64]{0,1:T(8,128)(2,1)} %param.20), kind=kOutput, calls=%fused_computation.5 | convolution fusion | flops 1077936128 | bytes 10747904 | tf_op jit(solution)/shard_map/dot_general | solution.py:154
  122.3 5.7 %fusion = f32[512,64]{1,0:T(8,128)S(1)} fusion(bf16[8192,64]{0,1:T(8,128)(2,1)S(1)} %copy-done, bf16[512,16384]{1,0:T(8,128)(2,1)} %constant_dynamic-update-slice_fusion.act_ref.cot_ref), kind=kOutput, calls=%fused_computation.3 | convolution fusion | flops 536870912 | bytes 9568256 | tf_op jit(solution)/shard_map/dot_general | solution.py:160
  131.1 8.9 %all-to-all-start.1 = ((f32[128,4,192]{2,1,0:T(4,128)}), f32[128,4,192]{2,1,0:T(4,128)S(1)}, u32[]{:S(2)}, u32[]{:S(2)}) async-start(f32[128,4,192]{2,1,0:T(4,128)} %broadcast_in_dim.58), calls=%async_computation.1 | async-start | bytes 1048576 | tf_op jit(solution)/shard_map/all_to_all | solution.py:125
  140.3 13.8 %all-to-all-done.1 = f32[128,4,192]{2,1,0:T(4,128)S(1)} async-done(((f32[128,4,192]{2,1,0:T(4,128)}), f32[128,4,192]{2,1,0:T(4,128)S(1)}, u32[]{:S(2)}, u32[]{:S(2)}) %all-to-all-start.1) | async-done | bytes 393248 | tf_op jit(solution)/shard_map/all_to_all | solution.py:125
  154.4 2.8 %convolution_convert_fusion = bf16[16,3,64,64]{3,2,1,0:T(8,128)(2,1)S(1)} fusion(f32[1,16,32,64]{3,2,0,1:T(8,128)S(1)} %bitcast.81, f32[1,16,32,64]{3,2,0,1:T(8,128)S(1)} %bitcast.78, f32[1,16,32,64]{3,2,0,1:T(8,128)S(1)} %bitcast.77, f32[1,16,32,64]{3,2,0,1:T(8,128)S(1)} %bitcast_select_fusion, f32[1,16,32,64]{3,2,0,1:T(8,128)S(1)} %bitcast.80, ...), kind=kOutput, calls=%fused_computation.12 | convolution fusion | flops 76087296 | bytes 1179648 | tf_op jit(solution)/shard_map/bdlr,bdls->dbrs/dot_general | solution.py:169
  160.7 3.9 %all-to-all-start.2 = ((f32[128,1,128]{2,1,0:T(1,128)}), f32[128,1,128]{2,1,0:T(1,128)S(1)}, u32[]{:S(2)}, u32[]{:S(2)}) async-start(f32[128,1,128]{2,1,0:T(1,128)} %reshape.90), calls=%async_computation.2 | async-start | bytes 131072 | tf_op jit(solution)/shard_map/all_to_all | solution.py:120
  165.2 9.2 %all-to-all-done.2 = f32[128,1,128]{2,1,0:T(1,128)S(1)} async-done(((f32[128,1,128]{2,1,0:T(1,128)}), f32[128,1,128]{2,1,0:T(1,128)S(1)}, u32[]{:S(2)}, u32[]{:S(2)}) %all-to-all-start.2) | async-done | bytes 65568 | tf_op jit(solution)/shard_map/all_to_all | solution.py:120
  (72 shorter events, 41.6 us)
Async XLA Ops:
  0.6 121.6 %copy-start = (bf16[8192,64]{0,1:T(8,128)(2,1)S(1)}, bf16[8192,64]{0,1:T(8,128)(2,1)}, u32[]{:S(2)}) copy-start(bf16[8192,64]{0,1:T(8,128)(2,1)} %param.22) | copy-start | bytes 3145732
  5.1 27.8 %collective-permute-start = (bf16[32,16384]{1,0:T(8,128)(2,1)}, bf16[32,16384]{1,0:T(8,128)(2,1)}, u32[]{:S(2)}, u32[]{:S(2)}) collective-permute-start(bf16[32,16384]{1,0:T(8,128)(2,1)} %get-tuple-element.4), channel_id=1, source_target_pairs={{0,32},{8,40},{16,48},{24,56},{32,64},{40,72},{48,80},{56,88},{64,... | collective-permute-start | bytes 3145736 | tf_op jit(solution)/shard_map/ppermute | solution.py:87
  7.6 25.3 %collective-permute-start.1 = (bf16[32,16384]{1,0:T(8,128)(2,1)}, bf16[32,16384]{1,0:T(8,128)(2,1)S(1)}, u32[]{:S(2)}, u32[]{:S(2)}) collective-permute-start(bf16[32,16384]{1,0:T(8,128)(2,1)} %get-tuple-element.4), channel_id=1, source_target_pairs={{0,96},{8,104},{16,112},{24,120},{32,0},{40,8},{48,16},{56,24},{64... | collective-permute-start | bytes 3145736 | tf_op jit(solution)/shard_map/ppermute | solution.py:87
  9.7 24.0 %collective-permute-start.2 = (bf16[32,16384]{1,0:T(8,128)(2,1)}, bf16[32,16384]{1,0:T(8,128)(2,1)S(1)}, u32[]{:S(2)}, u32[]{:S(2)}) collective-permute-start(bf16[32,16384]{1,0:T(8,128)(2,1)} %get-tuple-element.4), channel_id=1, source_target_pairs={{0,16},{8,24},{16,0},{24,8},{32,48},{40,56},{48,32},{56,40},{64,80... | collective-permute-start | bytes 3145736 | tf_op jit(solution)/shard_map/ppermute | solution.py:87
  11.0 69.0 %collective-permute-start.8 = (bf16[32,16384]{1,0:T(8,128)(2,1)}, bf16[32,16384]{1,0:T(8,128)(2,1)}, u32[]{:S(2)}, u32[]{:S(2)}) collective-permute-start(bf16[32,16384]{1,0:T(8,128)(2,1)} %get-tuple-element.4), channel_id=1, source_target_pairs={{0,8},{8,0},{16,24},{24,16},{32,40},{40,32},{48,56},{56,48},{64,72... | collective-permute-start | bytes 3145736 | tf_op jit(solution)/shard_map/ppermute | solution.py:87
  35.3 47.0 %collective-permute-start.9 = (bf16[3,32,16384]{2,1,0:T(8,128)(2,1)S(1)}, bf16[3,32,16384]{2,1,0:T(8,128)(2,1)S(1)}, u32[]{:S(2)}, u32[]{:S(2)}) collective-permute-start(bf16[3,32,16384]{2,1,0:T(8,128)(2,1)S(1)} %pad_maximum_fusion), channel_id=1, source_target_pairs={{0,8},{8,0},{16,24},{24,16},{32,40},{40,32},{48,56},{56,48},{64,72... | collective-permute-start | bytes 9437192 | tf_op jit(solution)/shard_map/ppermute | solution.py:87
  37.1 24.6 %collective-permute-start.3 = (bf16[32,16384]{1,0:T(8,128)(2,1)S(1)}, bf16[32,16384]{1,0:T(8,128)(2,1)S(1)}, u32[]{:S(2)}, u32[]{:S(2)}) collective-permute-start(bf16[32,16384]{1,0:T(8,128)(2,1)S(1)} %collective-permute-done.1), channel_id=1, source_target_pairs={{0,96},{8,104},{16,112},{24,120},{32,0},{40,8},{48,16},{56,24},{64... | collective-permute-start | bytes 3145736 | tf_op jit(solution)/shard_map/ppermute | solution.py:87
  38.6 27.4 %collective-permute-start.4 = (bf16[32,16384]{1,0:T(8,128)(2,1)S(1)}, bf16[32,16384]{1,0:T(8,128)(2,1)S(1)}, u32[]{:S(2)}, u32[]{:S(2)}) collective-permute-start(bf16[32,16384]{1,0:T(8,128)(2,1)S(1)} %collective-permute-done.2), channel_id=1, source_target_pairs={{0,32},{8,40},{16,48},{24,56},{32,64},{40,72},{48,80},{56,88},{64,... | collective-permute-start | bytes 3145736 | tf_op jit(solution)/shard_map/ppermute | solution.py:87
  38.6 24.6 %collective-permute-start.5 = (bf16[32,16384]{1,0:T(8,128)(2,1)S(1)}, bf16[32,16384]{1,0:T(8,128)(2,1)S(1)}, u32[]{:S(2)}, u32[]{:S(2)}) collective-permute-start(bf16[32,16384]{1,0:T(8,128)(2,1)S(1)} %collective-permute-done.1), channel_id=1, source_target_pairs={{0,16},{8,24},{16,0},{24,8},{32,48},{40,56},{48,32},{56,40},{64,80... | collective-permute-start | bytes 3145736 | tf_op jit(solution)/shard_map/ppermute | solution.py:87
  61.8 12.6 %collective-permute-start.6 = (bf16[16,16384]{1,0:T(8,128)(2,1)S(1)}, bf16[16,16384]{1,0:T(8,128)(2,1)S(1)}, u32[]{:S(2)}, u32[]{:S(2)}) collective-permute-start(bf16[16,16384]{1,0:T(8,128)(2,1)S(1)} %slice.66), channel_id=1, source_target_pairs={{0,16},{8,24},{16,0},{24,8},{32,48},{40,56},{48,32},{56,40},{64,80... | collective-permute-start | bytes 1572872 | tf_op jit(solution)/shard_map/ppermute | solution.py:87
  63.2 12.8 %collective-permute-start.7 = (bf16[16,16384]{1,0:T(8,128)(2,1)S(1)}, bf16[16,16384]{1,0:T(8,128)(2,1)S(1)}, u32[]{:S(2)}, u32[]{:S(2)}) collective-permute-start(bf16[16,16384]{1,0:T(8,128)(2,1)S(1)} %slice.67), channel_id=1, source_target_pairs={{0,96},{8,104},{16,112},{24,120},{32,0},{40,8},{48,16},{56,24},{64... | collective-permute-start | bytes 1572872 | tf_op jit(solution)/shard_map/ppermute | solution.py:87
  66.3 19.1 %collective-permute-start.10 = (bf16[3,32,16384]{2,1,0:T(8,128)(2,1)S(1)}, bf16[3,32,16384]{2,1,0:T(8,128)(2,1)S(1)}, u32[]{:S(2)}, u32[]{:S(2)}) collective-permute-start(bf16[3,32,16384]{2,1,0:T(8,128)(2,1)S(1)} %pad_maximum_fusion.1), channel_id=1, source_target_pairs={{0,8},{8,0},{16,24},{24,16},{32,40},{40,32},{48,56},{56,48},{64,72... | collective-permute-start | bytes 9437192 | tf_op jit(solution)/shard_map/ppermute | solution.py:87
  76.1 12.6 %collective-permute-start.11 = (bf16[32,16384]{1,0:T(8,128)(2,1)S(1)}, bf16[32,16384]{1,0:T(8,128)(2,1)S(1)}, u32[]{:S(2)}, u32[]{:S(2)}) collective-permute-start(bf16[32,16384]{1,0:T(8,128)(2,1)S(1)} %pad_maximum_fusion.2), channel_id=1, source_target_pairs={{0,8},{8,0},{16,24},{24,16},{32,40},{40,32},{48,56},{56,48},{64,72... | collective-permute-start | bytes 3145736 | tf_op jit(solution)/shard_map/ppermute | solution.py:87
  106.5 23.5 %all-to-all-start = ((f32[128,4,192]{2,1,0:T(4,128)}), f32[128,4,192]{2,1,0:T(4,128)S(1)}, u32[]{:S(2)}, u32[]{:S(2)}) async-start(f32[128,4,192]{2,1,0:T(4,128)} %broadcast_select_fusion), calls=%async_computation | async-start | bytes 1048576 | tf_op jit(solution)/shard_map/all_to_all | solution.py:120
  122.3 37.0 %copy-start.1 = (s32[32]{0:T(128)S(1)}, s32[32]{0:T(128)}, u32[]{:S(2)}) copy-start(s32[32]{0:T(128)} %param.27) | copy-start | bytes 388
  131.1 23.0 %all-to-all-start.1 = ((f32[128,4,192]{2,1,0:T(4,128)}), f32[128,4,192]{2,1,0:T(4,128)S(1)}, u32[]{:S(2)}, u32[]{:S(2)}) async-start(f32[128,4,192]{2,1,0:T(4,128)} %broadcast_in_dim.58), calls=%async_computation.1 | async-start | bytes 1048576 | tf_op jit(solution)/shard_map/all_to_all | solution.py:125
  160.7 13.8 %all-to-all-start.2 = ((f32[128,1,128]{2,1,0:T(1,128)}), f32[128,1,128]{2,1,0:T(1,128)S(1)}, u32[]{:S(2)}, u32[]{:S(2)}) async-start(f32[128,1,128]{2,1,0:T(1,128)} %reshape.90), calls=%async_computation.2 | async-start | bytes 131072 | tf_op jit(solution)/shard_map/all_to_all | solution.py:120

commit v11 on v10

--- a/solution.py
+++ b/solution.py
@@ -89,7 +89,6 @@
     zm = ring_perm(n, lambda i: i - 4)
     yy = ring_perm(n, lambda i: i ^ 2)
     cc = ring_perm(n, lambda i: i ^ 1)
-    half = x.shape[0] // 2
     from_zm = pp(x, zp)
     from_zp = pp(x, zm)
     from_y = pp(x, yy)
@@ -98,7 +97,15 @@
     b_zm_y = pp(from_y, zp)
     b_zp_y = pp(from_zp, yy)
     o_b = pp(jnp.stack([from_zm, from_zp, from_y]), cc)
-    c_z2_y = jnp.concatenate([pp(b_z2[:half], yy), pp(b_zp_y[half:], zm)], axis=0)
+    third = (x.shape[1] // 3) // 128 * 128
+    c_z2_y = jnp.concatenate(
+        [
+            pp(b_z2[:, :third], yy),
+            pp(b_zp_y[:, third : 2 * third], zm),
+            pp(b_zm_y[:, 2 * third :], zp),
+        ],
+        axis=1,
+    )
     o_c = pp(jnp.stack([b_z2, b_zm_y, b_zp_y]), cc)
     o_d = pp(c_z2_y, cc)
     slots = [x, from_zm, from_zp, from_y, b_z2, b_zm_y, b_zp_y, c_z2_y,

time: 177 us -> 173 us (0.977)
  starting transfers between devices: 41.9 us -> 39.3 us
  waiting for transfers between devices: 61.6 us -> 59.4 us
    all_to_all x2, starting transfers between devices: 13.4 us -> 10.3 us  [scatter_sum(): return jnp.sum(lax.all_to_all(blocks, ALL, 0, 0, tiled=False), axis=0)]
    ppermute x12 -> x13, waiting for transfers between devices: 37.7 us -> 35.6 us  [shared_gather(): pp = lambda v, p: lax.ppermute(v, 'dp', p)]
    unnamed x24 -> x25, local copies, waits for them, and re-layouts: 23.5 us -> 24.1 us
    ppermute x12 -> x13, starting transfers between devices: 19.6 us -> 20.1 us  [shared_gather(): pp = lambda v, p: lax.ppermute(v, 'dp', p)]
  transfers between devices with their start and end apart: 15 -> 16, of which waited for: 8 -> 8; matrix products, arithmetic and copies ran while one was open for 23% -> 24% of each run, Pallas kernels for 0% -> 0%
where the time goes in v11:
time: 173 us
  waiting for transfers between devices  59.4 us (34%)
  starting transfers between devices  39.3 us (23%)
  local copies, waits for them, and re-layouts  31.7 us (18%)
  matrix products  16.7 us (10%)
  Pallas kernels  14 us (8%)
  other arithmetic  10.6 us (6%)
    ppermute x13, waiting for transfers between devices, shared_gather(): pp = lambda v, p: lax.ppermute(v, 'dp', p)  35.6 us
    unnamed x25, local copies, waits for them, and re-layouts  24.1 us
    ppermute x13, starting transfers between devices, shared_gather(): pp = lambda v, p: lax.ppermute(v, 'dp', p)  20.1 us
    pallas_call x1, Pallas kernels, layer_call(): pl.pallas_call(layer_kernel, grid=(nk,), in_specs=[pl.BlockSpec((rows, KC...  14 us
    all_to_all x1, waiting for transfers between devices, gather_rows(): got = lax.all_to_all(copies, ALL, 0, 0, tiled=False)  13.8 us
    all_to_all x2, starting transfers between devices, scatter_sum(): return jnp.sum(lax.all_to_all(blocks, ALL, 0, 0, tiled=False), axis=0)  10.3 us
    all_to_all x2, waiting for transfers between devices, scatter_sum(): return jnp.sum(lax.all_to_all(blocks, ALL, 0, 0, tiled=False), axis=0)  10.1 us
    all_to_all x1, starting transfers between devices, gather_rows(): got = lax.all_to_all(copies, ALL, 0, 0, tiled=False)  8.94 us
  transfers between devices with their start and end apart: 16, of which 8 were waited for; matrix products, arithmetic and copies ran while one was open for 24% of the time, Pallas kernels for 0%

profile of v11, /device:TPU:1, one launch (start us, length us, event | category | flops | bytes accessed | tf_op | source)
XLA Modules:
  0.0 172.6 jit_solution(17008266510734288218)
XLA Ops:
  2.5 2.5 %pad_maximum_fusion.3 = (bf16[32,16384]{1,0:T(8,128)(2,1)}, bf16[512,16384]{1,0:T(8,128)(2,1)}) fusion(bf16[32,8192]{1,0:T(8,128)(2,1)S(1)} %broadcast_multiply_fusion, bf16[32,8192]{1,0:T(8,128)(2,1)} %param.15), kind=kLoop, calls=%fused_computation.27 | loop fusion | flops 2097151 | bytes 3145728 | tf_op jit(solution)/shard_map/concatenate | solution.py:156
  5.1 2.5 %collective-permute-start = (bf16[32,16384]{1,0:T(8,128)(2,1)}, bf16[32,16384]{1,0:T(8,128)(2,1)}, u32[]{:S(2)}, u32[]{:S(2)}) collective-permute-start(bf16[32,16384]{1,0:T(8,128)(2,1)} %get-tuple-element.4), channel_id=1, source_target_pairs={{0,32},{8,40},{16,48},{24,56},{32,64},{40,72},{48,80},{56,88},{64,... | collective-permute-start | bytes 3145736 | tf_op jit(solution)/shard_map/ppermute | solution.py:87
  7.5 2.1 %collective-permute-start.1 = (bf16[32,16384]{1,0:T(8,128)(2,1)}, bf16[32,16384]{1,0:T(8,128)(2,1)S(1)}, u32[]{:S(2)}, u32[]{:S(2)}) collective-permute-start(bf16[32,16384]{1,0:T(8,128)(2,1)} %get-tuple-element.4), channel_id=1, source_target_pairs={{0,96},{8,104},{16,112},{24,120},{32,0},{40,8},{48,16},{56,24},{64... | collective-permute-start | bytes 3145736 | tf_op jit(solution)/shard_map/ppermute | solution.py:87
  15.1 1.5 copy.21.di_ref
  18.3 14.5 %collective-permute-done = bf16[32,16384]{1,0:T(8,128)(2,1)} collective-permute-done((bf16[32,16384]{1,0:T(8,128)(2,1)}, bf16[32,16384]{1,0:T(8,128)(2,1)}, u32[]{:S(2)}, u32[]{:S(2)}) %collective-permute-start) | collective-permute-done | bytes 1048608 | tf_op jit(solution)/shard_map/ppermute | solution.py:87
  33.7 1.6 pad_maximum_fusion
  35.3 1.8 %collective-permute-start.10 = (bf16[3,32,16384]{2,1,0:T(8,128)(2,1)S(1)}, bf16[3,32,16384]{2,1,0:T(8,128)(2,1)S(1)}, u32[]{:S(2)}, u32[]{:S(2)}) collective-permute-start(bf16[3,32,16384]{2,1,0:T(8,128)(2,1)S(1)} %pad_maximum_fusion), channel_id=1, source_target_pairs={{0,8},{8,0},{16,24},{24,16},{32,40},{40,32},{48,56},{56,48},{64,72... | collective-permute-start | bytes 9437192 | tf_op jit(solution)/shard_map/ppermute | solution.py:87
  39.9 2.3 %constant_dynamic-update-slice_fusion.8 = bf16[512,16384]{1,0:T(8,128)(2,1)} fusion(bf16[512,16384]{1,0:T(8,128)(2,1)} %get-tuple-element.5, bf16[32,16384]{1,0:T(8,128)(2,1)} %collective-permute-done), kind=kLoop, calls=%fused_computation.53 | loop fusion | bytes 2097152
  44.3 17.4 %collective-permute-done.3 = bf16[32,16384]{1,0:T(8,128)(2,1)S(1)} collective-permute-done((bf16[32,16384]{1,0:T(8,128)(2,1)S(1)}, bf16[32,16384]{1,0:T(8,128)(2,1)S(1)}, u32[]{:S(2)}, u32[]{:S(2)}) %collective-permute-start.3) | collective-permute-done | bytes 1048608 | tf_op jit(solution)/shard_map/ppermute | solution.py:87
  63.2 2.7 %collective-permute-start.7 = (bf16[32,5376]{1,0:T(8,128)(2,1)S(1)}, bf16[32,5376]{1,0:T(8,128)(2,1)S(1)}, u32[]{:S(2)}, u32[]{:S(2)}) collective-permute-start(bf16[32,5376]{1,0:T(8,128)(2,1)S(1)} %slice.71), channel_id=1, source_target_pairs={{0,96},{8,104},{16,112},{24,120},{32,0},{40,8},{48,16},{56,24},{64... | collective-permute-start | bytes 1032200 | tf_op jit(solution)/shard_map/ppermute | solution.py:87
  70.5 1.8 %collective-permute-start.11 = (bf16[3,32,16384]{2,1,0:T(8,128)(2,1)S(1)}, bf16[3,32,16384]{2,1,0:T(8,128)(2,1)S(1)}, u32[]{:S(2)}, u32[]{:S(2)}) collective-permute-start(bf16[3,32,16384]{2,1,0:T(8,128)(2,1)S(1)} %pad_maximum_fusion.1), channel_id=1, source_target_pairs={{0,8},{8,0},{16,24},{24,16},{32,40},{40,32},{48,56},{56,48},{64,72... | collective-permute-start | bytes 9437192 | tf_op jit(solution)/shard_map/ppermute | solution.py:87
  73.9 1.8 %collective-permute-done.8 = bf16[32,5632]{1,0:T(8,128)(2,1)S(1)} collective-permute-done((bf16[32,5632]{1,0:T(8,128)(2,1)S(1)}, bf16[32,5632]{1,0:T(8,128)(2,1)S(1)}, u32[]{:S(2)}, u32[]{:S(2)}) %collective-permute-start.8) | collective-permute-done | bytes 360480 | tf_op jit(solution)/shard_map/ppermute | solution.py:87
  75.8 2.4 %collective-permute-start.12 = (bf16[32,16384]{1,0:T(8,128)(2,1)S(1)}, bf16[32,16384]{1,0:T(8,128)(2,1)S(1)}, u32[]{:S(2)}, u32[]{:S(2)}) collective-permute-start(bf16[32,16384]{1,0:T(8,128)(2,1)S(1)} %pad_maximum_fusion.2), channel_id=1, source_target_pairs={{0,8},{8,0},{16,24},{24,16},{32,40},{40,32},{48,56},{56,48},{64,72... | collective-permute-start | bytes 3145736 | tf_op jit(solution)/shard_map/ppermute | solution.py:87
  79.0 2.3 %constant_dynamic-update-slice_fusion.1 = bf16[512,16384]{1,0:T(8,128)(2,1)} fusion(bf16[512,16384]{1,0:T(8,128)(2,1)} %constant_dynamic-update-slice_fusion.10, bf16[32,16384]{1,0:T(8,128)(2,1)} %collective-permute-done.9), kind=kLoop, calls=%fused_computation.46 | loop fusion | bytes 2097152
  88.7 14.0 %shard_map.149 = f32[512,192]{1,0:T(8,128)} custom-call(bf16[512,16384]{1,0:T(8,128)(2,1)} %constant_dynamic-update-slice_fusion.act_ref.cot_ref, bf16[512,16384]{1,0:T(8,128)(2,1)} %constant_dynamic-update-slice_fusion.act_ref.cot_ref, bf16[224,8192]{1,0:T(8,128)(2,1)} %bitcast.74, bf16[224,8192]{1,0:T(8,128)(2,1)} %bitcast.75, bf16[224,8192]{1,0:T(8,128)(2,1)} %dw_ref.1, ...), custom_call_target="tpu_custom_call" | custom-call | flops 5681184768 | bytes 28266496 | tf_op jit(solution)/shard_map/pallas_call | solution.py:55
  102.8 1.6 gather_fusion.1
  105.6 6.4 %all-to-all-start = ((f32[128,4,192]{2,1,0:T(4,128)}), f32[128,4,192]{2,1,0:T(4,128)S(1)}, u32[]{:S(2)}, u32[]{:S(2)}) async-start(f32[128,4,192]{2,1,0:T(4,128)} %broadcast_select_fusion), calls=%async_computation | async-start | bytes 1048576 | tf_op jit(solution)/shard_map/all_to_all | solution.py:127
  112.0 6.2 %fusion.2 = f32[512,128]{1,0:T(8,128)S(1)} fusion(bf16[512,16384]{1,0:T(8,128)(2,1)} %constant_dynamic-update-slice_fusion.act_ref.cot_ref, bf16[8192,64]{0,1:T(8,128)(2,1)} %param.21, bf16[8192,64]{0,1:T(8,128)(2,1)} %param.20), kind=kOutput, calls=%fused_computation.5 | convolution fusion | flops 1077936128 | bytes 10747904 | tf_op jit(solution)/shard_map/dot_general | solution.py:161
  118.2 5.7 %fusion = f32[512,64]{1,0:T(8,128)S(1)} fusion(bf16[8192,64]{0,1:T(8,128)(2,1)S(1)} %copy-done, bf16[512,16384]{1,0:T(8,128)(2,1)} %constant_dynamic-update-slice_fusion.act_ref.cot_ref), kind=kOutput, calls=%fused_computation.3 | convolution fusion | flops 536870912 | bytes 9568256 | tf_op jit(solution)/shard_map/dot_general | solution.py:167
  127.0 8.9 %all-to-all-start.1 = ((f32[128,4,192]{2,1,0:T(4,128)}), f32[128,4,192]{2,1,0:T(4,128)S(1)}, u32[]{:S(2)}, u32[]{:S(2)}) async-start(f32[128,4,192]{2,1,0:T(4,128)} %broadcast_in_dim.58), calls=%async_computation.1 | async-start | bytes 1048576 | tf_op jit(solution)/shard_map/all_to_all | solution.py:132
  136.2 13.8 %all-to-all-done.1 = f32[128,4,192]{2,1,0:T(4,128)S(1)} async-done(((f32[128,4,192]{2,1,0:T(4,128)}), f32[128,4,192]{2,1,0:T(4,128)S(1)}, u32[]{:S(2)}, u32[]{:S(2)}) %all-to-all-start.1) | async-done | bytes 393248 | tf_op jit(solution)/shard_map/all_to_all | solution.py:132
  150.3 2.8 %convolution_convert_fusion = bf16[16,3,64,64]{3,2,1,0:T(8,128)(2,1)S(1)} fusion(f32[1,16,32,64]{3,2,0,1:T(8,128)S(1)} %bitcast.81, f32[1,16,32,64]{3,2,0,1:T(8,128)S(1)} %bitcast.78, f32[1,16,32,64]{3,2,0,1:T(8,128)S(1)} %bitcast.77, f32[1,16,32,64]{3,2,0,1:T(8,128)S(1)} %bitcast_select_fusion, f32[1,16,32,64]{3,2,0,1:T(8,128)S(1)} %bitcast.80, ...), kind=kOutput, calls=%fused_computation.12 | convolution fusion | flops 76087296 | bytes 1179648 | tf_op jit(solution)/shard_map/bdlr,bdls->dbrs/dot_general | solution.py:176
  156.6 3.9 %all-to-all-start.2 = ((f32[128,1,128]{2,1,0:T(1,128)}), f32[128,1,128]{2,1,0:T(1,128)S(1)}, u32[]{:S(2)}, u32[]{:S(2)}) async-start(f32[128,1,128]{2,1,0:T(1,128)} %reshape.90), calls=%async_computation.2 | async-start | bytes 131072 | tf_op jit(solution)/shard_map/all_to_all | solution.py:127
  161.2 9.2 %all-to-all-done.2 = f32[128,1,128]{2,1,0:T(1,128)S(1)} async-done(((f32[128,1,128]{2,1,0:T(1,128)}), f32[128,1,128]{2,1,0:T(1,128)S(1)}, u32[]{:S(2)}, u32[]{:S(2)}) %all-to-all-start.2) | async-done | bytes 65568 | tf_op jit(solution)/shard_map/all_to_all | solution.py:127
  (76 shorter events, 41.8 us)
Async XLA Ops:
  0.6 117.6 %copy-start = (bf16[8192,64]{0,1:T(8,128)(2,1)S(1)}, bf16[8192,64]{0,1:T(8,128)(2,1)}, u32[]{:S(2)}) copy-start(bf16[8192,64]{0,1:T(8,128)(2,1)} %param.22) | copy-start | bytes 3145732
  5.1 27.8 %collective-permute-start = (bf16[32,16384]{1,0:T(8,128)(2,1)}, bf16[32,16384]{1,0:T(8,128)(2,1)}, u32[]{:S(2)}, u32[]{:S(2)}) collective-permute-start(bf16[32,16384]{1,0:T(8,128)(2,1)} %get-tuple-element.4), channel_id=1, source_target_pairs={{0,32},{8,40},{16,48},{24,56},{32,64},{40,72},{48,80},{56,88},{64,... | collective-permute-start | bytes 3145736 | tf_op jit(solution)/shard_map/ppermute | solution.py:87
  7.5 25.3 %collective-permute-start.1 = (bf16[32,16384]{1,0:T(8,128)(2,1)}, bf16[32,16384]{1,0:T(8,128)(2,1)S(1)}, u32[]{:S(2)}, u32[]{:S(2)}) collective-permute-start(bf16[32,16384]{1,0:T(8,128)(2,1)} %get-tuple-element.4), channel_id=1, source_target_pairs={{0,96},{8,104},{16,112},{24,120},{32,0},{40,8},{48,16},{56,24},{64... | collective-permute-start | bytes 3145736 | tf_op jit(solution)/shard_map/ppermute | solution.py:87
  9.7 24.0 %collective-permute-start.2 = (bf16[32,16384]{1,0:T(8,128)(2,1)}, bf16[32,16384]{1,0:T(8,128)(2,1)S(1)}, u32[]{:S(2)}, u32[]{:S(2)}) collective-permute-start(bf16[32,16384]{1,0:T(8,128)(2,1)} %get-tuple-element.4), channel_id=1, source_target_pairs={{0,16},{8,24},{16,0},{24,8},{32,48},{40,56},{48,32},{56,40},{64,80... | collective-permute-start | bytes 3145736 | tf_op jit(solution)/shard_map/ppermute | solution.py:87
  11.0 68.0 %collective-permute-start.9 = (bf16[32,16384]{1,0:T(8,128)(2,1)}, bf16[32,16384]{1,0:T(8,128)(2,1)}, u32[]{:S(2)}, u32[]{:S(2)}) collective-permute-start(bf16[32,16384]{1,0:T(8,128)(2,1)} %get-tuple-element.4), channel_id=1, source_target_pairs={{0,8},{8,0},{16,24},{24,16},{32,40},{40,32},{48,56},{56,48},{64,72... | collective-permute-start | bytes 3145736 | tf_op jit(solution)/shard_map/ppermute | solution.py:87
  35.3 46.0 %collective-permute-start.10 = (bf16[3,32,16384]{2,1,0:T(8,128)(2,1)S(1)}, bf16[3,32,16384]{2,1,0:T(8,128)(2,1)S(1)}, u32[]{:S(2)}, u32[]{:S(2)}) collective-permute-start(bf16[3,32,16384]{2,1,0:T(8,128)(2,1)S(1)} %pad_maximum_fusion), channel_id=1, source_target_pairs={{0,8},{8,0},{16,24},{24,16},{32,40},{40,32},{48,56},{56,48},{64,72... | collective-permute-start | bytes 9437192 | tf_op jit(solution)/shard_map/ppermute | solution.py:87
  37.1 24.6 %collective-permute-start.3 = (bf16[32,16384]{1,0:T(8,128)(2,1)S(1)}, bf16[32,16384]{1,0:T(8,128)(2,1)S(1)}, u32[]{:S(2)}, u32[]{:S(2)}) collective-permute-start(bf16[32,16384]{1,0:T(8,128)(2,1)S(1)} %collective-permute-done.1), channel_id=1, source_target_pairs={{0,96},{8,104},{16,112},{24,120},{32,0},{40,8},{48,16},{56,24},{64... | collective-permute-start | bytes 3145736 | tf_op jit(solution)/shard_map/ppermute | solution.py:87
  38.6 27.4 %collective-permute-start.4 = (bf16[32,16384]{1,0:T(8,128)(2,1)S(1)}, bf16[32,16384]{1,0:T(8,128)(2,1)S(1)}, u32[]{:S(2)}, u32[]{:S(2)}) collective-permute-start(bf16[32,16384]{1,0:T(8,128)(2,1)S(1)} %collective-permute-done.2), channel_id=1, source_target_pairs={{0,32},{8,40},{16,48},{24,56},{32,64},{40,72},{48,80},{56,88},{64,... | collective-permute-start | bytes 3145736 | tf_op jit(solution)/shard_map/ppermute | solution.py:87
  38.6 24.6 %collective-permute-start.5 = (bf16[32,16384]{1,0:T(8,128)(2,1)S(1)}, bf16[32,16384]{1,0:T(8,128)(2,1)S(1)}, u32[]{:S(2)}, u32[]{:S(2)}) collective-permute-start(bf16[32,16384]{1,0:T(8,128)(2,1)S(1)} %collective-permute-done.1), channel_id=1, source_target_pairs={{0,16},{8,24},{16,0},{24,8},{32,48},{40,56},{48,32},{56,40},{64,80... | collective-permute-start | bytes 3145736 | tf_op jit(solution)/shard_map/ppermute | solution.py:87
  61.8 8.8 %collective-permute-start.6 = (bf16[32,5376]{1,0:T(8,128)(2,1)S(1)}, bf16[32,5376]{1,0:T(8,128)(2,1)S(1)}, u32[]{:S(2)}, u32[]{:S(2)}) collective-permute-start(bf16[32,5376]{1,0:T(8,128)(2,1)S(1)} %slice.70), channel_id=1, source_target_pairs={{0,16},{8,24},{16,0},{24,8},{32,48},{40,56},{48,32},{56,40},{64,80... | collective-permute-start | bytes 1032200 | tf_op jit(solution)/shard_map/ppermute | solution.py:87
  63.2 9.9 %collective-permute-start.7 = (bf16[32,5376]{1,0:T(8,128)(2,1)S(1)}, bf16[32,5376]{1,0:T(8,128)(2,1)S(1)}, u32[]{:S(2)}, u32[]{:S(2)}) collective-permute-start(bf16[32,5376]{1,0:T(8,128)(2,1)S(1)} %slice.71), channel_id=1, source_target_pairs={{0,96},{8,104},{16,112},{24,120},{32,0},{40,8},{48,16},{56,24},{64... | collective-permute-start | bytes 1032200 | tf_op jit(solution)/shard_map/ppermute | solution.py:87
  65.9 9.8 %collective-permute-start.8 = (bf16[32,5632]{1,0:T(8,128)(2,1)S(1)}, bf16[32,5632]{1,0:T(8,128)(2,1)S(1)}, u32[]{:S(2)}, u32[]{:S(2)}) collective-permute-start(bf16[32,5632]{1,0:T(8,128)(2,1)S(1)} %slice.72), channel_id=1, source_target_pairs={{0,32},{8,40},{16,48},{24,56},{32,64},{40,72},{48,80},{56,88},{64,... | collective-permute-start | bytes 1081352 | tf_op jit(solution)/shard_map/ppermute | solution.py:87
  70.5 13.9 %collective-permute-start.11 = (bf16[3,32,16384]{2,1,0:T(8,128)(2,1)S(1)}, bf16[3,32,16384]{2,1,0:T(8,128)(2,1)S(1)}, u32[]{:S(2)}, u32[]{:S(2)}) collective-permute-start(bf16[3,32,16384]{2,1,0:T(8,128)(2,1)S(1)} %pad_maximum_fusion.1), channel_id=1, source_target_pairs={{0,8},{8,0},{16,24},{24,16},{32,40},{40,32},{48,56},{56,48},{64,72... | collective-permute-start | bytes 9437192 | tf_op jit(solution)/shard_map/ppermute | solution.py:87
  75.8 11.9 %collective-permute-start.12 = (bf16[32,16384]{1,0:T(8,128)(2,1)S(1)}, bf16[32,16384]{1,0:T(8,128)(2,1)S(1)}, u32[]{:S(2)}, u32[]{:S(2)}) collective-permute-start(bf16[32,16384]{1,0:T(8,128)(2,1)S(1)} %pad_maximum_fusion.2), channel_id=1, source_target_pairs={{0,8},{8,0},{16,24},{24,16},{32,40},{40,32},{48,56},{56,48},{64,72... | collective-permute-start | bytes 3145736 | tf_op jit(solution)/shard_map/ppermute | solution.py:87
  105.6 20.4 %all-to-all-start = ((f32[128,4,192]{2,1,0:T(4,128)}), f32[128,4,192]{2,1,0:T(4,128)S(1)}, u32[]{:S(2)}, u32[]{:S(2)}) async-start(f32[128,4,192]{2,1,0:T(4,128)} %broadcast_select_fusion), calls=%async_computation | async-start | bytes 1048576 | tf_op jit(solution)/shard_map/all_to_all | solution.py:127
  118.2 37.0 %copy-start.1 = (s32[32]{0:T(128)S(1)}, s32[32]{0:T(128)}, u32[]{:S(2)}) copy-start(s32[32]{0:T(128)} %param.27) | copy-start | bytes 388
  127.0 23.0 %all-to-all-start.1 = ((f32[128,4,192]{2,1,0:T(4,128)}), f32[128,4,192]{2,1,0:T(4,128)S(1)}, u32[]{:S(2)}, u32[]{:S(2)}) async-start(f32[128,4,192]{2,1,0:T(4,128)} %broadcast_in_dim.58), calls=%async_computation.1 | async-start | bytes 1048576 | tf_op jit(solution)/shard_map/all_to_all | solution.py:132
  156.6 13.8 %all-to-all-start.2 = ((f32[128,1,128]{2,1,0:T(1,128)}), f32[128,1,128]{2,1,0:T(1,128)S(1)}, u32[]{:S(2)}, u32[]{:S(2)}) async-start(f32[128,1,128]{2,1,0:T(1,128)} %reshape.90), calls=%async_computation.2 | async-start | bytes 131072 | tf_op jit(solution)/shard_map/all_to_all | solution.py:127

commit v12 on v11

--- a/solution.py
+++ b/solution.py
@@ -113,7 +113,11 @@
     d = lax.axis_index("dp")
     mine = [d, d - 4, d + 4, d ^ 2, d + 8, (d - 4) % n ^ 2, (d ^ 2) + 4, (d ^ 2) + 8]
     ids = jnp.stack([m % n for m in mine] + [(m % n) ^ 1 for m in mine])
-    return jnp.concatenate(slots, axis=0), jnp.argsort(ids)
+    first = [0, 1, 2, 3, 4, 5, 6, 8, 9, 10, 11]
+    last = [7, 12, 13, 14, 15]
+    early = jnp.concatenate([slots[i] for i in first], axis=0)
+    late = jnp.concatenate([slots[i] for i in last], axis=0)
+    return early, late, jnp.argsort(ids[jnp.array(first + last)])
 
 
 def to_dp_order(x, order):
@@ -153,19 +157,24 @@
     proj_rank = gate_in_proj.shape[1]
     pad_mask = (token_ids != 0).astype(jnp.bfloat16)[:, None]
     masked = cotangent * pad_mask
-    both, order = shared_gather(jnp.concatenate([hidden_in, masked], axis=1), lax.axis_size("dp"))
+    early, late, order = shared_gather(jnp.concatenate([hidden_in, masked], axis=1), lax.axis_size("dp"))
     f32 = jnp.float32
-    block = layer_call(both, gate_weight, up_weight, down_weight, gate_out_proj, up_out_proj, down_in_proj)
+    weights = (gate_weight, up_weight, down_weight, gate_out_proj, up_out_proj, down_in_proj)
+    block = jnp.concatenate([layer_call(early, *weights), layer_call(late, *weights)], axis=0)
     summed = gather_rows(scatter_sum(to_dp_order(block, order), n_all), n_all)
     d_model = hidden_in.shape[1]
-    in_both = jnp.dot(
-        both[:, :d_model], jnp.concatenate([gate_in_proj, up_in_proj], axis=1), preferred_element_type=f32
+    in_proj = jnp.concatenate([gate_in_proj, up_in_proj], axis=1)
+    in_both = jnp.concatenate(
+        [jnp.dot(rows[:, :d_model], in_proj, preferred_element_type=f32) for rows in (early, late)], axis=0
     )
     in_both = to_dp_order(in_both, order)
     in_gate = in_both[:, :proj_rank]
     in_up = in_both[:, proj_rank:]
-    out_down = to_dp_order(jnp.dot(both[:, d_model:], down_out_proj, preferred_element_type=f32), order)
-    docs = both.shape[0] // LEN
+    out_down = jnp.concatenate(
+        [jnp.dot(rows[:, d_model:], down_out_proj, preferred_element_type=f32) for rows in (early, late)], axis=0
+    )
+    out_down = to_dp_order(out_down, order)
+    docs = (early.shape[0] + late.shape[0]) // LEN
 
     side_gate = summed[:, :proj_rank]
     side_up = summed[:, proj_rank : 2 * proj_rank]

time: 173 us -> 195 us (1.13)
  waiting for transfers between devices: 59.4 us -> 68.1 us
  starting transfers between devices: 39.3 us -> 32.2 us
  local copies, waits for them, and re-layouts: 31.7 us -> 38.7 us
  Pallas kernels: 14 us -> 20.9 us
  other arithmetic: 10.6 us -> 14.8 us
  matrix products: 16.7 us -> 18.9 us
    all_to_all x2, waiting for transfers between devices: 10.1 us -> 21.8 us  [scatter_sum(): return jnp.sum(lax.all_to_all(blocks, ALL, 0, 0, tiled=False), axis=0)]
    pallas_call x1 -> x2, Pallas kernels: 14 us -> 20.9 us  [layer_call(): pl.pallas_call(layer_kernel, grid=(nk,), in_specs=[pl.BlockSpec((rows, KC...]
    all_to_all x1, starting transfers between devices: 8.94 us -> 3.9 us  [gather_rows(): got = lax.all_to_all(copies, ALL, 0, 0, tiled=False)]
    concatenate x1 -> x4, local copies, waits for them, and re-layouts: 1.05 us -> 5.76 us  [the longest x1 2.3 us: body(): in_proj = jnp.concatenate([gate_in_proj, up_in_proj], axis=1)]
    ppermute x13, waiting for transfers between devices: 35.6 us -> 32.6 us  [shared_gather(): pp = lambda v, p: lax.ppermute(v, 'dp', p)]
    unnamed x25 -> x35, local copies, waits for them, and re-layouts: 24.1 us -> 26.8 us
    unnamed x0 -> x1, other arithmetic: none -> 2.49 us
    dot_general x2 -> x4, matrix products: 11.9 us -> 14.1 us  [the longest x2 7.26 us: body(): jnp.dot(rows[:, d_model:], down_out_proj, preferred_element_type=f32)]
  transfers between devices with their start and end apart: 16 -> 16, of which waited for: 8 -> 7; matrix products, arithmetic and copies ran while one was open for 24% -> 25% of each run, Pallas kernels for 0% -> 6%
where the time goes in v12:
time: 195 us
  waiting for transfers between devices  68.1 us (35%)
  local copies, waits for them, and re-layouts  38.7 us (20%)
  starting transfers between devices  32.2 us (17%)
  Pallas kernels  20.9 us (11%)
  matrix products  18.9 us (10%)
  other arithmetic  14.8 us (8%)
    ppermute x13, waiting for transfers between devices, shared_gather(): pp = lambda v, p: lax.ppermute(v, 'dp', p)  32.6 us
    unnamed x35, local copies, waits for them, and re-layouts  26.8 us
    all_to_all x2, waiting for transfers between devices, scatter_sum(): return jnp.sum(lax.all_to_all(blocks, ALL, 0, 0, tiled=False), axis=0)  21.8 us
    pallas_call x2, Pallas kernels, layer_call(): pl.pallas_call(layer_kernel, grid=(nk,), in_specs=[pl.BlockSpec((rows, KC...  20.9 us
    ppermute x13, starting transfers between devices, shared_gather(): pp = lambda v, p: lax.ppermute(v, 'dp', p)  18.1 us
    all_to_all x1, waiting for transfers between devices, gather_rows(): got = lax.all_to_all(copies, ALL, 0, 0, tiled=False)  13.8 us
    all_to_all x2, starting transfers between devices, scatter_sum(): return jnp.sum(lax.all_to_all(blocks, ALL, 0, 0, tiled=False), axis=0)  10.3 us
    dot_general x2, matrix products, body(): jnp.dot(rows[:, d_model:], down_out_proj, preferred_element_type=f32)  7.26 us
  transfers between devices with their start and end apart: 16, of which 7 were waited for; matrix products, arithmetic and copies ran while one was open for 25% of the time, Pallas kernels for 6%

profile of v12, /device:TPU:1, one launch (start us, length us, event | category | flops | bytes accessed | tf_op | source)
XLA Modules:
  0.0 194.6 jit_solution(998711899975883414)
XLA Ops:
  2.6 2.5 %constant_dynamic-update-slice_fusion.7 = (bf16[352,16384]{1,0:T(8,128)(2,1)}, bf16[32,16384]{1,0:T(8,128)(2,1)}) fusion(bf16[32,8192]{1,0:T(8,128)(2,1)S(1)} %broadcast_multiply_fusion, bf16[32,8192]{1,0:T(8,128)(2,1)} %param.16), kind=kLoop, calls=%fused_computation.57 | loop fusion | flops 2097151 | bytes 3145728
  7.2 3.8 %collective-permute-start.1 = (bf16[32,16384]{1,0:T(8,128)(2,1)}, bf16[32,16384]{1,0:T(8,128)(2,1)S(1)}, u32[]{:S(2)}, u32[]{:S(2)}) collective-permute-start(bf16[32,16384]{1,0:T(8,128)(2,1)} %get-tuple-element.5), channel_id=1, source_target_pairs={{0,96},{8,104},{16,112},{24,120},{32,0},{40,8},{48,16},{56,24},{64... | collective-permute-start | bytes 3145736 | tf_op jit(solution)/shard_map/ppermute | solution.py:87
  19.7 2.3 %constant_dynamic-update-slice_fusion.8 = bf16[8192,128]{0,1:T(8,128)(2,1)} fusion(bf16[8192,128]{0,1:T(8,128)(2,1)} %constant_dynamic-update-slice_fusion.9, bf16[8192,64]{0,1:T(8,128)(2,1)} %param.22), kind=kLoop, calls=%fused_computation.58 | loop fusion | bytes 2097152 | tf_op jit(solution)/shard_map/concatenate | solution.py:166
  22.0 8.0 %collective-permute-done.2 = bf16[32,16384]{1,0:T(8,128)(2,1)S(1)} collective-permute-done((bf16[32,16384]{1,0:T(8,128)(2,1)}, bf16[32,16384]{1,0:T(8,128)(2,1)S(1)}, u32[]{:S(2)}, u32[]{:S(2)}) %collective-permute-start.2) | collective-permute-done | bytes 1048608 | tf_op jit(solution)/shard_map/ppermute | solution.py:87
  30.0 2.8 %collective-permute-done.1 = bf16[32,16384]{1,0:T(8,128)(2,1)S(1)} collective-permute-done((bf16[32,16384]{1,0:T(8,128)(2,1)}, bf16[32,16384]{1,0:T(8,128)(2,1)S(1)}, u32[]{:S(2)}, u32[]{:S(2)}) %collective-permute-start.1) | collective-permute-done | bytes 1048608 | tf_op jit(solution)/shard_map/ppermute | solution.py:87
  32.8 3.1 %collective-permute-done = bf16[32,16384]{1,0:T(8,128)(2,1)} collective-permute-done((bf16[32,16384]{1,0:T(8,128)(2,1)}, bf16[32,16384]{1,0:T(8,128)(2,1)}, u32[]{:S(2)}, u32[]{:S(2)}) %collective-permute-start) | collective-permute-done | bytes 1048608 | tf_op jit(solution)/shard_map/ppermute | solution.py:87
  39.9 2.7 %collective-permute-start.3 = (bf16[32,16384]{1,0:T(8,128)(2,1)S(1)}, bf16[32,16384]{1,0:T(8,128)(2,1)S(1)}, u32[]{:S(2)}, u32[]{:S(2)}) collective-permute-start(bf16[32,16384]{1,0:T(8,128)(2,1)S(1)} %collective-permute-done.1), channel_id=1, source_target_pairs={{0,96},{8,104},{16,112},{24,120},{32,0},{40,8},{48,16},{56,24},{64... | collective-permute-start | bytes 3145736 | tf_op jit(solution)/shard_map/ppermute | solution.py:87
  46.9 18.6 %collective-permute-done.4 = bf16[32,16384]{1,0:T(8,128)(2,1)S(1)} collective-permute-done((bf16[32,16384]{1,0:T(8,128)(2,1)S(1)}, bf16[32,16384]{1,0:T(8,128)(2,1)S(1)}, u32[]{:S(2)}, u32[]{:S(2)}) %collective-permute-start.4) | collective-permute-done | bytes 1048608 | tf_op jit(solution)/shard_map/ppermute | solution.py:87
  65.7 2.7 %collective-permute-start.9 = (bf16[32,5376]{1,0:T(8,128)(2,1)S(1)}, bf16[32,5376]{1,0:T(8,128)(2,1)S(1)}, u32[]{:S(2)}, u32[]{:S(2)}) collective-permute-start(bf16[32,5376]{1,0:T(8,128)(2,1)S(1)} %slice.85), channel_id=1, source_target_pairs={{0,96},{8,104},{16,112},{24,120},{32,0},{40,8},{48,16},{56,24},{64... | collective-permute-start | bytes 1032200 | tf_op jit(solution)/shard_map/ppermute | solution.py:87
  75.6 2.3 %constant_dynamic-update-slice_fusion = bf16[352,16384]{1,0:T(8,128)(2,1)} fusion(bf16[352,16384]{1,0:T(8,128)(2,1)} %constant_dynamic-update-slice_fusion.1, bf16[32,16384]{1,0:T(8,128)(2,1)} %collective-permute-done.6), kind=kLoop, calls=%fused_computation.50 | loop fusion | bytes 2097152
  85.6 11.6 %shard_map.158 = f32[352,192]{1,0:T(8,128)} custom-call(bf16[352,16384]{1,0:T(8,128)(2,1)} %fusion.11.act_ref.cot_ref, bf16[352,16384]{1,0:T(8,128)(2,1)} %fusion.11.act_ref.cot_ref, bf16[224,8192]{1,0:T(8,128)(2,1)} %bitcast.72, bf16[224,8192]{1,0:T(8,128)(2,1)} %bitcast.74, bf16[224,8192]{1,0:T(8,128)(2,1)} %dw_ref.3, bf16[224,64]{1,0:T(8,128)(2,1)} %copy.23.go_ref, ...), custom_call_target="tpu_custom_call" | custom-call | flops 3905814528 | bytes 22900736 | tf_op jit(solution)/shard_map/pallas_call | solution.py:55
  97.2 4.5 %fusion = f32[352,64]{0,1:T(8,128)S(1)} fusion(bf16[8192,64]{0,1:T(8,128)(2,1)S(1)} %copy-done, bf16[352,16384]{1,0:T(8,128)(2,1)} %fusion.11.act_ref.cot_ref), kind=kOutput, calls=%fused_computation.4 | convolution fusion | flops 369098752 | bytes 6905856 | tf_op jit(solution)/shard_map/dot_general | solution.py:174
  101.7 4.3 %fusion.2 = f32[352,128]{1,0:T(8,128)S(1)} fusion(bf16[8192,128]{0,1:T(8,128)(2,1)S(1)} %copy-done.2, bf16[352,16384]{1,0:T(8,128)(2,1)} %fusion.11.act_ref.cot_ref), kind=kOutput, calls=%fused_computation.6 | convolution fusion | flops 738197504 | bytes 8044544 | tf_op jit(solution)/shard_map/dot_general | solution.py:168
  106.0 2.4 %fusion.10 = bf16[160,16384]{1,0:T(8,128)(2,1)} fusion(bf16[160,16384]{1,0:T(8,128)(2,1)} %constant_dynamic-update-slice_fusion.11, bf16[3,32,16384]{2,1,0:T(8,128)(2,1)} %collective-permute-done.11), kind=kLoop, calls=%fused_computation.21 | loop fusion | bytes 2097152
  115.2 2.6 %fusion.6 = f32[160,128]{1,0:T(8,128)S(1)} fusion(bf16[8192,128]{0,1:T(8,128)(2,1)S(1)} %copy-done.2, bf16[160,16384]{1,0:T(8,128)(2,1)} %constant_dynamic-update-slice_fusion.10.act_ref.cot_ref), kind=kOutput, calls=%fused_computation.12 | convolution fusion | flops 335544320 | bytes 4800512 | tf_op jit(solution)/shard_map/dot_general | solution.py:168
  117.8 9.4 %shard_map.159 = f32[160,192]{1,0:T(8,128)} custom-call(bf16[160,16384]{1,0:T(8,128)(2,1)} %constant_dynamic-update-slice_fusion.10.act_ref.cot_ref, bf16[160,16384]{1,0:T(8,128)(2,1)} %constant_dynamic-update-slice_fusion.10.act_ref.cot_ref, bf16[224,8192]{1,0:T(8,128)(2,1)} %bitcast.73, bf16[224,8192]{1,0:T(8,128)(2,1)} %bitcast.75, ...), custom_call_target="tpu_custom_call" | custom-call | flops 1775370240 | bytes 16461824 | tf_op jit(solution)/shard_map/pallas_call | solution.py:55
  127.1 2.7 %fusion.4 = f32[160,64]{0,1:T(8,128)S(1)} fusion(bf16[8192,64]{0,1:T(8,128)(2,1)S(1)} %copy-done, bf16[160,16384]{1,0:T(8,128)(2,1)} %constant_dynamic-update-slice_fusion.10.act_ref.cot_ref), kind=kOutput, calls=%fused_computation.10 | convolution fusion | flops 167772160 | bytes 3710976 | tf_op jit(solution)/shard_map/dot_general | solution.py:174
  132.6 6.4 %all-to-all-start = ((f32[128,4,192]{2,1,0:T(4,128)}), f32[128,4,192]{2,1,0:T(4,128)S(1)}, u32[]{:S(2)}, u32[]{:S(2)}) async-start(f32[128,4,192]{2,1,0:T(4,128)} %broadcast_select_fusion), calls=%async_computation | async-start | bytes 1048576 | tf_op jit(solution)/shard_map/all_to_all | solution.py:131
  140.4 12.6 %all-to-all-done = f32[128,4,192]{2,1,0:T(4,128)S(1)} async-done(((f32[128,4,192]{2,1,0:T(4,128)}), f32[128,4,192]{2,1,0:T(4,128)S(1)}, u32[]{:S(2)}, u32[]{:S(2)}) %all-to-all-start) | async-done | bytes 393248 | tf_op jit(solution)/shard_map/all_to_all | solution.py:131
  154.0 3.9 %all-to-all-start.1 = ((f32[128,4,192]{2,1,0:T(4,128)}), f32[128,4,192]{2,1,0:T(4,128)S(1)}, u32[]{:S(2)}, u32[]{:S(2)}) async-start(f32[128,4,192]{2,1,0:T(4,128)} %broadcast_in_dim.62), calls=%async_computation.1 | async-start | bytes 1048576 | tf_op jit(solution)/shard_map/all_to_all | solution.py:136
  158.2 13.8 %all-to-all-done.1 = f32[128,4,192]{2,1,0:T(4,128)S(1)} async-done(((f32[128,4,192]{2,1,0:T(4,128)}), f32[128,4,192]{2,1,0:T(4,128)S(1)}, u32[]{:S(2)}, u32[]{:S(2)}) %all-to-all-start.1) | async-done | bytes 393248 | tf_op jit(solution)/shard_map/all_to_all | solution.py:136
  172.3 2.8 %convolution_convert_fusion = bf16[16,3,64,64]{3,2,1,0:T(8,128)(2,1)S(1)} fusion(f32[1,16,32,64]{3,2,0,1:T(8,128)S(1)} %bitcast.88, f32[1,16,32,64]{3,2,0,1:T(8,128)S(1)} %bitcast.85, f32[1,16,32,64]{3,2,0,1:T(8,128)S(1)} %bitcast.84, f32[1,16,32,64]{3,2,0,1:T(8,128)S(1)} %bitcast_select_fusion, f32[1,16,32,64]{3,2,0,1:T(8,128)S(1)} %bitcast.87, ...), kind=kOutput, calls=%fused_computation.14 | convolution fusion | flops 76087296 | bytes 1179648 | tf_op jit(solution)/shard_map/bdlr,bdls->dbrs/dot_general | solution.py:185
  178.6 3.9 %all-to-all-start.2 = ((f32[128,1,128]{2,1,0:T(1,128)}), f32[128,1,128]{2,1,0:T(1,128)S(1)}, u32[]{:S(2)}, u32[]{:S(2)}) async-start(f32[128,1,128]{2,1,0:T(1,128)} %reshape.98), calls=%async_computation.2 | async-start | bytes 131072 | tf_op jit(solution)/shard_map/all_to_all | solution.py:131
  183.1 9.2 %all-to-all-done.2 = f32[128,1,128]{2,1,0:T(1,128)S(1)} async-done(((f32[128,1,128]{2,1,0:T(1,128)}), f32[128,1,128]{2,1,0:T(1,128)S(1)}, u32[]{:S(2)}, u32[]{:S(2)}) %all-to-all-start.2) | async-done | bytes 65568 | tf_op jit(solution)/shard_map/all_to_all | solution.py:131
  (97 shorter events, 55.0 us)
Async XLA Ops:
  0.6 96.5 %copy-start = (bf16[8192,64]{0,1:T(8,128)(2,1)S(1)}, bf16[8192,64]{0,1:T(8,128)(2,1)}, u32[]{:S(2)}) copy-start(bf16[8192,64]{0,1:T(8,128)(2,1)} %param.23) | copy-start | bytes 3145732
  0.6 16.8 %copy-start.3 = (bf16[224,64]{0,1:T(8,128)(2,1)S(1)}, bf16[224,64]{0,1:T(8,128)(2,1)}, u32[]{:S(2)}) copy-start(bf16[224,64]{0,1:T(8,128)(2,1)} %param.24) | copy-start | bytes 86020
  0.7 17.5 %copy-start.4 = (bf16[224,64]{0,1:T(8,128)(2,1)S(1)}, bf16[224,64]{0,1:T(8,128)(2,1)}, u32[]{:S(2)}) copy-start(bf16[224,64]{0,1:T(8,128)(2,1)} %param.25) | copy-start | bytes 86020
  0.7 18.3 %copy-start.5 = (bf16[224,64]{0,1:T(8,128)(2,1)S(1)}, bf16[224,64]{0,1:T(8,128)(2,1)}, u32[]{:S(2)}) copy-start(bf16[224,64]{0,1:T(8,128)(2,1)} %param.26) | copy-start | bytes 86020
  5.1 25.0 %collective-permute-start.2 = (bf16[32,16384]{1,0:T(8,128)(2,1)}, bf16[32,16384]{1,0:T(8,128)(2,1)S(1)}, u32[]{:S(2)}, u32[]{:S(2)}) collective-permute-start(bf16[32,16384]{1,0:T(8,128)(2,1)} %get-tuple-element.5), channel_id=1, source_target_pairs={{0,16},{8,24},{16,0},{24,8},{32,48},{40,56},{48,32},{56,40},{64,80... | collective-permute-start | bytes 3145736 | tf_op jit(solution)/shard_map/ppermute | solution.py:87
  7.2 25.6 %collective-permute-start.1 = (bf16[32,16384]{1,0:T(8,128)(2,1)}, bf16[32,16384]{1,0:T(8,128)(2,1)S(1)}, u32[]{:S(2)}, u32[]{:S(2)}) collective-permute-start(bf16[32,16384]{1,0:T(8,128)(2,1)} %get-tuple-element.5), channel_id=1, source_target_pairs={{0,96},{8,104},{16,112},{24,120},{32,0},{40,8},{48,16},{56,24},{64... | collective-permute-start | bytes 3145736 | tf_op jit(solution)/shard_map/ppermute | solution.py:87
  10.9 25.0 %collective-permute-start = (bf16[32,16384]{1,0:T(8,128)(2,1)}, bf16[32,16384]{1,0:T(8,128)(2,1)}, u32[]{:S(2)}, u32[]{:S(2)}) collective-permute-start(bf16[32,16384]{1,0:T(8,128)(2,1)} %get-tuple-element.5), channel_id=1, source_target_pairs={{0,32},{8,40},{16,48},{24,56},{32,64},{40,72},{48,80},{56,88},{64,... | collective-permute-start | bytes 3145736 | tf_op jit(solution)/shard_map/ppermute | solution.py:87
  10.9 62.9 %collective-permute-start.6 = (bf16[32,16384]{1,0:T(8,128)(2,1)}, bf16[32,16384]{1,0:T(8,128)(2,1)}, u32[]{:S(2)}, u32[]{:S(2)}) collective-permute-start(bf16[32,16384]{1,0:T(8,128)(2,1)} %get-tuple-element.5), channel_id=1, source_target_pairs={{0,8},{8,0},{16,24},{24,16},{32,40},{40,32},{48,56},{56,48},{64,72... | collective-permute-start | bytes 3145736 | tf_op jit(solution)/shard_map/ppermute | solution.py:87
  37.5 44.9 %collective-permute-start.7 = (bf16[3,32,16384]{2,1,0:T(8,128)(2,1)S(1)}, bf16[3,32,16384]{2,1,0:T(8,128)(2,1)S(1)}, u32[]{:S(2)}, u32[]{:S(2)}) collective-permute-start(bf16[3,32,16384]{2,1,0:T(8,128)(2,1)S(1)} %pad_maximum_fusion), channel_id=1, source_target_pairs={{0,8},{8,0},{16,24},{24,16},{32,40},{40,32},{48,56},{56,48},{64,72... | collective-permute-start | bytes 9437192 | tf_op jit(solution)/shard_map/ppermute | solution.py:87
  39.7 25.8 %collective-permute-start.4 = (bf16[32,16384]{1,0:T(8,128)(2,1)S(1)}, bf16[32,16384]{1,0:T(8,128)(2,1)S(1)}, u32[]{:S(2)}, u32[]{:S(2)}) collective-permute-start(bf16[32,16384]{1,0:T(8,128)(2,1)S(1)} %collective-permute-done.2), channel_id=1, source_target_pairs={{0,32},{8,40},{16,48},{24,56},{32,64},{40,72},{48,80},{56,88},{64,... | collective-permute-start | bytes 3145736 | tf_op jit(solution)/shard_map/ppermute | solution.py:87
  39.7 26.0 %collective-permute-start.5 = (bf16[32,16384]{1,0:T(8,128)(2,1)S(1)}, bf16[32,16384]{1,0:T(8,128)(2,1)S(1)}, u32[]{:S(2)}, u32[]{:S(2)}) collective-permute-start(bf16[32,16384]{1,0:T(8,128)(2,1)S(1)} %collective-permute-done.1), channel_id=1, source_target_pairs={{0,16},{8,24},{16,0},{24,8},{32,48},{40,56},{48,32},{56,40},{64,80... | collective-permute-start | bytes 3145736 | tf_op jit(solution)/shard_map/ppermute | solution.py:87
  39.9 28.6 %collective-permute-start.3 = (bf16[32,16384]{1,0:T(8,128)(2,1)S(1)}, bf16[32,16384]{1,0:T(8,128)(2,1)S(1)}, u32[]{:S(2)}, u32[]{:S(2)}) collective-permute-start(bf16[32,16384]{1,0:T(8,128)(2,1)S(1)} %collective-permute-done.1), channel_id=1, source_target_pairs={{0,96},{8,104},{16,112},{24,120},{32,0},{40,8},{48,16},{56,24},{64... | collective-permute-start | bytes 3145736 | tf_op jit(solution)/shard_map/ppermute | solution.py:87
  65.6 13.9 %collective-permute-start.10 = (bf16[32,5632]{1,0:T(8,128)(2,1)S(1)}, bf16[32,5632]{1,0:T(8,128)(2,1)S(1)}, u32[]{:S(2)}, u32[]{:S(2)}) collective-permute-start(bf16[32,5632]{1,0:T(8,128)(2,1)S(1)} %slice.86), channel_id=1, source_target_pairs={{0,32},{8,40},{16,48},{24,56},{32,64},{40,72},{48,80},{56,88},{64,... | collective-permute-start | bytes 1081352 | tf_op jit(solution)/shard_map/ppermute | solution.py:87
  65.7 13.0 %collective-permute-start.9 = (bf16[32,5376]{1,0:T(8,128)(2,1)S(1)}, bf16[32,5376]{1,0:T(8,128)(2,1)S(1)}, u32[]{:S(2)}, u32[]{:S(2)}) collective-permute-start(bf16[32,5376]{1,0:T(8,128)(2,1)S(1)} %slice.85), channel_id=1, source_target_pairs={{0,96},{8,104},{16,112},{24,120},{32,0},{40,8},{48,16},{56,24},{64... | collective-permute-start | bytes 1032200 | tf_op jit(solution)/shard_map/ppermute | solution.py:87
  68.4 9.4 %collective-permute-start.8 = (bf16[32,5376]{1,0:T(8,128)(2,1)S(1)}, bf16[32,5376]{1,0:T(8,128)(2,1)S(1)}, u32[]{:S(2)}, u32[]{:S(2)}) collective-permute-start(bf16[32,5376]{1,0:T(8,128)(2,1)S(1)} %slice.84), channel_id=1, source_target_pairs={{0,16},{8,24},{16,0},{24,8},{32,48},{40,56},{48,32},{56,40},{64,80... | collective-permute-start | bytes 1032200 | tf_op jit(solution)/shard_map/ppermute | solution.py:87
  73.8 32.2 %collective-permute-start.11 = (bf16[3,32,16384]{2,1,0:T(8,128)(2,1)}, bf16[3,32,16384]{2,1,0:T(8,128)(2,1)}, u32[]{:S(2)}, u32[]{:S(2)}) collective-permute-start(bf16[3,32,16384]{2,1,0:T(8,128)(2,1)} %pad_maximum_fusion.1), channel_id=1, source_target_pairs={{0,8},{8,0},{16,24},{24,16},{32,40},{40,32},{48,56},{56,48},{64,72... | collective-permute-start | bytes 9437192 | tf_op jit(solution)/shard_map/ppermute | solution.py:87
  80.5 32.4 %collective-permute-start.12 = (bf16[32,16384]{1,0:T(8,128)(2,1)}, bf16[32,16384]{1,0:T(8,128)(2,1)}, u32[]{:S(2)}, u32[]{:S(2)}) collective-permute-start(bf16[32,16384]{1,0:T(8,128)(2,1)} %pad_maximum_fusion.3), channel_id=1, source_target_pairs={{0,8},{8,0},{16,24},{24,16},{32,40},{40,32},{48,56},{56,48},{64,72... | collective-permute-start | bytes 3145736 | tf_op jit(solution)/shard_map/ppermute | solution.py:87
  97.1 4.5 %copy-start.2 = (bf16[8192,128]{0,1:T(8,128)(2,1)S(1)}, bf16[8192,128]{0,1:T(8,128)(2,1)}, u32[]{:S(2)}) copy-start(bf16[8192,128]{0,1:T(8,128)(2,1)} %constant_dynamic-update-slice_fusion.8) | copy-start | bytes 6291460
  117.8 12.1 %copy-start.1 = (f32[352,192]{1,0:T(8,128)S(1)}, f32[352,192]{1,0:T(8,128)}, u32[]{:S(2)}) copy-start(f32[352,192]{1,0:T(8,128)} %shard_map.158) | copy-start | bytes 811012
  132.6 20.4 %all-to-all-start = ((f32[128,4,192]{2,1,0:T(4,128)}), f32[128,4,192]{2,1,0:T(4,128)S(1)}, u32[]{:S(2)}, u32[]{:S(2)}) async-start(f32[128,4,192]{2,1,0:T(4,128)} %broadcast_select_fusion), calls=%async_computation | async-start | bytes 1048576 | tf_op jit(solution)/shard_map/all_to_all | solution.py:131
  153.2 24.0 %copy-start.6 = (s32[32]{0:T(128)S(1)}, s32[32]{0:T(128)}, u32[]{:S(2)}) copy-start(s32[32]{0:T(128)} %param.28) | copy-start | bytes 388
  154.0 17.9 %all-to-all-start.1 = ((f32[128,4,192]{2,1,0:T(4,128)}), f32[128,4,192]{2,1,0:T(4,128)S(1)}, u32[]{:S(2)}, u32[]{:S(2)}) async-start(f32[128,4,192]{2,1,0:T(4,128)} %broadcast_in_dim.62), calls=%async_computation.1 | async-start | bytes 1048576 | tf_op jit(solution)/shard_map/all_to_all | solution.py:136
  178.6 13.8 %all-to-all-start.2 = ((f32[128,1,128]{2,1,0:T(1,128)}), f32[128,1,128]{2,1,0:T(1,128)S(1)}, u32[]{:S(2)}, u32[]{:S(2)}) async-start(f32[128,1,128]{2,1,0:T(1,128)} %reshape.98), calls=%async_computation.2 | async-start | bytes 131072 | tf_op jit(solution)/shard_map/all_to_all | solution.py:131
